TPU v7x, 512 devices: a whole 4x8x8 slice. The times are simulated.
512 devices in a mesh: obs: 32 (over y, z_lo), gr: 4 (over x), gc: 4 (over z_hi, core).
Axes of the slice: x: 4, y: 8, z: 8 (z_hi: 2, z_lo: 4; z = z_hi * 4 + z_lo), core: 2. Of those that a mesh axis runs over, the one named last changes fastest.
Arguments:
- legendre: float32 [4, 256, 8192], P(None, 'obs'), may hold values from -6 to 6
- longitude: float32 [4, 256], P(None, 'obs'), may hold values from -3.140625 to 3.140625
- orders: int32 [8192], replicated, may hold values from 0 to 360, as said below
- whitening: float32 [4, 256, 256], replicated, as said below
Outputs:
- normal: float32 [16384, 16384], P('obs', ('gr', 'gc'))
Inputs may be any that keep to these rules, and one draw needn't show every extreme that they name: The orders of 8192 degree-order pairs that follow one another cyclically in the order-major ordering of a degree-360 field (order m holds degrees m to 360); the run passes from the last pair, of order 360, to the first, of order 0, so the orders rise, fall once from 360 to 0, and rise again. Each arc's whitening matrix is lower triangular with a positive diagonal.
All inputs are finite; a program needn't handle non-finite values.
Results may differ from a plain program's by a relative error of at most 0.0003.
Values sent between devices are 32-bit elements; how exact they have to be, the bound alone decides.
No kernel may reach another device: no remote copies, remote signals or barrier semaphores. Data moves between devices by JAX's collectives and lax.ppermute only.
A program may use at most 64 MiB of HBM per device.

v0:
```python
import jax
import jax.numpy as jnp
from jax import lax
from jax.sharding import PartitionSpec as P

highest = lax.Precision.HIGHEST


def trig_design(values, longitudes, order_values):
    angles = order_values * longitudes
    stacked = jnp.stack([values * jnp.cos(angles), values * jnp.sin(angles)], axis=-1)
    return stacked.reshape(values.shape[:-1] + (2 * values.shape[-1],))


def whiten(design, matrices):
    return jnp.einsum("kec,kfe->kcf", design, matrices, precision=highest)


def shards(legendre, longitude, orders, whitening):
    arcs_total, epochs_local, pairs_total = legendre.shape
    arc_length = whitening.shape[1]
    obs_count = lax.axis_size("obs")
    grid_count = lax.axis_size(("gr", "gc"))
    grid_position = lax.axis_index(("gr", "gc"))
    row_pairs = pairs_total // obs_count
    col_pairs = pairs_total // grid_count
    row_piece = row_pairs // grid_count
    order_values = orders.astype(jnp.float32)
    accumulated = jnp.zeros((2 * row_pairs, 2 * col_pairs), jnp.float32)
    for arc_index in range(arcs_total):
        values = legendre[arc_index : arc_index + 1]
        longitudes = longitude[arc_index : arc_index + 1]
        matrices = whitening[arc_index : arc_index + 1]
        batch = values.shape[0]
        col_values = lax.dynamic_slice_in_dim(values, grid_position * col_pairs, col_pairs, 2)
        col_orders = lax.dynamic_slice_in_dim(order_values, grid_position * col_pairs, col_pairs, 0)
        value_rows = lax.all_gather(col_values, "obs", axis=1, tiled=True)
        longitude_rows = lax.all_gather(longitudes, "obs", axis=1, tiled=True)
        design = trig_design(value_rows, longitude_rows[:, :, None], col_orders)
        col_panel = jnp.einsum("kec,kfe->kcf", design, matrices, precision=highest)
        grouped = values.reshape(batch, epochs_local, obs_count, grid_count, row_piece)
        row_values = lax.dynamic_index_in_dim(grouped, grid_position, 3, keepdims=False)
        row_orders = lax.dynamic_index_in_dim(
            order_values.reshape(obs_count, grid_count, row_piece), grid_position, 1, keepdims=False
        )
        outgoing = trig_design(row_values, longitudes[:, :, None, None], row_orders)
        arrived = lax.all_to_all(outgoing, "obs", split_axis=2, concat_axis=1, tiled=True)
        own_rows = whiten(arrived.reshape(batch, arc_length, 2 * row_piece), matrices)
        accumulated = accumulated + jnp.einsum(
            "kcf,kdf->cd",
            lax.all_gather(own_rows, ("gr", "gc"), axis=1, tiled=True),
            col_panel,
            precision=highest,
        )
    return accumulated


def solution(mesh):
    placed = (P(None, "obs", None), P(None, "obs"), P(), P())
    return jax.shard_map(
        shards, mesh=mesh, in_specs=placed, out_specs=P("obs", ("gr", "gc")), check_vma=False
    )
```

profile of v0, /device:TPU:1, one launch (start us, length us, event | category | flops | bytes accessed | tf_op | source)
XLA Modules:
  0.0 630.3 jit_solution(18091526618583735605)
XLA Ops:
  2.0 2.0 reshape.715
  4.1 1.5 constant_dynamic-slice_fusion.1
  8.2 2.0 reshape.702
  10.2 1.5 constant_dynamic-slice_fusion.5
  12.0 2.5 fusion.50
  15.5 13.6 %all-to-all-start.2 = ((f32[32,1,256]{2,1,0:T(1,128)}), f32[32,1,256]{2,1,0:T(1,128)}, u32[]{:S(2)}, u32[]{:S(2)}) async-start(f32[32,1,256]{2,1,0:T(1,128)} %reshape.759), calls=%async_computation.2 | async-start | bytes 65536 | tf_op jit(solution)/shard_map/all_to_all | solution.py:47
  29.8 67.4 %all_gather.57 = f32[1,256,512]{2,1,0:T(8,128)S(1)} all-gather(f32[1,8,512]{2,1,0:T(8,128)S(1)} %constant_dynamic-slice_fusion), channel_id=1, replica_groups=mesh['obs'=32,'gr'=4,'gc'=4] {'obs'}, dimensions={1}, use_global_device_ids=true | all-gather | bytes 540672 | tf_op jit(solution)/shard_map/all_gather | solution.py:37
  99.6 62.2 %all_gather.49 = f32[1,256,512]{2,1,0:T(8,128)S(1)} all-gather(f32[1,8,512]{2,1,0:T(8,128)S(1)} %constant_dynamic-slice_fusion.4), channel_id=1, replica_groups=mesh['obs'=32,'gr'=4,'gc'=4] {'obs'}, dimensions={1}, use_global_device_ids=true | all-gather | bytes 540672 | tf_op jit(solution)/shard_map/all_gather | solution.py:37
  161.8 64.1 %all_gather.53 = f32[1,256,512]{2,1,0:T(8,128)S(1)} all-gather(f32[1,8,512]{2,1,0:T(8,128)S(1)} %constant_dynamic-slice_fusion.2), channel_id=1, replica_groups=mesh['obs'=32,'gr'=4,'gc'=4] {'obs'}, dimensions={1}, use_global_device_ids=true | all-gather | bytes 540672 | tf_op jit(solution)/shard_map/all_gather | solution.py:37
  225.9 62.3 %all_gather.45 = f32[1,256,512]{2,1,0:T(8,128)S(1)} all-gather(f32[1,8,512]{2,1,0:T(8,128)S(1)} %constant_dynamic-slice_fusion.6), channel_id=1, replica_groups=mesh['obs'=32,'gr'=4,'gc'=4] {'obs'}, dimensions={1}, use_global_device_ids=true | all-gather | bytes 540672 | tf_op jit(solution)/shard_map/all_gather | solution.py:37
  288.2 62.8 %all-reduce.4 = (f32[256]{0:T(256)S(1)}, f32[256]{0:T(256)S(1)}, f32[256]{0:T(256)S(1)}, f32[256]{0:T(256)S(1)}) all-reduce(f32[256]{0:T(256)S(1)} %fusion.54, f32[256]{0:T(256)S(1)} %fusion.52, f32[256]{0:T(256)S(1)} %fusion.53, f32[256]{0:T(256)S(1)} %fusion.55), channel_id=1, replica_groups=mesh['obs'=32,'gr'=4,'gc'=4] {'obs'}, use_global_device_ids=true, to_apply=%add.2 | all-reduce | flops 1024 | bytes 8192
  351.0 8.8 %fusion.13 = (f32[1,256,512,1]{2,1,3,0:T(8,128)S(1)}, f32[1,256,512,1]{2,1,3,0:T(8,128)S(1)}, f32[1,256,512,1]{2,1,3,0:T(8,128)S(1)}, f32[1,256,512,1]{2,1,3,0:T...) fusion(f32[1,256,512]{2,1,0:T(8,128)S(1)} %all_gather.57, ...), kind=kLoop, calls=%fused_computation.26 | loop fusion | flops 1572864 | bytes 6297600 | tf_op jit(solution)/shard_map/stack | solution.py:11
  363.3 2.7 pad_maximum_fusion
  366.0 1.6 copy.58
  367.6 1.7 reshape.708
  372.5 1.5 copy.62
  374.1 1.7 reshape.714
  375.8 2.3 fusion.24
  378.1 2.3 copy.70
  380.3 2.9 reshape.726
  383.2 3.3 fusion.16
  387.5 4.3 all-to-all-start
  395.2 108.4 %all-gather.2 = f32[512,256]{1,0:T(8,128)} all-gather(f32[32,256]{1,0:T(8,128)S(1)} %fusion.22), channel_id=4, replica_groups=mesh['obs'=32,'gr'=4,'gc'=4] {'gr','gc'}, dimensions={0}, use_global_device_ids=true | all-gather | bytes 557056 | tf_op jit(solution)/shard_map/all_gather | solution.py:51
  503.6 7.2 %all-to-all-start.1 = ((f32[32,1,256]{2,1,0:T(1,128)}), f32[32,1,256]{2,1,0:T(1,128)S(1)}, u32[]{:S(2)}, u32[]{:S(2)}) async-start(f32[32,1,256]{2,1,0:T(1,128)} %reshape.763), calls=%async_computation.1 | async-start | bytes 65536 | tf_op jit(solution)/shard_map/all_to_all | solution.py:47
  512.9 28.4 %all-gather = f32[512,256]{1,0:T(8,128)} all-gather(f32[32,256]{1,0:T(8,128)S(1)} %fusion.30), channel_id=2, replica_groups=mesh['obs'=32,'gr'=4,'gc'=4] {'gr','gc'}, dimensions={0}, use_global_device_ids=true | all-gather | bytes 557056 | tf_op jit(solution)/shard_map/all_gather | solution.py:51
  541.3 10.0 %all-to-all-start.3 = ((f32[32,1,256]{2,1,0:T(1,128)}), f32[32,1,256]{2,1,0:T(1,128)S(1)}, u32[]{:S(2)}, u32[]{:S(2)}) async-start(f32[32,1,256]{2,1,0:T(1,128)} %reshape.765), calls=%async_computation.3 | async-start | bytes 65536 | tf_op jit(solution)/shard_map/all_to_all | solution.py:47
  553.4 37.7 %all-gather.1 = f32[512,256]{1,0:T(8,128)} all-gather(f32[32,256]{1,0:T(8,128)S(1)} %fusion.26), channel_id=3, replica_groups=mesh['obs'=32,'gr'=4,'gc'=4] {'gr','gc'}, dimensions={0}, use_global_device_ids=true | all-gather | bytes 557056 | tf_op jit(solution)/shard_map/all_gather | solution.py:51
  593.2 26.7 %all-gather.3 = f32[512,256]{1,0:T(8,128)S(1)} all-gather(f32[32,256]{1,0:T(8,128)S(1)} %fusion.18), channel_id=5, replica_groups=mesh['obs'=32,'gr'=4,'gc'=4] {'gr','gc'}, dimensions={0}, use_global_device_ids=true | all-gather | bytes 557056 | tf_op jit(solution)/shard_map/all_gather | solution.py:51
  620.0 2.9 fusion.63
  622.9 1.9 fusion.61
  624.8 1.9 fusion.62
  626.7 3.6 add_add_fusion
  (84 shorter events, 25.4 us)
Async XLA Ops:
  2.0 4.3 copy-start.8
  2.0 4.9 copy-start.7
  6.9 0.6 copy-start.6
  11.7 87.5 %copy-start.9 = (f32[4,8]{1,0:T(4,128)S(1)}, f32[4,8]{1,0:T(4,128)}, u32[]{:S(2)}) copy-start(f32[4,8]{1,0:T(4,128)} %param.5) | copy-start | bytes 388
  15.5 372.0 %all-to-all-start.2 = ((f32[32,1,256]{2,1,0:T(1,128)}), f32[32,1,256]{2,1,0:T(1,128)}, u32[]{:S(2)}, u32[]{:S(2)}) async-start(f32[32,1,256]{2,1,0:T(1,128)} %reshape.759), calls=%async_computation.2 | async-start | bytes 65536 | tf_op jit(solution)/shard_map/all_to_all | solution.py:47
  361.0 1.3 copy-start.5
  366.0 3.4 copy-start.1
  369.3 1.2 copy-start.2
  387.5 116.2 %all-to-all-start = ((f32[32,1,256]{2,1,0:T(1,128)}), f32[32,1,256]{2,1,0:T(1,128)S(1)}, u32[]{:S(2)}, u32[]{:S(2)}) async-start(f32[32,1,256]{2,1,0:T(1,128)} %reshape.761), calls=%async_computation | async-start | bytes 65536 | tf_op jit(solution)/shard_map/all_to_all | solution.py:47
  503.6 37.6 %all-to-all-start.1 = ((f32[32,1,256]{2,1,0:T(1,128)}), f32[32,1,256]{2,1,0:T(1,128)S(1)}, u32[]{:S(2)}, u32[]{:S(2)}) async-start(f32[32,1,256]{2,1,0:T(1,128)} %reshape.763), calls=%async_computation.1 | async-start | bytes 65536 | tf_op jit(solution)/shard_map/all_to_all | solution.py:47
  541.3 49.9 %all-to-all-start.3 = ((f32[32,1,256]{2,1,0:T(1,128)}), f32[32,1,256]{2,1,0:T(1,128)S(1)}, u32[]{:S(2)}, u32[]{:S(2)}) async-start(f32[32,1,256]{2,1,0:T(1,128)} %reshape.765), calls=%async_computation.3 | async-start | bytes 65536 | tf_op jit(solution)/shard_map/all_to_all | solution.py:47
  593.2 29.7 %copy-start.3 = (f32[512,256]{1,0:T(8,128)S(1)}, f32[512,256]{1,0:T(8,128)}, u32[]{:S(2)}) copy-start(f32[512,256]{1,0:T(8,128)} %all-gather) | copy-start | bytes 1572868
  622.9 1.9 copy-start.4
  624.8 1.9 copy-start
where the time goes:
time: 631 us; the launch traced here: 630 us
  blocking collectives  520 us (82%)
  starting transfers between devices  35.1 us (6%)
  local copies, waits for them, and re-layouts  32.2 us (5%)
  matrix products  23 us (4%)
  other arithmetic  18.8 us (3%)
    all_gather x4, blocking collectives, shards(): value_rows = lax.all_gather(col_values, 'obs', axis=1, tiled=True)  256 us
    all_gather x4, blocking collectives, shards(): lax.all_gather(own_rows, ('gr', 'gc'), axis=1, tiled=True)  201 us
    unnamed x1, blocking collectives  62.8 us
    all_to_all x4, starting transfers between devices, shards(): lax.all_to_all(outgoing, 'obs', split_axis=2, concat_axis=1, tiled=True)  35.1 us
    another operation x7, other arithmetic, trig_design(): jnp.stack([values * jnp.cos(angles), values * jnp.sin(angles)], axis=-1)  12.7 us
  transfers between devices with their start and end apart: 4, of which 0 were waited for; matrix products, arithmetic and copies ran while one was open for 7% of the time, Pallas kernels for 0%

commit v1 on v0

v1 whole, which is shorter than its diff:
```python
import jax
import jax.numpy as jnp
from jax import lax
from jax.sharding import PartitionSpec as P

highest = lax.Precision.HIGHEST
LANES = 128


def trig_design(values, angles):
    stacked = jnp.stack([values * jnp.cos(angles), values * jnp.sin(angles)], axis=-1)
    return stacked.reshape(values.shape[:-1] + (2 * values.shape[-1],))


def shards(legendre, longitude, orders, whitening):
    arcs, epochs_local, pairs_total = legendre.shape
    obs_count = lax.axis_size("obs")
    grid_count = lax.axis_size(("gr", "gc"))
    grid_position = lax.axis_index(("gr", "gc"))
    obs_position = lax.axis_index("obs")
    row_pairs = pairs_total // obs_count
    col_pairs = pairs_total // grid_count
    order_values = orders.astype(jnp.float32)

    col_values = lax.dynamic_slice_in_dim(legendre, grid_position * col_pairs, col_pairs, 2)
    row_values = legendre.reshape(arcs, epochs_local, obs_count, row_pairs)
    lon_slab = jnp.broadcast_to(longitude[:, :, None], (arcs, epochs_local, LANES))
    payload = jnp.concatenate(
        [
            jnp.broadcast_to(col_values[:, :, None], (arcs, epochs_local, obs_count, col_pairs)),
            row_values,
            jnp.broadcast_to(lon_slab[:, :, None], (arcs, epochs_local, obs_count, LANES)),
        ],
        axis=3,
    )
    payload = jnp.moveaxis(payload, 2, 0)
    arrived = lax.all_to_all(payload, "obs", 0, 0, tiled=True)
    arrived = jnp.moveaxis(arrived, 0, 1).reshape(arcs, obs_count * epochs_local, -1)

    col_all = arrived[:, :, :col_pairs]
    row_all = arrived[:, :, col_pairs : col_pairs + row_pairs]
    lon_all = arrived[:, :, col_pairs + row_pairs]

    col_orders = lax.dynamic_slice_in_dim(order_values, grid_position * col_pairs, col_pairs, 0)
    row_orders = lax.dynamic_slice_in_dim(order_values, obs_position * row_pairs, row_pairs, 0)
    col_design = trig_design(col_all, lon_all[:, :, None] * col_orders)
    row_design = trig_design(row_all, lon_all[:, :, None] * row_orders)

    col_white = jnp.einsum("afe,aec->afc", whitening, col_design, precision=highest)
    row_white = jnp.einsum("afe,aer->afr", whitening, row_design, precision=highest)
    return jnp.einsum("afr,afc->rc", row_white, col_white, precision=highest)


def solution(mesh):
    placed = (P(None, "obs", None), P(None, "obs"), P(), P())
    return jax.shard_map(
        shards, mesh=mesh, in_specs=placed, out_specs=P("obs", ("gr", "gc")), check_vma=False
    )
```

time: 631 us -> 158 us (0.25)
  the two profiles are of different devices: /device:TPU:1 before, /device:TPU:46 now
where the time goes in v1:
time: 158 us; the launch traced here: 157 us
  waiting for transfers between devices  95.9 us (61%)
  other arithmetic  19.3 us (12%)
  local copies, waits for them, and re-layouts  14.6 us (9%)
  matrix products  14.5 us (9%)
  starting transfers between devices  12.9 us (8%)
    all_to_all x1, waiting for transfers between devices, shards(): arrived = lax.all_to_all(payload, 'obs', 0, 0, tiled=True)  95.9 us
    another operation x4, other arithmetic, trig_design(): jnp.stack([values * jnp.cos(angles), values * jnp.sin(angles)], axis=-1)  17.1 us
    all_to_all x1, starting transfers between devices, shards(): arrived = lax.all_to_all(payload, 'obs', 0, 0, tiled=True)  12.9 us
    dot_general x1, matrix products, shards(): return jnp.einsum('afr,afc->rc', row_white, col_white, precision=highest)  8.23 us
    another operation x2, local copies, waits for them, and re-layouts, trig_design(): jnp.stack([values * jnp.cos(angles), values * jnp.sin(angles)], axis=-1)  7.72 us
    dot_general x1, matrix products, shards(): jnp.einsum('afe,aec->afc', whitening, col_design, precision=highest)  4.14 us
  transfers between devices with their start and end apart: 1, of which 1 were waited for; matrix products, arithmetic and copies ran while one was open for 0% of the time, Pallas kernels for 0%

profile of v1, /device:TPU:46, one launch (start us, length us, event | category | flops | bytes accessed | tf_op | source)
XLA Modules:
  0.0 157.4 jit_solution(15769668845248288372)
XLA Ops:
  0.0 0.0 copy-start
  0.0 0.0 copy-start.4
  0.0 0.9 constant_dynamic-slice_fusion
  1.0 1.4 copy.30
  2.3 0.0 copy-done.4
  2.3 0.1 broadcast_in_dim_broadcast_in_dim_broadcast_in_dim.2
  2.4 0.3 broadcast_in_dim.2
  2.7 2.2 %maximum_bitcast_fusion = f32[32,4,8,896]{3,2,1,0:T(8,128)} fusion(f32[4,8,32,128]{3,1,0,2:T(8,128)S(1)} %broadcast_in_dim_broadcast_in_dim_broadcast_in_dim.2, f32[4,8,32,256]{3,1,0,2:T(8,128)S(1)} %bitcast.40, f32[4,8,32,512]{3,1,0,2:T(8,128)S(1)} %broadcast_in_dim.2), kind=kLoop, calls=%fused_computation.5 | loop fusion | flops 1835008 | bytes 7340032 | tf_op jit(solution)/shard_map/transpose | solution.py:36
  4.9 0.0 copy-start.3
  4.9 12.9 %all-to-all-start = ((f32[32,4,8,896]{3,2,1,0:T(8,128)}), f32[32,4,8,896]{3,2,1,0:T(8,128)}, u32[]{:S(2)}, u32[]{:S(2)}) async-start(f32[32,4,8,896]{3,2,1,0:T(8,128)} %maximum_bitcast_fusion), calls=%async_computation | async-start | bytes 7340032 | tf_op jit(solution)/shard_map/all_to_all | solution.py:37
  17.8 0.0 copy-done.3
  17.8 0.1 dynamic_slice.11
  17.9 0.1 dynamic_slice.10
  18.0 95.9 %all-to-all-done = f32[32,4,8,896]{3,2,1,0:T(8,128)} async-done(((f32[32,4,8,896]{3,2,1,0:T(8,128)}), f32[32,4,8,896]{3,2,1,0:T(8,128)}, u32[]{:S(2)}, u32[]{:S(2)}) %all-to-all-start) | async-done | bytes 3670048 | tf_op jit(solution)/shard_map/all_to_all | solution.py:37
  113.9 2.3 %copy.29 = f32[32,4,8,896]{3,2,0,1:T(8,128)S(1)} copy(f32[32,4,8,896]{3,2,1,0:T(8,128)} %all-to-all-done) | data formatting | bytes 7340032 | tf_op jit(solution)/shard_map/all_to_all | solution.py:37
  116.2 0.0 copy-start.2
  116.2 0.2 slice_reduce_fusion
  116.4 1.6 copy-done.2
  118.0 3.9 %fusion.17 = (f32[4,256,256,1]{2,1,0,3:T(8,128)S(1)}, f32[4,256,256,1]{2,1,0,3:T(8,128)S(1)}) fusion(f32[4,256,896]{2,1,0:T(8,128)S(1)} %bitcast.37, f32[256]{0:T(256)S(1)} %dynamic_slice.10, f32[4,256]{1,0:T(4,128)S(1)} %slice_reduce_fusion), kind=kLoop, calls=%fused_computation.21 | loop fusion | flops 786432 | bytes 3150848 | tf_op jit(solution)/shard_map/stack | solution.py:11
  121.8 1.5 pad_maximum_fusion.1
  123.3 2.2 %copy.16 = f32[4,256,256,2]{1,0,3,2:T(4,128)S(1)} copy(f32[4,256,256,2]{2,1,0,3:T(8,128)} %pad_maximum_fusion.1) | data formatting | bytes 4194304 | tf_op jit(solution)/shard_map/stack | solution.py:11
  125.6 9.1 %fusion.5 = (f32[4,256,512,1]{2,1,0,3:T(8,128)S(1)}, f32[4,256,512,1]{2,1,0,3:T(8,128)S(1)}) fusion(f32[4,256,896]{2,1,0:T(8,128)} %bitcast.38, f32[512]{0:T(512)S(1)} %dynamic_slice.11, f32[4,256]{1,0:T(4,128)S(1)} %slice_reduce_fusion), kind=kLoop, calls=%fused_computation.10 | loop fusion | flops 1572864 | bytes 6297600 | tf_op jit(solution)/shard_map/stack | solution.py:11
  134.7 2.7 %pad_maximum_fusion = f32[4,256,512,2]{2,1,0,3:T(8,128)} fusion(f32[4,256,512,1]{2,1,0,3:T(8,128)S(1)} %get-tuple-element.6, f32[4,256,512,1]{2,1,0,3:T(8,128)S(1)} %get-tuple-element.5), kind=kLoop, calls=%fused_computation | loop fusion | flops 1048576 | bytes 8388608 | tf_op jit(solution)/shard_map/stack | solution.py:11
  137.4 5.5 %copy.18 = f32[4,256,512,2]{1,0,3,2:T(4,128)} copy(f32[4,256,512,2]{2,1,0,3:T(8,128)} %pad_maximum_fusion) | data formatting | bytes 8388608 | tf_op jit(solution)/shard_map/stack | solution.py:11
  142.8 0.0 copy-done
  142.8 0.0 copy-start.1
  142.8 2.2 %fusion.9 = f32[4,512,256]{2,1,0:T(8,128)S(1)} fusion(f32[4,256,256]{2,1,0:T(8,128)S(1)} %copy-done, f32[4,256,512]{1,0,2:T(4,128)S(1)} %bitcast.39), kind=kOutput, calls=%fused_computation.15 | convolution fusion | flops 1610612736 | bytes 5242880 | tf_op jit(solution)/shard_map/afe,aer->afr/dot_general | solution.py:50
  145.0 0.0 copy-done.1
  145.0 4.1 %fusion.2 = f32[4,1024,256]{2,1,0:T(8,128)S(1)} fusion(f32[4,256,256]{2,1,0:T(8,128)S(1)} %copy-done, f32[4,256,1024]{1,0,2:T(4,128)S(1)} %bitcast.35), kind=kOutput, calls=%fused_computation.3 | convolution fusion | flops 3221225472 | bytes 9437184 | tf_op jit(solution)/shard_map/afe,aec->afc/dot_general | solution.py:49
  149.2 8.2 %fusion.11 = f32[512,1024]{1,0:T(8,128)} fusion(f32[4,1024,256]{2,1,0:T(8,128)S(1)} %fusion.2, f32[4,512,256]{2,1,0:T(8,128)S(1)} %fusion.9), kind=kOutput, calls=%fused_computation.17 | convolution fusion | flops 6442450944 | bytes 8388608 | tf_op jit(solution)/shard_map/afr,afc->rc/dot_general | solution.py:51
  (1 shorter events, 0.0 us)
Async XLA Ops:
  0.0 142.8 %copy-start = (f32[4,256,256]{2,1,0:T(8,128)S(1)}, f32[4,256,256]{2,1,0:T(8,128)}, u32[]{:S(2)}) copy-start(f32[4,256,256]{2,1,0:T(8,128)} %param.7) | copy-start | bytes 3145732
  0.0 2.3 %copy-start.4 = (f32[4,8]{1,0:T(4,128)S(1)}, f32[4,8]{1,0:T(4,128)}, u32[]{:S(2)}) copy-start(f32[4,8]{1,0:T(4,128)} %param.5) | copy-start | bytes 388
  4.9 12.9 %copy-start.3 = (s32[8192]{0:T(1024)S(1)}, s32[8192]{0:T(1024)}, u32[]{:S(2)}) copy-start(s32[8192]{0:T(1024)} %param.6) | copy-start | bytes 98308
  4.9 109.0 %all-to-all-start = ((f32[32,4,8,896]{3,2,1,0:T(8,128)}), f32[32,4,8,896]{3,2,1,0:T(8,128)}, u32[]{:S(2)}, u32[]{:S(2)}) async-start(f32[32,4,8,896]{3,2,1,0:T(8,128)} %maximum_bitcast_fusion), calls=%async_computation | async-start | bytes 7340032 | tf_op jit(solution)/shard_map/all_to_all | solution.py:37
  116.2 1.8 %copy-start.2 = (f32[32,4,8,896]{3,2,0,1:T(8,128)}, f32[32,4,8,896]{3,2,0,1:T(8,128)S(1)}, u32[]{:S(2)}) copy-start(f32[32,4,8,896]{3,2,0,1:T(8,128)S(1)} %copy.29) | copy-start | bytes 11010052
  142.8 2.2 %copy-start.1 = (f32[4,256,512,2]{1,0,3,2:T(4,128)S(1)}, f32[4,256,512,2]{1,0,3,2:T(4,128)}, u32[]{:S(2)}) copy-start(f32[4,256,512,2]{1,0,3,2:T(4,128)} %copy.18) | copy-start | bytes 12582916

commit v2 on v1

v2 whole, which is shorter than its diff:
```python
import jax
import jax.numpy as jnp
from jax import lax
from jax.sharding import PartitionSpec as P

high = lax.Precision.HIGH
LANES = 128


def shards(legendre, longitude, orders, whitening):
    arcs, epochs_local, pairs_total = legendre.shape
    obs_count = lax.axis_size("obs")
    grid_count = lax.axis_size(("gr", "gc"))
    grid_position = lax.axis_index(("gr", "gc"))
    obs_position = lax.axis_index("obs")
    row_pairs = pairs_total // obs_count
    col_pairs = pairs_total // grid_count
    width = col_pairs + row_pairs
    epochs = obs_count * epochs_local
    order_values = orders.astype(jnp.float32)

    col_values = lax.dynamic_slice_in_dim(legendre, grid_position * col_pairs, col_pairs, 2)
    row_values = legendre.reshape(arcs, epochs_local, obs_count, row_pairs)
    data = jnp.concatenate(
        [jnp.broadcast_to(col_values[:, :, None], (arcs, epochs_local, obs_count, col_pairs)), row_values],
        axis=3,
    )
    data = jnp.transpose(data, (2, 1, 0, 3)).reshape(obs_count, epochs_local, arcs * width)
    lon_tile = jnp.pad(longitude.T, ((0, 0), (0, LANES - arcs)))
    lon_tile = jnp.broadcast_to(lon_tile[None], (obs_count, epochs_local, LANES))
    payload = jnp.concatenate([data, lon_tile], axis=2)
    arrived = lax.all_to_all(payload, "obs", 0, 0, tiled=True).reshape(epochs, arcs * width + LANES)
    lon_all = arrived[:, arcs * width : arcs * width + arcs]

    col_orders = lax.dynamic_slice_in_dim(order_values, grid_position * col_pairs, col_pairs, 0)
    row_orders = lax.dynamic_slice_in_dim(order_values, obs_position * row_pairs, row_pairs, 0)

    total = None
    for arc in range(arcs):
        block = arrived[:, arc * width : (arc + 1) * width]
        angles = lon_all[:, arc : arc + 1]
        col_values_all = block[:, :col_pairs]
        row_values_all = block[:, col_pairs:]
        col_angles = angles * col_orders
        row_angles = angles * row_orders
        col_design = jnp.concatenate(
            [col_values_all * jnp.cos(col_angles), col_values_all * jnp.sin(col_angles)], axis=1
        )
        row_design = jnp.concatenate(
            [row_values_all * jnp.cos(row_angles), row_values_all * jnp.sin(row_angles)], axis=1
        )
        col_white = jnp.dot(whitening[arc], col_design, precision=high)
        row_white = jnp.dot(whitening[arc], row_design, precision=high)
        part = lax.dot_general(row_white, col_white, (((0,), (0,)), ((), ())), precision=high)
        total = part if total is None else total + part
    halves = []
    for part_rows in (total[:row_pairs], total[row_pairs:]):
        paired = jnp.stack([part_rows[:, :col_pairs], part_rows[:, col_pairs:]], axis=-1)
        halves.append(paired.reshape(row_pairs, 2 * col_pairs))
    return jnp.stack(halves, axis=1).reshape(2 * row_pairs, 2 * col_pairs)


def solution(mesh):
    placed = (P(None, "obs", None), P(None, "obs"), P(), P())
    return jax.shard_map(
        shards, mesh=mesh, in_specs=placed, out_specs=P("obs", ("gr", "gc")), check_vma=False
    )
```

time: 158 us -> 147 us (0.930)
  the two profiles are of different devices: /device:TPU:46 before, /device:TPU:42 now
where the time goes in v2:
time: 147 us
  waiting for transfers between devices  84.1 us (57%)
  local copies, waits for them, and re-layouts  20.4 us (14%)
  other arithmetic  17.9 us (12%)
  starting transfers between devices  12.8 us (9%)
  matrix products  11.1 us (8%)
    all_to_all x1, waiting for transfers between devices, shards(): lax.all_to_all(payload, 'obs', 0, 0, tiled=True)  84.1 us
    all_to_all x1, starting transfers between devices, shards(): lax.all_to_all(payload, 'obs', 0, 0, tiled=True)  12.8 us
    mul x1, other arithmetic, shards(): col_values_all * jnp.cos(col_angles)  7.75 us
    another operation x3, local copies, waits for them, and re-layouts, shards(): return jnp.stack(halves, axis=1).reshape(2 * row_pairs, 2 * col_pairs)  4.8 us
    dot_general x4, matrix products, shards(): lax.dot_general(row_white, col_white, (((0,), (0,)), ((), ())), precision...  4.61 us
    mul x1, other arithmetic, shards(): row_values_all * jnp.cos(row_angles)  4.09 us
    dot_general x4, matrix products, shards(): col_white = jnp.dot(whitening[arc], col_design, precision=high)  4.07 us
    reshape x1, local copies, waits for them, and re-layouts, shards(): return jnp.stack(halves, axis=1).reshape(2 * row_pairs, 2 * col_pairs)  3.65 us
  transfers between devices with their start and end apart: 1, of which 1 were waited for; matrix products, arithmetic and copies ran while one was open for 1% of the time, Pallas kernels for 0%

profile of v2, /device:TPU:42, one launch (start us, length us, event | category | flops | bytes accessed | tf_op | source)
XLA Modules:
  0.0 146.6 jit_solution(14256164899116028840)
XLA Ops:
  0.0 0.8 constant_dynamic-slice_fusion
  0.9 1.9 %copy.17 = f32[4,8,32,256]{3,0,1,2:T(4,128)S(1)} copy(f32[4,8,32,256]{3,1,2,0:T(8,128)} %bitcast.52) | data formatting | bytes 2097152 | tf_op jit(solution)/shard_map/reshape | solution.py:23
  3.3 2.5 %maximum_bitcast_fusion = f32[32,8,4,768]{3,2,1,0:T(4,128)} fusion(f32[4,8,32,256]{3,0,1,2:T(4,128)S(1)} %copy.17, f32[4,8,32,512]{3,0,1,2:T(4,128)S(1)} %broadcast_in_dim.4), kind=kLoop, calls=%fused_computation.1 | loop fusion | flops 786432 | bytes 6291456 | tf_op jit(solution)/shard_map/transpose | solution.py:28
  5.8 3.6 %reshape.17 = f32[32,8,3072]{2,1,0:T(8,128)S(1)} reshape(f32[32,8,4,768]{3,2,1,0:T(4,128)} %maximum_bitcast_fusion) | data formatting | bytes 6291456 | tf_op jit(solution)/shard_map/reshape | solution.py:28
  9.5 1.9 %pad_maximum_fusion = f32[32,8,3200]{2,1,0:T(8,128)} fusion(f32[32,8,128]{2,1,0:T(8,128)S(1)} %broadcast_in_dim.5, f32[32,8,3072]{2,1,0:T(8,128)S(1)} %reshape.17), kind=kLoop, calls=%fused_computation | loop fusion | flops 819200 | bytes 6553600 | tf_op jit(solution)/shard_map/concatenate | solution.py:31
  11.4 12.8 %all-to-all-start = ((f32[32,8,3200]{2,1,0:T(8,128)}), f32[32,8,3200]{2,1,0:T(8,128)S(1)}, u32[]{:S(2)}, u32[]{:S(2)}) async-start(f32[32,8,3200]{2,1,0:T(8,128)} %pad_maximum_fusion), calls=%async_computation | async-start | bytes 6553600 | tf_op jit(solution)/shard_map/all_to_all | solution.py:32
  24.4 0.6 dynamic_slice.10
  25.0 84.1 %all-to-all-done = f32[32,8,3200]{2,1,0:T(8,128)S(1)} async-done(((f32[32,8,3200]{2,1,0:T(8,128)}), f32[32,8,3200]{2,1,0:T(8,128)S(1)}, u32[]{:S(2)}, u32[]{:S(2)}) %all-to-all-start) | async-done | bytes 3276832 | tf_op jit(solution)/shard_map/all_to_all | solution.py:32
  109.1 0.8 fusion.72
  109.9 1.0 copy.29
  110.9 1.0 copy.26
  112.1 7.8 %fusion.22 = (f32[256,512]{1,0:T(8,128)S(1)}, f32[256,512]{1,0:T(8,128)S(1)}, f32[256,512]{1,0:T(8,128)S(1)}, f32[256,512]{1,0:T(8,128)S(1)}, f32[256,512]{1,0:T...) fusion(f32[256,3200]{1,0:T(8,128)S(1)} %bitcast.50, f32[256]{0:T(256)S(1)} %bitcast.53, ...), kind=kLoop, calls=%fused_computation.36 | loop fusion | flops 1572864 | bytes 6297600 | tf_op jit(solution)/shard_map/mul | solution.py:47
  119.9 4.1 %fusion.46 = (f32[256,256]{1,0:T(8,128)S(1)}, f32[256,256]{1,0:T(8,128)S(1)}, f32[256,256]{1,0:T(8,128)S(1)}, f32[256,256]{1,0:T(8,128)S(1)}, f32[256,256]{1,0:T...) fusion(f32[256,3200]{1,0:T(8,128)S(1)} %bitcast.51, f32[256]{0:T(256)S(1)} %bitcast.54, ...), kind=kLoop, calls=%fused_computation.72 | loop fusion | flops 786432 | bytes 3150848 | tf_op jit(solution)/shard_map/mul | solution.py:50
  124.0 1.0 fusion.12
  125.0 0.6 fusion.36
  125.6 1.0 fusion.4
  126.6 0.6 fusion.28
  127.3 1.0 fusion.74
  128.3 1.0 fusion
  129.3 0.6 fusion.24
  129.9 1.0 fusion.73
  131.0 1.0 fusion.8
  132.0 0.6 fusion.32
  132.7 1.0 fusion.75
  133.7 1.5 %add_add_fusion = f32[512,1024]{1,0:T(8,128)S(1)} fusion(f32[512,1024]{1,0:T(8,128)S(1)} %fusion.75, f32[512,1024]{1,0:T(8,128)S(1)} %fusion.73, f32[512,1024]{1,0:T(8,128)S(1)} %fusion.74, f32[512,256]{1,0:T(8,128)S(1)} %fusion.36, f32[1024,256]{1,0:T(8,128)S(1)} %fusion.12), kind=kOutput, calls=%fused_computation.3 | convolution fusion | flops 806879232 | bytes 9961472 | tf_op jit(solution)/shard_map/dot_general | solution.py:54
  135.6 0.6 copy.23
  136.2 0.7 stack_reshape.6
  136.9 0.6 copy.24
  137.5 1.7 %stack_reshape.7 = f32[256,1,1024]{0,2,1:T(8,128)} reshape(f32[256,512,2]{0,2,1:T(2,128)S(1)} %copy.24) | data formatting | bytes 2097152 | tf_op jit(solution)/shard_map/stack;reshape | solution.py:60
  139.2 1.4 pad_maximum_fusion.1
  140.6 2.4 %copy.25 = f32[256,2,1024]{2,1,0:T(2,128)} copy(f32[256,2,1024]{0,2,1:T(8,128)S(1)} %pad_maximum_fusion.1) | data formatting | bytes 4194304 | tf_op jit(solution)/shard_map/stack | solution.py:60
  143.0 3.6 %reshape.19 = f32[512,1024]{1,0:T(8,128)} reshape(f32[256,2,1024]{2,1,0:T(2,128)} %copy.25) | data formatting | bytes 4194304 | tf_op jit(solution)/shard_map/reshape | solution.py:60
  (19 shorter events, 1.3 us)
Async XLA Ops:
  5.8 3.6 %copy-start.3 = (f32[4,8]{1,0:T(4,128)S(1)}, f32[4,8]{1,0:T(4,128)}, u32[]{:S(2)}) copy-start(f32[4,8]{1,0:T(4,128)} %param.5) | copy-start | bytes 388
  11.4 12.8 %copy-start.1 = (s32[8192]{0:T(1024)S(1)}, s32[8192]{0:T(1024)}, u32[]{:S(2)}) copy-start(s32[8192]{0:T(1024)} %param.6) | copy-start | bytes 98308
  11.4 97.7 %all-to-all-start = ((f32[32,8,3200]{2,1,0:T(8,128)}), f32[32,8,3200]{2,1,0:T(8,128)S(1)}, u32[]{:S(2)}, u32[]{:S(2)}) async-start(f32[32,8,3200]{2,1,0:T(8,128)} %pad_maximum_fusion), calls=%async_computation | async-start | bytes 6553600 | tf_op jit(solution)/shard_map/all_to_all | solution.py:32
  112.1 7.8 %copy-start.2 = (f32[256]{0:T(256)S(1)}, f32[256]{0:T(256)}, u32[]{:S(2)}) copy-start(f32[256]{0:T(256)} %dynamic_slice.10) | copy-start | bytes 3076
  119.8 4.1 %copy-start = (f32[4,256,256]{2,1,0:T(8,128)S(1)}, f32[4,256,256]{2,1,0:T(8,128)}, u32[]{:S(2)}) copy-start(f32[4,256,256]{2,1,0:T(8,128)} %param.7) | copy-start | bytes 3145732

commit v3 on v2

--- a/solution.py
+++ b/solution.py
@@ -5,6 +5,36 @@
 
 high = lax.Precision.HIGH
 LANES = 128
+
+
+def split3(x):
+    hi = lax.reduce_precision(x, exponent_bits=8, mantissa_bits=7)
+    rest = x - hi
+    mid = lax.reduce_precision(rest, exponent_bits=8, mantissa_bits=7)
+    return [p.astype(jnp.bfloat16) for p in (hi, mid, rest - mid)]
+
+
+def permute_exact(x, perm, left=False):
+    out = None
+    for piece in split3(x):
+        if left:
+            term = jnp.dot(perm, piece, preferred_element_type=jnp.float32)
+        else:
+            term = jnp.dot(piece, perm, preferred_element_type=jnp.float32)
+        out = term if out is None else out + term
+    return out
+
+
+def col_perm(half):
+    src = lax.broadcasted_iota(jnp.int32, (2 * half, 2 * half), 0)
+    dst = lax.broadcasted_iota(jnp.int32, (2 * half, 2 * half), 1)
+    return (dst == 2 * (src % half) + src // half).astype(jnp.bfloat16)
+
+
+def row_perm(half):
+    dst = lax.broadcasted_iota(jnp.int32, (2 * half, 2 * half), 0)
+    src = lax.broadcasted_iota(jnp.int32, (2 * half, 2 * half), 1)
+    return (dst == 2 * (src % half) + src // half).astype(jnp.bfloat16)
 
 
 def shards(legendre, longitude, orders, whitening):
@@ -19,16 +49,14 @@
     epochs = obs_count * epochs_local
     order_values = orders.astype(jnp.float32)
 
-    col_values = lax.dynamic_slice_in_dim(legendre, grid_position * col_pairs, col_pairs, 2)
-    row_values = legendre.reshape(arcs, epochs_local, obs_count, row_pairs)
-    data = jnp.concatenate(
-        [jnp.broadcast_to(col_values[:, :, None], (arcs, epochs_local, obs_count, col_pairs)), row_values],
-        axis=3,
-    )
-    data = jnp.transpose(data, (2, 1, 0, 3)).reshape(obs_count, epochs_local, arcs * width)
+    pieces = []
+    for arc in range(arcs):
+        col_values = lax.dynamic_slice_in_dim(legendre[arc], grid_position * col_pairs, col_pairs, 1)
+        pieces.append(jnp.broadcast_to(col_values[None], (obs_count, epochs_local, col_pairs)))
+        pieces.append(jnp.transpose(legendre[arc].reshape(epochs_local, obs_count, row_pairs), (1, 0, 2)))
     lon_tile = jnp.pad(longitude.T, ((0, 0), (0, LANES - arcs)))
-    lon_tile = jnp.broadcast_to(lon_tile[None], (obs_count, epochs_local, LANES))
-    payload = jnp.concatenate([data, lon_tile], axis=2)
+    pieces.append(jnp.broadcast_to(lon_tile[None], (obs_count, epochs_local, LANES)))
+    payload = jnp.concatenate(pieces, axis=2)
     arrived = lax.all_to_all(payload, "obs", 0, 0, tiled=True).reshape(epochs, arcs * width + LANES)
     lon_all = arrived[:, arcs * width : arcs * width + arcs]
 
@@ -53,12 +81,7 @@
         row_white = jnp.dot(whitening[arc], row_design, precision=high)
         part = lax.dot_general(row_white, col_white, (((0,), (0,)), ((), ())), precision=high)
         total = part if total is None else total + part
-    halves = []
-    for part_rows in (total[:row_pairs], total[row_pairs:]):
-        paired = jnp.stack([part_rows[:, :col_pairs], part_rows[:, col_pairs:]], axis=-1)
-        halves.append(paired.reshape(row_pairs, 2 * col_pairs))
-    return jnp.stack(halves, axis=1).reshape(2 * row_pairs, 2 * col_pairs)
-
+    return permute_exact(permute_exact(total, col_perm(col_pairs)), row_perm(row_pairs), left=True)
 
 def solution(mesh):
     placed = (P(None, "obs", None), P(None, "obs"), P(), P())

time: 147 us -> 140 us (0.952)
  the two profiles are of different devices: /device:TPU:42 before, /device:TPU:46 now
where the time goes in v3:
time: 140 us; the launch traced here: 139 us
  waiting for transfers between devices  84.6 us (60%)
  matrix products  20.5 us (15%)
  starting transfers between devices  12.8 us (9%)
  other arithmetic  11.9 us (8%)
  local copies, waits for them, and re-layouts  9.2 us (7%)
    all_to_all x1, waiting for transfers between devices, shards(): lax.all_to_all(payload, 'obs', 0, 0, tiled=True)  84.6 us
    all_to_all x1, starting transfers between devices, shards(): lax.all_to_all(payload, 'obs', 0, 0, tiled=True)  12.8 us
    mul x1, other arithmetic, shards(): col_values_all * jnp.cos(col_angles)  7.76 us
    unnamed x15, local copies, waits for them, and re-layouts  6.71 us
    dot_general x3, matrix products, permute_exact(): term = jnp.dot(piece, perm, preferred_element_type=jnp.float32)  5.68 us
    dot_general x4, matrix products, shards(): lax.dot_general(row_white, col_white, (((0,), (0,)), ((), ())), precision...  4.61 us
    mul x1, other arithmetic, shards(): row_values_all * jnp.cos(row_angles)  4.09 us
    dot_general x4, matrix products, shards(): col_white = jnp.dot(whitening[arc], col_design, precision=high)  4.09 us
  transfers between devices with their start and end apart: 1, of which 1 were waited for; matrix products, arithmetic and copies ran while one was open for 0% of the time, Pallas kernels for 0%

profile of v3, /device:TPU:46, one launch (start us, length us, event | category | flops | bytes accessed | tf_op | source)
XLA Modules:
  0.0 139.3 jit_solution(3503950686916396910)
XLA Ops:
  0.0 1.3 fusion.92
  1.3 0.9 broadcast_dynamic-update-slice_fusion.3
  2.3 0.8 constant_dynamic-update-slice_fusion.3
  3.1 0.9 broadcast_dynamic-update-slice_fusion.2
  4.0 0.7 constant_dynamic-update-slice_fusion.2
  4.7 0.9 broadcast_dynamic-update-slice_fusion.1
  5.6 0.7 constant_dynamic-update-slice_fusion.1
  6.4 0.9 broadcast_dynamic-update-slice_fusion
  7.2 0.8 constant_dynamic-update-slice_fusion
  8.0 0.7 broadcast_dynamic-update-slice_fusion.4
  8.7 12.8 %all-to-all-start = ((f32[32,8,3200]{2,1,0:T(8,128)}), f32[32,8,3200]{2,1,0:T(8,128)S(1)}, u32[]{:S(2)}, u32[]{:S(2)}) async-start(f32[32,8,3200]{2,1,0:T(8,128)} %broadcast_dynamic-update-slice_fusion.4), calls=%async_computation | async-start | bytes 6553600 | tf_op jit(solution)/shard_map/all_to_all | solution.py:60
  21.8 84.6 %all-to-all-done = f32[32,8,3200]{2,1,0:T(8,128)S(1)} async-done(((f32[32,8,3200]{2,1,0:T(8,128)}), f32[32,8,3200]{2,1,0:T(8,128)S(1)}, u32[]{:S(2)}, u32[]{:S(2)}) %all-to-all-start) | async-done | bytes 3276832 | tf_op jit(solution)/shard_map/all_to_all | solution.py:60
  106.8 7.8 %fusion.30 = (f32[256,512]{1,0:T(8,128)S(1)}, f32[256,512]{1,0:T(8,128)S(1)}, f32[256,512]{1,0:T(8,128)S(1)}, f32[256,512]{1,0:T(8,128)S(1)}, f32[256,512]{1,0:T...) fusion(f32[256,3200]{1,0:T(8,128)S(1)} %bitcast.51, ...), kind=kLoop, calls=%fused_computation.49 | loop fusion | flops 1572864 | bytes 6297600 | tf_op jit(solution)/shard_map/mul | solution.py:75
  114.6 4.1 %fusion.54 = (f32[256,256]{1,0:T(8,128)S(1)}, f32[256,256]{1,0:T(8,128)S(1)}, f32[256,256]{1,0:T(8,128)S(1)}, f32[256,256]{1,0:T(8,128)S(1)}, f32[256,256]{1,0:T...) fusion(f32[256,3200]{1,0:T(8,128)S(1)} %bitcast.52, ...), kind=kLoop, calls=%fused_computation.81 | loop fusion | flops 786432 | bytes 3150848 | tf_op jit(solution)/shard_map/mul | solution.py:78
  118.7 1.0 fusion.20
  119.7 0.6 fusion.44
  120.3 1.0 fusion.12
  121.3 0.6 fusion.36
  122.0 1.0 fusion.94
  123.0 1.0 fusion.8
  124.1 0.6 fusion.32
  124.7 1.0 fusion.93
  125.7 1.0 fusion.16
  126.8 0.6 fusion.40
  127.4 1.0 fusion.95
  128.4 1.5 %add_add_fusion.2 = f32[512,1024]{1,0:T(8,128)S(1)} fusion(f32[512,1024]{1,0:T(8,128)S(1)} %fusion.95, f32[512,1024]{1,0:T(8,128)S(1)} %fusion.93, f32[512,1024]{1,0:T(8,128)S(1)} %fusion.94, f32[512,256]{1,0:T(8,128)S(1)} %fusion.44, f32[1024,256]{1,0:T(8,128)S(1)} %fusion.20), kind=kOutput, calls=%fused_computation.13 | convolution fusion | flops 806879232 | bytes 9961472 | tf_op jit(solution)/shard_map/dot_general | solution.py:82
  129.9 1.8 %fusion.5 = f32[512,1024]{1,0:T(8,128)S(1)} fusion(f32[512,1024]{1,0:T(8,128)S(1)} %add_add_fusion.2, s32[1024]{0:T(1024)S(1)} %get-tuple-element.45, s32[1024]{0:T(1024)S(1)} %get-tuple-element.48, s32[1024]{0:T(1024)S(1)} %get-tuple-element.46, s32[1024]{0:T(1024)S(1)} %get-tuple-element.47, pred[1024]{0:T(1024)(128)(4,1)S(1)} %get-tuple-element.49, ...), kind=kOutput, calls=%fused_computation.15 | convolution fusion | flops 1081081856 | bytes 4212736 | tf_op jit(solution)/shard_map/dot_general | solution.py:23
  131.7 2.0 %fusion.4 = f32[512,1024]{1,0:T(8,128)S(1)} fusion(f32[512,1024]{1,0:T(8,128)S(1)} %add_add_fusion.2, s32[1024]{0:T(1024)S(1)} %get-tuple-element.45, s32[1024]{0:T(1024)S(1)} %get-tuple-element.48, s32[1024]{0:T(1024)S(1)} %get-tuple-element.46, s32[1024]{0:T(1024)S(1)} %get-tuple-element.47, pred[1024]{0:T(1024)(128)(4,1)S(1)} %get-tuple-element.49, ...), kind=kOutput, calls=%fused_computation.14 | convolution fusion | flops 1080033280 | bytes 4212736 | tf_op jit(solution)/shard_map/dot_general | solution.py:23
  133.8 1.8 %add_add_fusion.1 = f32[512,1024]{1,0:T(8,128)S(1)} fusion(f32[512,1024]{1,0:T(8,128)S(1)} %fusion.4, f32[512,1024]{1,0:T(8,128)S(1)} %fusion.5, f32[512,1024]{1,0:T(8,128)S(1)} %add_add_fusion.2, s32[1024]{0:T(1024)S(1)} %get-tuple-element.45, s32[1024]{0:T(1024)S(1)} %get-tuple-element.48, s32[1024]{0:T(1024)S(1)} %get-tuple-element.46, ...), kind=kOutput, calls=%fused_computation.12 | convolution fusion | flops 1082654720 | bytes 8407040 | tf_op jit(solution)/shard_map/dot_general | solution.py:23
  135.6 0.7 fusion.7
  136.4 0.7 fusion.6
  137.1 2.2 %add_add_fusion = f32[512,1024]{1,0:T(8,128)} fusion(f32[512,1024]{1,0:T(8,128)S(1)} %fusion.6, f32[512,1024]{1,0:T(8,128)S(1)} %fusion.7, f32[512,1024]{1,0:T(8,128)S(1)} %add_add_fusion.1, s32[512]{0:T(512)S(1)} %get-tuple-element.51, s32[512]{0:T(512)S(1)} %get-tuple-element.54, s32[512]{0:T(512)S(1)} %get-tuple-element.52, ...), kind=kOutput, calls=%fused_computation.11 | convolution fusion | flops 541851648 | bytes 8397824 | tf_op jit(solution)/shard_map/dot_general | solution.py:21
  (20 shorter events, 0.7 us)
Async XLA Ops:
  0.0 2.2 %copy-start.2 = (f32[4,8]{1,0:T(4,128)S(1)}, f32[4,8]{1,0:T(4,128)}, u32[]{:S(2)}) copy-start(f32[4,8]{1,0:T(4,128)} %param.5) | copy-start | bytes 388
  8.7 12.8 %copy-start.1 = (s32[8192]{0:T(1024)S(1)}, s32[8192]{0:T(1024)}, u32[]{:S(2)}) copy-start(s32[8192]{0:T(1024)} %param.6) | copy-start | bytes 98308
  8.7 97.7 %all-to-all-start = ((f32[32,8,3200]{2,1,0:T(8,128)}), f32[32,8,3200]{2,1,0:T(8,128)S(1)}, u32[]{:S(2)}, u32[]{:S(2)}) async-start(f32[32,8,3200]{2,1,0:T(8,128)} %broadcast_dynamic-update-slice_fusion.4), calls=%async_computation | async-start | bytes 6553600 | tf_op jit(solution)/shard_map/all_to_all | solution.py:60
  114.5 4.1 %copy-start = (f32[4,256,256]{2,1,0:T(8,128)S(1)}, f32[4,256,256]{2,1,0:T(8,128)}, u32[]{:S(2)}) copy-start(f32[4,256,256]{2,1,0:T(8,128)} %param.7) | copy-start | bytes 3145732

commit v4 on v3

--- a/solution.py
+++ b/solution.py
@@ -45,20 +45,32 @@
     obs_position = lax.axis_index("obs")
     row_pairs = pairs_total // obs_count
     col_pairs = pairs_total // grid_count
-    width = col_pairs + row_pairs
     epochs = obs_count * epochs_local
     order_values = orders.astype(jnp.float32)
 
+    core = grid_position % 2
+    half_rows = row_pairs // 2
+    width = col_pairs + half_rows
     pieces = []
     for arc in range(arcs):
         col_values = lax.dynamic_slice_in_dim(legendre[arc], grid_position * col_pairs, col_pairs, 1)
         pieces.append(jnp.broadcast_to(col_values[None], (obs_count, epochs_local, col_pairs)))
-        pieces.append(jnp.transpose(legendre[arc].reshape(epochs_local, obs_count, row_pairs), (1, 0, 2)))
+        row_values = legendre[arc].reshape(epochs_local, obs_count, 2, half_rows)
+        row_values = lax.dynamic_index_in_dim(row_values, core, 2, keepdims=False)
+        pieces.append(jnp.transpose(row_values, (1, 0, 2)))
     lon_tile = jnp.pad(longitude.T, ((0, 0), (0, LANES - arcs)))
     pieces.append(jnp.broadcast_to(lon_tile[None], (obs_count, epochs_local, LANES)))
     payload = jnp.concatenate(pieces, axis=2)
     arrived = lax.all_to_all(payload, "obs", 0, 0, tiled=True).reshape(epochs, arcs * width + LANES)
     lon_all = arrived[:, arcs * width : arcs * width + arcs]
+
+    mine = jnp.stack([arrived[:, arc * width + col_pairs : (arc + 1) * width] for arc in range(arcs)])
+    gc_count = lax.axis_size("gc")
+    swap = [(k, k ^ 1) for k in range(gc_count)]
+    theirs = lax.ppermute(mine, "gc", swap)
+    row_all = jnp.where(
+        core == 0, jnp.concatenate([mine, theirs], axis=2), jnp.concatenate([theirs, mine], axis=2)
+    )
 
     col_orders = lax.dynamic_slice_in_dim(order_values, grid_position * col_pairs, col_pairs, 0)
     row_orders = lax.dynamic_slice_in_dim(order_values, obs_position * row_pairs, row_pairs, 0)
@@ -68,7 +80,7 @@
         block = arrived[:, arc * width : (arc + 1) * width]
         angles = lon_all[:, arc : arc + 1]
         col_values_all = block[:, :col_pairs]
-        row_values_all = block[:, col_pairs:]
+        row_values_all = row_all[arc]
         col_angles = angles * col_orders
         row_angles = angles * row_orders
         col_design = jnp.concatenate(

time: 140 us -> 126 us (0.900)
  the two profiles are of different devices: /device:TPU:46 before, /device:TPU:1 now
where the time goes in v4:
time: 126 us; the launch traced here: 125 us
  waiting for transfers between devices  66.6 us (53%)
  matrix products  20.2 us (16%)
  starting transfers between devices  17.2 us (14%)
  other arithmetic  12 us (10%)
  local copies, waits for them, and re-layouts  8.94 us (7%)
    all_to_all x1, waiting for transfers between devices, shards(): lax.all_to_all(payload, 'obs', 0, 0, tiled=True)  66.6 us
    all_to_all x1, starting transfers between devices, shards(): lax.all_to_all(payload, 'obs', 0, 0, tiled=True)  13.6 us
    mul x1, other arithmetic, shards(): col_values_all * jnp.cos(col_angles)  7.76 us
    unnamed x15, local copies, waits for them, and re-layouts  6.43 us
    dot_general x3, matrix products, permute_exact(): term = jnp.dot(piece, perm, preferred_element_type=jnp.float32)  5.46 us
    dot_general x4, matrix products, shards(): lax.dot_general(row_white, col_white, (((0,), (0,)), ((), ())), precision...  4.61 us
    mul x1, other arithmetic, shards(): row_values_all * jnp.cos(row_angles)  4.09 us
    dot_general x4, matrix products, shards(): col_white = jnp.dot(whitening[arc], col_design, precision=high)  4.03 us
  transfers between devices with their start and end apart: 2, of which 1 were waited for; matrix products, arithmetic and copies ran while one was open for 10% of the time, Pallas kernels for 0%

profile of v4, /device:TPU:1, one launch (start us, length us, event | category | flops | bytes accessed | tf_op | source)
XLA Modules:
  0.0 125.2 jit_solution(9398329612352478925)
XLA Ops:
  0.0 1.3 %fusion.92 = (f32[1,8,8192]{2,1,0:T(8,128)S(1)}, f32[1,8,8192]{2,1,0:T(8,128)S(1)}, f32[1,8,8192]{2,1,0:T(8,128)S(1)}, f32[1,8,8192]{2,1,0:T(8,128)S(1)}) fusion(f32[4,8,8192]{2,1,0:T(8,128)} %param.4), kind=kLoop, calls=%fused_computation.154 | loop fusion | bytes 2097152 | tf_op jit(solution)/shard_map/slice | solution.py:56
  1.3 0.9 broadcast_dynamic-update-slice_fusion.3
  2.3 0.7 bitcast_dynamic-update-slice_fusion.3
  3.0 0.9 broadcast_dynamic-update-slice_fusion.2
  3.9 0.7 bitcast_dynamic-update-slice_fusion.2
  4.5 0.9 broadcast_dynamic-update-slice_fusion.1
  5.4 0.7 bitcast_dynamic-update-slice_fusion.1
  6.1 0.9 broadcast_dynamic-update-slice_fusion
  7.0 0.7 bitcast_dynamic-update-slice_fusion
  7.7 0.7 broadcast_dynamic-update-slice_fusion.4
  8.4 13.6 %all-to-all-start = ((f32[32,8,2688]{2,1,0:T(8,128)}), f32[32,8,2688]{2,1,0:T(8,128)S(1)}, u32[]{:S(2)}, u32[]{:S(2)}) async-start(f32[32,8,2688]{2,1,0:T(8,128)} %broadcast_dynamic-update-slice_fusion.4), calls=%async_computation | async-start | bytes 5505024 | tf_op jit(solution)/shard_map/all_to_all | solution.py:64
  22.3 66.6 %all-to-all-done = f32[32,8,2688]{2,1,0:T(8,128)S(1)} async-done(((f32[32,8,2688]{2,1,0:T(8,128)}), f32[32,8,2688]{2,1,0:T(8,128)S(1)}, u32[]{:S(2)}, u32[]{:S(2)}) %all-to-all-start) | async-done | bytes 2752544 | tf_op jit(solution)/shard_map/all_to_all | solution.py:64
  89.3 3.6 %collective-permute-start = (f32[4,256,128]{2,1,0:T(8,128)S(1)}, f32[4,256,128]{2,1,0:T(8,128)S(1)}, u32[]{:S(2)}, u32[]{:S(2)}) collective-permute-start(f32[4,256,128]{2,1,0:T(8,128)S(1)} %pad_maximum_fusion), channel_id=1, source_target_pairs={{0,1},{1,0},{2,3},{3,2},{4,5},{5,4},{6,7},{7,6},{8,9},{9,8},{10,11... | collective-permute-start | bytes 1572872 | tf_op jit(solution)/shard_map/ppermute | solution.py:70
  92.9 7.8 %fusion.30 = (f32[256,512]{1,0:T(8,128)S(1)}, f32[256,512]{1,0:T(8,128)S(1)}, f32[256,512]{1,0:T(8,128)S(1)}, f32[256,512]{1,0:T(8,128)S(1)}, f32[256,512]{1,0:T...) fusion(f32[256,2688]{1,0:T(8,128)S(1)} %bitcast.96, ...), kind=kLoop, calls=%fused_computation.50 | loop fusion | flops 1572864 | bytes 6297600 | tf_op jit(solution)/shard_map/mul | solution.py:87
  100.7 1.0 fusion.20
  101.7 1.0 fusion.12
  102.7 1.0 fusion.8
  103.7 1.0 fusion.16
  104.8 4.1 %fusion.54 = (f32[256,256]{1,0:T(8,128)S(1)}, f32[256,256]{1,0:T(8,128)S(1)}, f32[256,256]{1,0:T(8,128)S(1)}, f32[256,256]{1,0:T(8,128)S(1)}, f32[256,256]{1,0:T...) fusion(f32[4,256,256]{2,1,0:T(8,128)S(1)} %maximum_select_fusion, ...), kind=kLoop, calls=%fused_computation.83 | loop fusion | flops 786432 | bytes 3150848 | tf_op jit(solution)/shard_map/mul | solution.py:90
  108.9 0.6 fusion.44
  110.2 1.0 fusion.94
  111.2 0.6 fusion.32
  111.9 1.0 fusion.93
  112.9 0.6 fusion.40
  113.6 1.0 fusion.95
  114.6 1.5 %add_add_fusion.2 = f32[512,1024]{1,0:T(8,128)S(1)} fusion(f32[512,1024]{1,0:T(8,128)S(1)} %fusion.95, f32[512,1024]{1,0:T(8,128)S(1)} %fusion.93, f32[512,1024]{1,0:T(8,128)S(1)} %fusion.94, f32[512,256]{1,0:T(8,128)S(1)} %fusion.44, f32[1024,256]{1,0:T(8,128)S(1)} %fusion.20), kind=kOutput, calls=%fused_computation.13 | convolution fusion | flops 806879232 | bytes 9961472 | tf_op jit(solution)/shard_map/dot_general | solution.py:94
  116.1 1.8 %fusion.5 = f32[512,1024]{1,0:T(8,128)S(1)} fusion(f32[512,1024]{1,0:T(8,128)S(1)} %add_add_fusion.2, s32[1024]{0:T(1024)S(1)} %get-tuple-element.51, s32[1024]{0:T(1024)S(1)} %get-tuple-element.54, s32[1024]{0:T(1024)S(1)} %get-tuple-element.52, s32[1024]{0:T(1024)S(1)} %get-tuple-element.53, pred[1024]{0:T(1024)(128)(4,1)S(1)} %get-tuple-element.55, ...), kind=kOutput, calls=%fused_computation.15 | convolution fusion | flops 1081081856 | bytes 4212736 | tf_op jit(solution)/shard_map/dot_general | solution.py:23
  117.9 1.8 %fusion.4 = f32[512,1024]{1,0:T(8,128)S(1)} fusion(f32[512,1024]{1,0:T(8,128)S(1)} %add_add_fusion.2, s32[1024]{0:T(1024)S(1)} %get-tuple-element.51, s32[1024]{0:T(1024)S(1)} %get-tuple-element.54, s32[1024]{0:T(1024)S(1)} %get-tuple-element.52, s32[1024]{0:T(1024)S(1)} %get-tuple-element.53, pred[1024]{0:T(1024)(128)(4,1)S(1)} %get-tuple-element.55, ...), kind=kOutput, calls=%fused_computation.14 | convolution fusion | flops 1080033280 | bytes 4212736 | tf_op jit(solution)/shard_map/dot_general | solution.py:23
  119.7 1.8 %add_add_fusion.1 = f32[512,1024]{1,0:T(8,128)S(1)} fusion(f32[512,1024]{1,0:T(8,128)S(1)} %fusion.4, f32[512,1024]{1,0:T(8,128)S(1)} %fusion.5, f32[512,1024]{1,0:T(8,128)S(1)} %add_add_fusion.2, s32[1024]{0:T(1024)S(1)} %get-tuple-element.51, s32[1024]{0:T(1024)S(1)} %get-tuple-element.54, s32[1024]{0:T(1024)S(1)} %get-tuple-element.52, ...), kind=kOutput, calls=%fused_computation.12 | convolution fusion | flops 1082654720 | bytes 8407040 | tf_op jit(solution)/shard_map/dot_general | solution.py:23
  121.6 0.7 fusion.7
  122.3 0.7 fusion.6
  123.0 2.2 %add_add_fusion = f32[512,1024]{1,0:T(8,128)} fusion(f32[512,1024]{1,0:T(8,128)S(1)} %fusion.6, f32[512,1024]{1,0:T(8,128)S(1)} %fusion.7, f32[512,1024]{1,0:T(8,128)S(1)} %add_add_fusion.1, s32[512]{0:T(512)S(1)} %get-tuple-element.57, s32[512]{0:T(512)S(1)} %get-tuple-element.60, s32[512]{0:T(512)S(1)} %get-tuple-element.58, ...), kind=kOutput, calls=%fused_computation.11 | convolution fusion | flops 541851648 | bytes 8397824 | tf_op jit(solution)/shard_map/dot_general | solution.py:21
  (25 shorter events, 1.4 us)
Async XLA Ops:
  0.0 2.2 %copy-start.2 = (f32[4,8]{1,0:T(4,128)S(1)}, f32[4,8]{1,0:T(4,128)}, u32[]{:S(2)}) copy-start(f32[4,8]{1,0:T(4,128)} %param.5) | copy-start | bytes 388
  8.4 13.6 %copy-start.1 = (s32[8192]{0:T(1024)S(1)}, s32[8192]{0:T(1024)}, u32[]{:S(2)}) copy-start(s32[8192]{0:T(1024)} %param.6) | copy-start | bytes 98308
  8.4 80.4 %all-to-all-start = ((f32[32,8,2688]{2,1,0:T(8,128)}), f32[32,8,2688]{2,1,0:T(8,128)S(1)}, u32[]{:S(2)}, u32[]{:S(2)}) async-start(f32[32,8,2688]{2,1,0:T(8,128)} %broadcast_dynamic-update-slice_fusion.4), calls=%async_computation | async-start | bytes 5505024 | tf_op jit(solution)/shard_map/all_to_all | solution.py:64
  89.3 15.5 %collective-permute-start = (f32[4,256,128]{2,1,0:T(8,128)S(1)}, f32[4,256,128]{2,1,0:T(8,128)S(1)}, u32[]{:S(2)}, u32[]{:S(2)}) collective-permute-start(f32[4,256,128]{2,1,0:T(8,128)S(1)} %pad_maximum_fusion), channel_id=1, source_target_pairs={{0,1},{1,0},{2,3},{3,2},{4,5},{5,4},{6,7},{7,6},{8,9},{9,8},{10,11... | collective-permute-start | bytes 1572872 | tf_op jit(solution)/shard_map/ppermute | solution.py:70
  92.9 7.8 %copy-start = (f32[4,256,256]{2,1,0:T(8,128)S(1)}, f32[4,256,256]{2,1,0:T(8,128)}, u32[]{:S(2)}) copy-start(f32[4,256,256]{2,1,0:T(8,128)} %param.7) | copy-start | bytes 3145732

commit v5 on v4

--- a/solution.py
+++ b/solution.py
@@ -37,6 +37,18 @@
     return (dst == 2 * (src % half) + src // half).astype(jnp.bfloat16)
 
 
+SLOTS = 64
+
+
+def runs_of(block_orders):
+    n = block_orders.shape[0]
+    change = (block_orders[1:] != block_orders[:-1]).astype(jnp.int32)
+    run = jnp.cumsum(jnp.concatenate([jnp.zeros((1,), jnp.int32), change]))
+    hot = run[None, :] == lax.broadcasted_iota(jnp.int32, (SLOTS, n), 0)
+    value = jnp.max(jnp.where(hot, block_orders[None, :], 0), axis=1).astype(jnp.float32)
+    return hot.astype(jnp.bfloat16), value
+
+
 def shards(legendre, longitude, orders, whitening):
     arcs, epochs_local, pairs_total = legendre.shape
     obs_count = lax.axis_size("obs")
@@ -46,7 +58,6 @@
     row_pairs = pairs_total // obs_count
     col_pairs = pairs_total // grid_count
     epochs = obs_count * epochs_local
-    order_values = orders.astype(jnp.float32)
 
     core = grid_position % 2
     half_rows = row_pairs // 2
@@ -72,22 +83,29 @@
         core == 0, jnp.concatenate([mine, theirs], axis=2), jnp.concatenate([theirs, mine], axis=2)
     )
 
-    col_orders = lax.dynamic_slice_in_dim(order_values, grid_position * col_pairs, col_pairs, 0)
-    row_orders = lax.dynamic_slice_in_dim(order_values, obs_position * row_pairs, row_pairs, 0)
+    col_hot, col_value = runs_of(lax.dynamic_slice_in_dim(orders, grid_position * col_pairs, col_pairs, 0))
+    row_hot, row_value = runs_of(lax.dynamic_slice_in_dim(orders, obs_position * row_pairs, row_pairs, 0))
+    hot = jnp.concatenate(
+        [
+            jnp.concatenate([col_hot, jnp.zeros((SLOTS, row_pairs), col_hot.dtype)], axis=1),
+            jnp.concatenate([jnp.zeros((SLOTS, col_pairs), row_hot.dtype), row_hot], axis=1),
+        ],
+        axis=0,
+    )
+    run_values = jnp.concatenate([col_value, row_value])
+    run_angles = lon_all.T[:, :, None] * run_values
+    cos_all = permute_exact(jnp.cos(run_angles), hot)
+    sin_all = permute_exact(jnp.sin(run_angles), hot)
 
     total = None
     for arc in range(arcs):
-        block = arrived[:, arc * width : (arc + 1) * width]
-        angles = lon_all[:, arc : arc + 1]
-        col_values_all = block[:, :col_pairs]
+        col_values_all = arrived[:, arc * width : arc * width + col_pairs]
         row_values_all = row_all[arc]
-        col_angles = angles * col_orders
-        row_angles = angles * row_orders
         col_design = jnp.concatenate(
-            [col_values_all * jnp.cos(col_angles), col_values_all * jnp.sin(col_angles)], axis=1
+            [col_values_all * cos_all[arc, :, :col_pairs], col_values_all * sin_all[arc, :, :col_pairs]], axis=1
         )
         row_design = jnp.concatenate(
-            [row_values_all * jnp.cos(row_angles), row_values_all * jnp.sin(row_angles)], axis=1
+            [row_values_all * cos_all[arc, :, col_pairs:], row_values_all * sin_all[arc, :, col_pairs:]], axis=1
         )
         col_white = jnp.dot(whitening[arc], col_design, precision=high)
         row_white = jnp.dot(whitening[arc], row_design, precision=high)

time: 126 us -> 129 us (1.024)
  matrix products: 20.2 us -> 34.3 us
  other arithmetic: 12 us -> 2.53 us
  waiting for transfers between devices: 66.6 us -> 63.3 us
  local copies, waits for them, and re-layouts: 8.94 us -> 10.9 us
    dot_general x3 -> x9, matrix products: 5.46 us -> 19.3 us  [permute_exact(): term = jnp.dot(piece, perm, preferred_element_type=jnp.float32)]
    mul x2, other arithmetic: 11.9 us -> 0.87 us  [the longest x1 0.66 us: shards(): col_values_all * cos_all[arc, :, :col_pairs]]
    all_to_all x1, waiting for transfers between devices: 66.6 us -> 63.3 us  [shards(): lax.all_to_all(payload, 'obs', 0, 0, tiled=True)]
    dynamic_slice x2, local copies, waits for them, and re-layouts: 0.15 us -> 1.53 us  [the longest x1 0.77 us: shards(): lax.dynamic_slice_in_dim(orders, obs_position * row_pairs, row_pairs, 0)]
    unnamed x15 -> x13, local copies, waits for them, and re-layouts: 6.43 us -> 6.94 us
where the time goes in v5:
time: 129 us
  waiting for transfers between devices  63.3 us (49%)
  matrix products  34.3 us (27%)
  starting transfers between devices  17.2 us (13%)
  local copies, waits for them, and re-layouts  10.9 us (8%)
  other arithmetic  2.53 us (2%)
    all_to_all x1, waiting for transfers between devices, shards(): lax.all_to_all(payload, 'obs', 0, 0, tiled=True)  63.3 us
    dot_general x9, matrix products, permute_exact(): term = jnp.dot(piece, perm, preferred_element_type=jnp.float32)  19.3 us
    all_to_all x1, starting transfers between devices, shards(): lax.all_to_all(payload, 'obs', 0, 0, tiled=True)  13.5 us
    unnamed x13, local copies, waits for them, and re-layouts  6.94 us
    dot_general x4, matrix products, shards(): lax.dot_general(row_white, col_white, (((0,), (0,)), ((), ())), precision...  4.87 us
    dot_general x4, matrix products, shards(): col_white = jnp.dot(whitening[arc], col_design, precision=high)  4.08 us
    ppermute x1, starting transfers between devices, shards(): theirs = lax.ppermute(mine, 'gc', swap)  3.78 us
    dot_general x3, matrix products, permute_exact(): term = jnp.dot(perm, piece, preferred_element_type=jnp.float32)  3.66 us
  transfers between devices with their start and end apart: 2, of which 1 were waited for; matrix products, arithmetic and copies ran while one was open for 10% of the time, Pallas kernels for 0%

profile of v5, /device:TPU:1, one launch (start us, length us, event | category | flops | bytes accessed | tf_op | source)
XLA Modules:
  0.0 128.7 jit_solution(8347389731297790061)
XLA Ops:
  0.0 1.3 fusion.120
  1.3 0.9 broadcast_dynamic-update-slice_fusion.3
  3.0 0.9 broadcast_dynamic-update-slice_fusion.2
  3.9 0.7 bitcast_dynamic-update-slice_fusion.2
  4.6 0.9 broadcast_dynamic-update-slice_fusion.1
  6.1 0.9 broadcast_dynamic-update-slice_fusion
  7.0 0.7 bitcast_dynamic-update-slice_fusion
  8.4 13.5 %all-to-all-start = ((f32[32,8,2688]{2,1,0:T(8,128)}), f32[32,8,2688]{2,1,0:T(8,128)S(1)}, u32[]{:S(2)}, u32[]{:S(2)}) async-start(f32[32,8,2688]{2,1,0:T(8,128)} %broadcast_dynamic-update-slice_fusion.4), calls=%async_computation | async-start | bytes 5505024 | tf_op jit(solution)/shard_map/all_to_all | solution.py:75
  21.8 0.8 dynamic_slice.39
  23.5 0.8 dynamic_slice.40
  25.4 63.3 %all-to-all-done = f32[32,8,2688]{2,1,0:T(8,128)S(1)} async-done(((f32[32,8,2688]{2,1,0:T(8,128)}), f32[32,8,2688]{2,1,0:T(8,128)S(1)}, u32[]{:S(2)}, u32[]{:S(2)}) %all-to-all-start) | async-done | bytes 2752544 | tf_op jit(solution)/shard_map/all_to_all | solution.py:75
  88.8 2.3 %fusion.54 = f32[4,256,768]{2,1,0:T(8,128)S(1)} fusion(f32[128]{0:T(128)S(1)} %pad_maximum_fusion.1, f32[4,256]{1,0:T(4,128)S(1)} %copy.8, pred[64,256]{1,0:T(32,128)(4,1)S(1)} %iota_compare_fusion.1, pred[64,512]{1,0:T(32,128)(4,1)S(1)} %iota_compare_fusion), kind=kOutput, calls=%fused_computation.86 | convolution fusion | flops 202080256 | bytes 3199488 | tf_op jit(solution)/shard_map/dot_general | solution.py:23
  91.1 2.2 %fusion.56 = f32[4,256,768]{2,1,0:T(8,128)S(1)} fusion(f32[128]{0:T(128)S(1)} %pad_maximum_fusion.1, f32[4,256]{1,0:T(4,128)S(1)} %copy.8, pred[64,256]{1,0:T(32,128)(4,1)S(1)} %iota_compare_fusion.1, pred[64,512]{1,0:T(32,128)(4,1)S(1)} %iota_compare_fusion), kind=kOutput, calls=%fused_computation.88 | convolution fusion | flops 201818112 | bytes 3199488 | tf_op jit(solution)/shard_map/dot_general | solution.py:23
  93.3 2.3 %fusion.53 = f32[4,256,768]{2,1,0:T(8,128)S(1)} fusion(f32[128]{0:T(128)S(1)} %pad_maximum_fusion.1, f32[4,256]{1,0:T(4,128)S(1)} %copy.8, pred[64,256]{1,0:T(32,128)(4,1)S(1)} %iota_compare_fusion.1, pred[64,512]{1,0:T(32,128)(4,1)S(1)} %iota_compare_fusion), kind=kOutput, calls=%fused_computation.85 | convolution fusion | flops 202080256 | bytes 3199488 | tf_op jit(solution)/shard_map/dot_general | solution.py:23
  95.6 2.2 %fusion.55 = f32[4,256,768]{2,1,0:T(8,128)S(1)} fusion(f32[128]{0:T(128)S(1)} %pad_maximum_fusion.1, f32[4,256]{1,0:T(4,128)S(1)} %copy.8, pred[64,256]{1,0:T(32,128)(4,1)S(1)} %iota_compare_fusion.1, pred[64,512]{1,0:T(32,128)(4,1)S(1)} %iota_compare_fusion), kind=kOutput, calls=%fused_computation.87 | convolution fusion | flops 201818112 | bytes 3199488 | tf_op jit(solution)/shard_map/dot_general | solution.py:23
  97.9 3.8 %collective-permute-start = (f32[4,256,128]{2,1,0:T(8,128)S(1)}, f32[4,256,128]{2,1,0:T(8,128)S(1)}, u32[]{:S(2)}, u32[]{:S(2)}) collective-permute-start(f32[4,256,128]{2,1,0:T(8,128)S(1)} %pad_maximum_fusion), channel_id=1, source_target_pairs={{0,1},{1,0},{2,3},{3,2},{4,5},{5,4},{6,7},{7,6},{8,9},{9,8},{10,11... | collective-permute-start | bytes 1572872 | tf_op jit(solution)/shard_map/ppermute | solution.py:81
  101.7 2.4 %add_add_fusion = f32[4,256,768]{2,1,0:T(8,128)S(1)} fusion(f32[4,256,768]{2,1,0:T(8,128)S(1)} %fusion.56, f32[4,256,768]{2,1,0:T(8,128)S(1)} %fusion.54, f32[128]{0:T(128)S(1)} %pad_maximum_fusion.1, f32[4,256]{1,0:T(4,128)S(1)} %copy.8, pred[64,256]{1,0:T(32,128)(4,1)S(1)} %iota_compare_fusion.1, pred[64,512]{1,0:T(32,128)(4,1)S(1)} %iota_compare_fusion), kind=kOutput, calls=%fused_computation.1 | convolution fusion | flops 203784192 | bytes 9490944 | tf_op jit(solution)/shard_map/dot_general | solution.py:23
  104.1 2.4 %add_add_fusion.1 = f32[4,256,768]{2,1,0:T(8,128)S(1)} fusion(f32[4,256,768]{2,1,0:T(8,128)S(1)} %fusion.55, f32[4,256,768]{2,1,0:T(8,128)S(1)} %fusion.53, f32[128]{0:T(128)S(1)} %pad_maximum_fusion.1, f32[4,256]{1,0:T(4,128)S(1)} %copy.8, pred[64,256]{1,0:T(32,128)(4,1)S(1)} %iota_compare_fusion.1, pred[64,512]{1,0:T(32,128)(4,1)S(1)} %iota_compare_fusion), kind=kOutput, calls=%fused_computation.2 | convolution fusion | flops 203784192 | bytes 9490944 | tf_op jit(solution)/shard_map/dot_general | solution.py:23
  107.7 1.0 fusion.20
  108.7 1.0 fusion.12
  109.7 1.0 fusion.8
  110.8 1.0 fusion.16
  113.4 1.0 fusion.122
  115.1 1.3 fusion.121
  117.0 1.0 fusion.123
  118.0 1.5 %add_add_fusion.4 = f32[512,1024]{1,0:T(8,128)S(1)} fusion(f32[512,1024]{1,0:T(8,128)S(1)} %fusion.123, f32[512,1024]{1,0:T(8,128)S(1)} %fusion.121, f32[512,1024]{1,0:T(8,128)S(1)} %fusion.122, f32[512,256]{1,0:T(8,128)S(1)} %fusion.46, f32[1024,256]{1,0:T(8,128)S(1)} %fusion.20), kind=kOutput, calls=%fused_computation.15 | convolution fusion | flops 806879232 | bytes 9961472 | tf_op jit(solution)/shard_map/dot_general | solution.py:112
  119.5 1.8 %fusion.5 = f32[512,1024]{1,0:T(8,128)S(1)} fusion(f32[512,1024]{1,0:T(8,128)S(1)} %add_add_fusion.4, s32[1024]{0:T(1024)S(1)} %get-tuple-element.43, s32[1024]{0:T(1024)S(1)} %get-tuple-element.46, s32[1024]{0:T(1024)S(1)} %get-tuple-element.44, s32[1024]{0:T(1024)S(1)} %get-tuple-element.45, pred[1024]{0:T(1024)(128)(4,1)S(1)} %get-tuple-element.47, ...), kind=kOutput, calls=%fused_computation.17 | convolution fusion | flops 1081081856 | bytes 4212736 | tf_op jit(solution)/shard_map/dot_general | solution.py:23
  121.3 1.8 %fusion.4 = f32[512,1024]{1,0:T(8,128)S(1)} fusion(f32[512,1024]{1,0:T(8,128)S(1)} %add_add_fusion.4, s32[1024]{0:T(1024)S(1)} %get-tuple-element.43, s32[1024]{0:T(1024)S(1)} %get-tuple-element.46, s32[1024]{0:T(1024)S(1)} %get-tuple-element.44, s32[1024]{0:T(1024)S(1)} %get-tuple-element.45, pred[1024]{0:T(1024)(128)(4,1)S(1)} %get-tuple-element.47, ...), kind=kOutput, calls=%fused_computation.16 | convolution fusion | flops 1080033280 | bytes 4212736 | tf_op jit(solution)/shard_map/dot_general | solution.py:23
  123.1 1.9 %add_add_fusion.3 = f32[512,1024]{1,0:T(8,128)S(1)} fusion(f32[512,1024]{1,0:T(8,128)S(1)} %fusion.4, f32[512,1024]{1,0:T(8,128)S(1)} %fusion.5, f32[512,1024]{1,0:T(8,128)S(1)} %add_add_fusion.4, s32[1024]{0:T(1024)S(1)} %get-tuple-element.43, s32[1024]{0:T(1024)S(1)} %get-tuple-element.46, s32[1024]{0:T(1024)S(1)} %get-tuple-element.44, ...), kind=kOutput, calls=%fused_computation.14 | convolution fusion | flops 1082654720 | bytes 8407040 | tf_op jit(solution)/shard_map/dot_general | solution.py:23
  125.0 0.7 fusion.7
  125.7 0.7 fusion.6
  126.5 2.2 %add_add_fusion.2 = f32[512,1024]{1,0:T(8,128)} fusion(f32[512,1024]{1,0:T(8,128)S(1)} %fusion.6, f32[512,1024]{1,0:T(8,128)S(1)} %fusion.7, f32[512,1024]{1,0:T(8,128)S(1)} %add_add_fusion.3, s32[512]{0:T(512)S(1)} %get-tuple-element.49, s32[512]{0:T(512)S(1)} %get-tuple-element.52, s32[512]{0:T(512)S(1)} %get-tuple-element.50, ...), kind=kOutput, calls=%fused_computation.13 | convolution fusion | flops 541851648 | bytes 8397824 | tf_op jit(solution)/shard_map/dot_general | solution.py:21
  (50 shorter events, 8.2 us)
Async XLA Ops:
  0.0 2.2 %copy-start.1 = (f32[4,8]{1,0:T(4,128)S(1)}, f32[4,8]{1,0:T(4,128)}, u32[]{:S(2)}) copy-start(f32[4,8]{1,0:T(4,128)} %param.5) | copy-start | bytes 388
  8.4 80.3 %all-to-all-start = ((f32[32,8,2688]{2,1,0:T(8,128)}), f32[32,8,2688]{2,1,0:T(8,128)S(1)}, u32[]{:S(2)}, u32[]{:S(2)}) async-start(f32[32,8,2688]{2,1,0:T(8,128)} %broadcast_dynamic-update-slice_fusion.4), calls=%async_computation | async-start | bytes 5505024 | tf_op jit(solution)/shard_map/all_to_all | solution.py:75
  97.9 13.9 %collective-permute-start = (f32[4,256,128]{2,1,0:T(8,128)S(1)}, f32[4,256,128]{2,1,0:T(8,128)S(1)}, u32[]{:S(2)}, u32[]{:S(2)}) collective-permute-start(f32[4,256,128]{2,1,0:T(8,128)S(1)} %pad_maximum_fusion), channel_id=1, source_target_pairs={{0,1},{1,0},{2,3},{3,2},{4,5},{5,4},{6,7},{7,6},{8,9},{9,8},{10,11... | collective-permute-start | bytes 1572872 | tf_op jit(solution)/shard_map/ppermute | solution.py:81
  106.5 1.2 copy-start

commit v6 on v5

--- a/solution.py
+++ b/solution.py
@@ -94,8 +94,9 @@
     )
     run_values = jnp.concatenate([col_value, row_value])
     run_angles = lon_all.T[:, :, None] * run_values
-    cos_all = permute_exact(jnp.cos(run_angles), hot)
-    sin_all = permute_exact(jnp.sin(run_angles), hot)
+    run_cos, run_sin = lax.optimization_barrier((jnp.cos(run_angles), jnp.sin(run_angles)))
+    cos_all = permute_exact(run_cos, hot)
+    sin_all = permute_exact(run_sin, hot)
 
     total = None
     for arc in range(arcs):

time: 129 us -> 121 us (0.938)
  matrix products: 34.3 us -> 23.9 us
  other arithmetic: 2.53 us -> 4.42 us
    dot_general x9, matrix products: 19.3 us -> 8.88 us  [permute_exact(): term = jnp.dot(piece, perm, preferred_element_type=jnp.float32)]
    sin x0 -> x1, other arithmetic: none -> 1.9 us  [shards(): jnp.sin(run_angles)]
  transfers between devices with their start and end apart: 2 -> 2, of which waited for: 1 -> 1; matrix products, arithmetic and copies ran while one was open for 10% -> 8% of each run, Pallas kernels for 0% -> 0%
where the time goes in v6:
time: 121 us; the launch traced here: 120 us
  waiting for transfers between devices  63.3 us (52%)
  matrix products  23.9 us (20%)
  starting transfers between devices  17.2 us (14%)
  local copies, waits for them, and re-layouts  10.9 us (9%)
  other arithmetic  4.42 us (4%)
    all_to_all x1, waiting for transfers between devices, shards(): lax.all_to_all(payload, 'obs', 0, 0, tiled=True)  63.3 us
    all_to_all x1, starting transfers between devices, shards(): lax.all_to_all(payload, 'obs', 0, 0, tiled=True)  13.5 us
    dot_general x9, matrix products, permute_exact(): term = jnp.dot(piece, perm, preferred_element_type=jnp.float32)  8.88 us
    unnamed x13, local copies, waits for them, and re-layouts  6.94 us
    dot_general x4, matrix products, shards(): lax.dot_general(row_white, col_white, (((0,), (0,)), ((), ())), precision...  4.85 us
    dot_general x4, matrix products, shards(): col_white = jnp.dot(whitening[arc], col_design, precision=high)  4.08 us
    ppermute x1, starting transfers between devices, shards(): theirs = lax.ppermute(mine, 'gc', swap)  3.78 us
    dot_general x3, matrix products, permute_exact(): term = jnp.dot(perm, piece, preferred_element_type=jnp.float32)  3.66 us
  transfers between devices with their start and end apart: 2, of which 1 were waited for; matrix products, arithmetic and copies ran while one was open for 8% of the time, Pallas kernels for 0%

profile of v6, /device:TPU:1, one launch (start us, length us, event | category | flops | bytes accessed | tf_op | source)
XLA Modules:
  0.0 120.2 jit_solution(713089472358544451)
XLA Ops:
  0.0 1.3 %fusion.108 = (f32[1,8,8192]{2,1,0:T(8,128)S(1)}, f32[1,8,8192]{2,1,0:T(8,128)S(1)}, f32[1,8,8192]{2,1,0:T(8,128)S(1)}, f32[1,8,8192]{2,1,0:T(8,128)S(1)}) fusion(f32[4,8,8192]{2,1,0:T(8,128)} %param.4), kind=kLoop, calls=%fused_computation.181 | loop fusion | bytes 2097152 | tf_op jit(solution)/shard_map/slice | solution.py:67
  1.3 0.9 broadcast_dynamic-update-slice_fusion.3
  2.3 0.7 bitcast_dynamic-update-slice_fusion.3
  3.0 0.9 broadcast_dynamic-update-slice_fusion.2
  3.9 0.7 bitcast_dynamic-update-slice_fusion.2
  4.6 0.9 broadcast_dynamic-update-slice_fusion.1
  5.5 0.7 bitcast_dynamic-update-slice_fusion.1
  6.1 0.9 broadcast_dynamic-update-slice_fusion
  7.0 0.7 bitcast_dynamic-update-slice_fusion
  7.7 0.7 broadcast_dynamic-update-slice_fusion.4
  8.4 13.5 %all-to-all-start = ((f32[32,8,2688]{2,1,0:T(8,128)}), f32[32,8,2688]{2,1,0:T(8,128)S(1)}, u32[]{:S(2)}, u32[]{:S(2)}) async-start(f32[32,8,2688]{2,1,0:T(8,128)} %broadcast_dynamic-update-slice_fusion.4), calls=%async_computation | async-start | bytes 5505024 | tf_op jit(solution)/shard_map/all_to_all | solution.py:75
  21.8 0.8 dynamic_slice.39
  23.5 0.8 dynamic_slice.40
  25.4 63.3 %all-to-all-done = f32[32,8,2688]{2,1,0:T(8,128)S(1)} async-done(((f32[32,8,2688]{2,1,0:T(8,128)}), f32[32,8,2688]{2,1,0:T(8,128)S(1)}, u32[]{:S(2)}, u32[]{:S(2)}) %all-to-all-start) | async-done | bytes 2752544 | tf_op jit(solution)/shard_map/all_to_all | solution.py:75
  88.8 1.9 %multiply_sine_fusion = (f32[4,256,128]{2,1,0:T(8,128)S(1)}, f32[4,256,128]{2,1,0:T(8,128)S(1)}) fusion(f32[128]{0:T(128)S(1)} %pad_maximum_fusion.1, f32[4,256]{1,0:T(4,128)S(1)} %copy.8), kind=kLoop, calls=%fused_computation.46 | loop fusion | flops 131072 | bytes 1053184 | tf_op jit(solution)/shard_map/sin | solution.py:97
  93.0 3.8 %collective-permute-start = (f32[4,256,128]{2,1,0:T(8,128)S(1)}, f32[4,256,128]{2,1,0:T(8,128)S(1)}, u32[]{:S(2)}, u32[]{:S(2)}) collective-permute-start(f32[4,256,128]{2,1,0:T(8,128)S(1)} %pad_maximum_fusion), channel_id=1, source_target_pairs={{0,1},{1,0},{2,3},{3,2},{4,5},{5,4},{6,7},{7,6},{8,9},{9,8},{10,11... | collective-permute-start | bytes 1572872 | tf_op jit(solution)/shard_map/ppermute | solution.py:81
  96.8 0.6 add_add_fusion
  98.0 0.7 fusion.27
  99.2 1.0 fusion.20
  100.2 1.0 fusion.12
  101.3 1.0 fusion.8
  102.3 1.0 fusion.16
  104.9 1.0 fusion.110
  106.6 1.0 fusion.109
  108.2 1.0 fusion.111
  109.3 1.7 %add_add_fusion.4 = f32[512,1024]{1,0:T(8,128)S(1)} fusion(f32[512,1024]{1,0:T(8,128)S(1)} %fusion.111, f32[512,1024]{1,0:T(8,128)S(1)} %fusion.109, f32[512,1024]{1,0:T(8,128)S(1)} %fusion.110, f32[512,256]{1,0:T(8,128)S(1)} %fusion.46, f32[1024,256]{1,0:T(8,128)S(1)} %fusion.20), kind=kOutput, calls=%fused_computation.15 | convolution fusion | flops 806879232 | bytes 9961472 | tf_op jit(solution)/shard_map/dot_general | solution.py:113
  111.0 1.8 %fusion.5 = f32[512,1024]{1,0:T(8,128)S(1)} fusion(f32[512,1024]{1,0:T(8,128)S(1)} %add_add_fusion.4, s32[1024]{0:T(1024)S(1)} %get-tuple-element.49, s32[1024]{0:T(1024)S(1)} %get-tuple-element.52, s32[1024]{0:T(1024)S(1)} %get-tuple-element.50, s32[1024]{0:T(1024)S(1)} %get-tuple-element.51, pred[1024]{0:T(1024)(128)(4,1)S(1)} %get-tuple-element.53, ...), kind=kOutput, calls=%fused_computation.17 | convolution fusion | flops 1081081856 | bytes 4212736 | tf_op jit(solution)/shard_map/dot_general | solution.py:23
  112.8 1.8 %fusion.4 = f32[512,1024]{1,0:T(8,128)S(1)} fusion(f32[512,1024]{1,0:T(8,128)S(1)} %add_add_fusion.4, s32[1024]{0:T(1024)S(1)} %get-tuple-element.49, s32[1024]{0:T(1024)S(1)} %get-tuple-element.52, s32[1024]{0:T(1024)S(1)} %get-tuple-element.50, s32[1024]{0:T(1024)S(1)} %get-tuple-element.51, pred[1024]{0:T(1024)(128)(4,1)S(1)} %get-tuple-element.53, ...), kind=kOutput, calls=%fused_computation.16 | convolution fusion | flops 1080033280 | bytes 4212736 | tf_op jit(solution)/shard_map/dot_general | solution.py:23
  114.6 1.9 %add_add_fusion.3 = f32[512,1024]{1,0:T(8,128)S(1)} fusion(f32[512,1024]{1,0:T(8,128)S(1)} %fusion.4, f32[512,1024]{1,0:T(8,128)S(1)} %fusion.5, f32[512,1024]{1,0:T(8,128)S(1)} %add_add_fusion.4, s32[1024]{0:T(1024)S(1)} %get-tuple-element.49, s32[1024]{0:T(1024)S(1)} %get-tuple-element.52, s32[1024]{0:T(1024)S(1)} %get-tuple-element.50, ...), kind=kOutput, calls=%fused_computation.14 | convolution fusion | flops 1082654720 | bytes 8407040 | tf_op jit(solution)/shard_map/dot_general | solution.py:23
  116.5 0.7 fusion.7
  117.2 0.7 fusion.6
  118.0 2.2 %add_add_fusion.2 = f32[512,1024]{1,0:T(8,128)} fusion(f32[512,1024]{1,0:T(8,128)S(1)} %fusion.6, f32[512,1024]{1,0:T(8,128)S(1)} %fusion.7, f32[512,1024]{1,0:T(8,128)S(1)} %add_add_fusion.3, s32[512]{0:T(512)S(1)} %get-tuple-element.55, s32[512]{0:T(512)S(1)} %get-tuple-element.58, s32[512]{0:T(512)S(1)} %get-tuple-element.56, ...), kind=kOutput, calls=%fused_computation.13 | convolution fusion | flops 541851648 | bytes 8397824 | tf_op jit(solution)/shard_map/dot_general | solution.py:21
  (51 shorter events, 8.3 us)
Async XLA Ops:
  0.0 2.2 %copy-start.1 = (f32[4,8]{1,0:T(4,128)S(1)}, f32[4,8]{1,0:T(4,128)}, u32[]{:S(2)}) copy-start(f32[4,8]{1,0:T(4,128)} %param.5) | copy-start | bytes 388
  8.4 80.3 %all-to-all-start = ((f32[32,8,2688]{2,1,0:T(8,128)}), f32[32,8,2688]{2,1,0:T(8,128)S(1)}, u32[]{:S(2)}, u32[]{:S(2)}) async-start(f32[32,8,2688]{2,1,0:T(8,128)} %broadcast_dynamic-update-slice_fusion.4), calls=%async_computation | async-start | bytes 5505024 | tf_op jit(solution)/shard_map/all_to_all | solution.py:75
  93.0 10.3 %collective-permute-start = (f32[4,256,128]{2,1,0:T(8,128)S(1)}, f32[4,256,128]{2,1,0:T(8,128)S(1)}, u32[]{:S(2)}, u32[]{:S(2)}) collective-permute-start(f32[4,256,128]{2,1,0:T(8,128)S(1)} %pad_maximum_fusion), channel_id=1, source_target_pairs={{0,1},{1,0},{2,3},{3,2},{4,5},{5,4},{6,7},{7,6},{8,9},{9,8},{10,11... | collective-permute-start | bytes 1572872 | tf_op jit(solution)/shard_map/ppermute | solution.py:81
  98.0 1.2 %copy-start = (f32[4,256,256]{2,1,0:T(8,128)S(1)}, f32[4,256,256]{2,1,0:T(8,128)}, u32[]{:S(2)}) copy-start(f32[4,256,256]{2,1,0:T(8,128)} %param.7) | copy-start | bytes 3145732

commit v7 on v6

--- a/solution.py
+++ b/solution.py
@@ -18,9 +18,9 @@
     out = None
     for piece in split3(x):
         if left:
-            term = jnp.dot(perm, piece, preferred_element_type=jnp.float32)
+            term = jnp.einsum("dk,...kc->...dc", perm, piece, preferred_element_type=jnp.float32)
         else:
-            term = jnp.dot(piece, perm, preferred_element_type=jnp.float32)
+            term = jnp.einsum("...k,kc->...c", piece, perm, preferred_element_type=jnp.float32)
         out = term if out is None else out + term
     return out
 
@@ -112,7 +112,14 @@
         row_white = jnp.dot(whitening[arc], row_design, precision=high)
         part = lax.dot_general(row_white, col_white, (((0,), (0,)), ((), ())), precision=high)
         total = part if total is None else total + part
-    return permute_exact(permute_exact(total, col_perm(col_pairs)), row_perm(row_pairs), left=True)
+    tile = LANES
+    rows_out, cols_out = total.shape
+    by_cols = total.reshape(rows_out, 2, cols_out // (2 * tile), tile)
+    by_cols = jnp.transpose(by_cols, (0, 2, 1, 3)).reshape(rows_out, cols_out // (2 * tile), 2 * tile)
+    by_cols = permute_exact(by_cols, col_perm(tile)).reshape(rows_out, cols_out)
+    by_rows = by_cols.reshape(2, rows_out // (2 * tile), tile, cols_out)
+    by_rows = jnp.transpose(by_rows, (1, 0, 2, 3)).reshape(rows_out // (2 * tile), 2 * tile, cols_out)
+    return permute_exact(by_rows, row_perm(tile), left=True).reshape(rows_out, cols_out)
 
 def solution(mesh):
     placed = (P(None, "obs", None), P(None, "obs"), P(), P())

time: 121 us -> 132 us (1.091)
  local copies, waits for them, and re-layouts: 10.9 us -> 25 us
  matrix products: 23.9 us -> 19.9 us
    transpose x0 -> x2, local copies, waits for them, and re-layouts: none -> 5.75 us  [the longest x1 4.02 us: shards(): jnp.transpose(by_cols, (0, 2, 1, 3))]
    reshape x0 -> x2, local copies, waits for them, and re-layouts: none -> 4.92 us  [the longest x1 2.93 us: shards(): jnp.transpose(by_cols, (0, 2, 1, 3))]
    dot_general x12, matrix products: 12.5 us -> 8.46 us  [the longest x9 5.69 us: permute_exact(): jnp.einsum('...k,kc->...c', piece, perm, preferred_element_type=jnp.float32)]
    another operation x3 -> x4, local copies, waits for them, and re-layouts: 0.31 us -> 2.39 us  [the longest x1 2.08 us: shards(): by_rows = by_cols.reshape(2, rows_out // (2 * tile), tile, cols_out)]
    add x0 -> x1, local copies, waits for them, and re-layouts: none -> 1.35 us  [permute_exact(): out = term if out is None else out + term]
  transfers between devices with their start and end apart: 2 -> 2, of which waited for: 1 -> 1; matrix products, arithmetic and copies ran while one was open for 8% -> 7% of each run, Pallas kernels for 0% -> 0%
where the time goes in v7:
time: 132 us; the launch traced here: 131 us
  waiting for transfers between devices  63.3 us (48%)
  local copies, waits for them, and re-layouts  25 us (19%)
  matrix products  19.9 us (15%)
  starting transfers between devices  17.2 us (13%)
  other arithmetic  5.02 us (4%)
    all_to_all x1, waiting for transfers between devices, shards(): lax.all_to_all(payload, 'obs', 0, 0, tiled=True)  63.3 us
    all_to_all x1, starting transfers between devices, shards(): lax.all_to_all(payload, 'obs', 0, 0, tiled=True)  13.5 us
    unnamed x13, local copies, waits for them, and re-layouts  6.94 us
    dot_general x9, matrix products, permute_exact(): jnp.einsum('...k,kc->...c', piece, perm, preferred_element_type=jnp.float32)  5.69 us
    dot_general x4, matrix products, shards(): lax.dot_general(row_white, col_white, (((0,), (0,)), ((), ())), precision...  4.85 us
    dot_general x4, matrix products, shards(): col_white = jnp.dot(whitening[arc], col_design, precision=high)  4.08 us
    transpose x1, local copies, waits for them, and re-layouts, shards(): jnp.transpose(by_cols, (0, 2, 1, 3))  4.02 us
    ppermute x1, starting transfers between devices, shards(): theirs = lax.ppermute(mine, 'gc', swap)  3.78 us
  transfers between devices with their start and end apart: 2, of which 1 were waited for; matrix products, arithmetic and copies ran while one was open for 7% of the time, Pallas kernels for 0%

profile of v7, /device:TPU:1, one launch (start us, length us, event | category | flops | bytes accessed | tf_op | source)
XLA Modules:
  0.0 130.8 jit_solution(9519357717154965806)
XLA Ops:
  0.0 1.3 fusion.105
  1.3 0.9 broadcast_dynamic-update-slice_fusion.3
  2.3 0.7 bitcast_dynamic-update-slice_fusion.3
  3.0 0.9 broadcast_dynamic-update-slice_fusion.2
  3.9 0.7 bitcast_dynamic-update-slice_fusion.2
  4.6 0.9 broadcast_dynamic-update-slice_fusion.1
  6.1 0.9 broadcast_dynamic-update-slice_fusion
  7.0 0.7 bitcast_dynamic-update-slice_fusion
  8.4 13.5 %all-to-all-start = ((f32[32,8,2688]{2,1,0:T(8,128)}), f32[32,8,2688]{2,1,0:T(8,128)S(1)}, u32[]{:S(2)}, u32[]{:S(2)}) async-start(f32[32,8,2688]{2,1,0:T(8,128)} %broadcast_dynamic-update-slice_fusion.4), calls=%async_computation | async-start | bytes 5505024 | tf_op jit(solution)/shard_map/all_to_all | solution.py:75
  21.8 0.8 dynamic_slice.39
  23.5 0.8 dynamic_slice.40
  25.3 63.3 %all-to-all-done = f32[32,8,2688]{2,1,0:T(8,128)S(1)} async-done(((f32[32,8,2688]{2,1,0:T(8,128)}), f32[32,8,2688]{2,1,0:T(8,128)S(1)}, u32[]{:S(2)}, u32[]{:S(2)}) %all-to-all-start) | async-done | bytes 2752544 | tf_op jit(solution)/shard_map/all_to_all | solution.py:75
  88.8 1.9 %multiply_sine_fusion = (f32[4,256,128]{2,1,0:T(8,128)S(1)}, f32[4,256,128]{2,1,0:T(8,128)S(1)}) fusion(f32[128]{0:T(128)S(1)} %pad_maximum_fusion.1, f32[4,256]{1,0:T(4,128)S(1)} %copy.13), kind=kLoop, calls=%fused_computation.42 | loop fusion | flops 131072 | bytes 1053184 | tf_op jit(solution)/shard_map/sin | solution.py:97
  93.0 3.8 %collective-permute-start = (f32[4,256,128]{2,1,0:T(8,128)S(1)}, f32[4,256,128]{2,1,0:T(8,128)S(1)}, u32[]{:S(2)}, u32[]{:S(2)}) collective-permute-start(f32[4,256,128]{2,1,0:T(8,128)S(1)} %pad_maximum_fusion), channel_id=1, source_target_pairs={{0,1},{1,0},{2,3},{3,2},{4,5},{5,4},{6,7},{7,6},{8,9},{9,8},{10,11... | collective-permute-start | bytes 1572872 | tf_op jit(solution)/shard_map/ppermute | solution.py:81
  97.3 0.7 add_add_fusion.1
  99.3 1.0 fusion.17
  100.3 1.0 fusion.9
  101.3 1.0 fusion.5
  102.3 1.0 fusion.13
  104.9 1.0 fusion.107
  106.6 1.0 fusion.106
  108.3 1.0 fusion.108
  109.4 1.7 %add_add_fusion.4 = f32[512,1024]{1,0:T(8,128)S(1)} fusion(f32[512,1024]{1,0:T(8,128)S(1)} %fusion.108, f32[512,1024]{1,0:T(8,128)S(1)} %fusion.106, f32[512,1024]{1,0:T(8,128)S(1)} %fusion.107, f32[512,256]{1,0:T(8,128)S(1)} %fusion.43, f32[1024,256]{1,0:T(8,128)S(1)} %fusion.17), kind=kOutput, calls=%fused_computation.14 | convolution fusion | flops 806879232 | bytes 9961472 | tf_op jit(solution)/shard_map/dot_general | solution.py:113
  111.1 2.0 %reshape.91 = f32[512,2,4,128]{3,2,1,0:T(4,128)} reshape(f32[512,1024]{1,0:T(8,128)S(1)} %add_add_fusion.4) | data formatting | bytes 4194304 | tf_op jit(solution)/shard_map/reshape | solution.py:117
  113.1 4.0 %copy.14 = f32[512,4,2,128]{3,2,0,1:T(2,128)} copy(f32[512,4,2,128]{3,1,2,0:T(4,128)} %bitcast.162) | data formatting | bytes 4194304 | tf_op jit(solution)/shard_map/transpose | solution.py:118
  117.1 2.9 %reshape.92 = f32[512,4,256]{2,0,1:T(8,128)S(1)} reshape(f32[512,4,2,128]{3,2,0,1:T(2,128)} %copy.14) | data formatting | bytes 4194304 | tf_op jit(solution)/shard_map/reshape | solution.py:118
  120.0 0.7 fusion.4
  121.4 0.8 add_add_fusion.3
  122.3 1.4 %copy.15 = f32[512,4,256]{2,1,0:T(4,128)S(1)} copy(f32[512,4,256]{2,0,1:T(8,128)S(1)} %add_add_fusion.3) | data formatting | bytes 4194304 | tf_op jit(solution)/shard_map/add | solution.py:24
  123.6 2.1 %reshape_reshape.3 = f32[2,2,128,1024]{3,2,1,0:T(8,128)} reshape(f32[512,4,256]{2,1,0:T(4,128)S(1)} %copy.15) | data formatting | bytes 4194304 | tf_op jit(solution)/shard_map/reshape;reshape | solution.py:120
  125.7 1.7 %copy.16 = f32[2,2,128,1024]{3,2,1,0:T(8,128)S(1)} copy(f32[2,2,128,1024]{3,2,0,1:T(8,128)} %bitcast.163) | data formatting | bytes 4194304 | tf_op jit(solution)/shard_map/transpose | solution.py:121
  129.0 1.9 %add_add_fusion.2 = f32[2,1024,256]{1,2,0:T(8,128)} fusion(f32[2,1024,256]{1,2,0:T(8,128)S(1)} %fusion.94, f32[2,1024,256]{1,2,0:T(8,128)S(1)} %fusion.92, bf16[2,256,1024]{2,1,0:T(8,128)(2,1)S(1)} %get-tuple-element.33, s32[256]{0:T(256)S(1)} %get-tuple-element.52, s32[256]{0:T(256)S(1)} %get-tuple-element.55, s32[256]{0:T(256)S(1)} %get-tuple-element.53, ...), kind=kOutput, calls=%fused_computation.12 | convolution fusion | flops 269811712 | bytes 7344640 | tf_op jit(solution)/shard_map/dk,...kc->...dc/dot_general | solution.py:21
  (55 shorter events, 12.5 us)
Async XLA Ops:
  0.0 2.2 %copy-start.1 = (f32[4,8]{1,0:T(4,128)S(1)}, f32[4,8]{1,0:T(4,128)}, u32[]{:S(2)}) copy-start(f32[4,8]{1,0:T(4,128)} %param.5) | copy-start | bytes 388
  8.4 80.3 %all-to-all-start = ((f32[32,8,2688]{2,1,0:T(8,128)}), f32[32,8,2688]{2,1,0:T(8,128)S(1)}, u32[]{:S(2)}, u32[]{:S(2)}) async-start(f32[32,8,2688]{2,1,0:T(8,128)} %broadcast_dynamic-update-slice_fusion.4), calls=%async_computation | async-start | bytes 5505024 | tf_op jit(solution)/shard_map/all_to_all | solution.py:75
  93.0 10.4 %collective-permute-start = (f32[4,256,128]{2,1,0:T(8,128)S(1)}, f32[4,256,128]{2,1,0:T(8,128)S(1)}, u32[]{:S(2)}, u32[]{:S(2)}) collective-permute-start(f32[4,256,128]{2,1,0:T(8,128)S(1)} %pad_maximum_fusion), channel_id=1, source_target_pairs={{0,1},{1,0},{2,3},{3,2},{4,5},{5,4},{6,7},{7,6},{8,9},{9,8},{10,11... | collective-permute-start | bytes 1572872 | tf_op jit(solution)/shard_map/ppermute | solution.py:81
  98.0 1.2 copy-start

commit v8 on v6

--- a/solution.py
+++ b/solution.py
@@ -98,20 +98,19 @@
     cos_all = permute_exact(run_cos, hot)
     sin_all = permute_exact(run_sin, hot)
 
-    total = None
+    gram = jnp.einsum("afe,afd->aed", whitening, whitening, precision=high)
+    col_designs, row_designs = [], []
     for arc in range(arcs):
         col_values_all = arrived[:, arc * width : arc * width + col_pairs]
         row_values_all = row_all[arc]
-        col_design = jnp.concatenate(
+        col_designs.append(jnp.concatenate(
             [col_values_all * cos_all[arc, :, :col_pairs], col_values_all * sin_all[arc, :, :col_pairs]], axis=1
-        )
-        row_design = jnp.concatenate(
+        ))
+        row_designs.append(jnp.concatenate(
             [row_values_all * cos_all[arc, :, col_pairs:], row_values_all * sin_all[arc, :, col_pairs:]], axis=1
-        )
-        col_white = jnp.dot(whitening[arc], col_design, precision=high)
-        row_white = jnp.dot(whitening[arc], row_design, precision=high)
-        part = lax.dot_general(row_white, col_white, (((0,), (0,)), ((), ())), precision=high)
-        total = part if total is None else total + part
+        ))
+    col_mixed = jnp.einsum("aed,adc->aec", gram, jnp.stack(col_designs), precision=high)
+    total = jnp.einsum("aer,aec->rc", jnp.stack(row_designs), col_mixed, precision=high)
     return permute_exact(permute_exact(total, col_perm(col_pairs)), row_perm(row_pairs), left=True)
 
 def solution(mesh):

time: 121 us -> 120 us (level)
  matrix products: 23.9 us -> 20.1 us
  other arithmetic: 4.42 us -> 6.45 us
  local copies, waits for them, and re-layouts: 10.9 us -> 12.5 us
    dot_general x12 -> x3, matrix products: 11.4 us -> 7.31 us  [the longest x1 3.83 us: shards(): jnp.einsum('aer,aec->rc', jnp.stack(row_designs), col_mixed, precision=high)]
    mul x1, other arithmetic: 0.66 us -> 2.2 us  [shards(): col_values_all * cos_all[arc, :, :col_pairs]]
  transfers between devices with their start and end apart: 2 -> 2, of which waited for: 1 -> 1; matrix products, arithmetic and copies ran while one was open for 8% -> 9% of each run, Pallas kernels for 0% -> 0%
where the time goes in v8:
time: 120 us; the launch traced here: 119 us
  waiting for transfers between devices  62.2 us (52%)
  matrix products  20.1 us (17%)
  starting transfers between devices  17.3 us (14%)
  local copies, waits for them, and re-layouts  12.5 us (10%)
  other arithmetic  6.45 us (5%)
    all_to_all x1, waiting for transfers between devices, shards(): lax.all_to_all(payload, 'obs', 0, 0, tiled=True)  62.2 us
    all_to_all x1, starting transfers between devices, shards(): lax.all_to_all(payload, 'obs', 0, 0, tiled=True)  13.6 us
    dot_general x9, matrix products, permute_exact(): term = jnp.dot(piece, perm, preferred_element_type=jnp.float32)  9.09 us
    unnamed x13, local copies, waits for them, and re-layouts  6.43 us
    dot_general x1, matrix products, shards(): jnp.einsum('aer,aec->rc', jnp.stack(row_designs), col_mixed, precision=high)  3.83 us
    ppermute x1, starting transfers between devices, shards(): theirs = lax.ppermute(mine, 'gc', swap)  3.78 us
    dot_general x3, matrix products, permute_exact(): term = jnp.dot(perm, piece, preferred_element_type=jnp.float32)  3.66 us
    dot_general x1, matrix products, shards(): jnp.einsum('aed,adc->aec', gram, jnp.stack(col_designs), precision=high)  2.42 us
  transfers between devices with their start and end apart: 2, of which 1 were waited for; matrix products, arithmetic and copies ran while one was open for 9% of the time, Pallas kernels for 0%

profile of v8, /device:TPU:1, one launch (start us, length us, event | category | flops | bytes accessed | tf_op | source)
XLA Modules:
  0.0 119.0 jit_solution(5871269533427003570)
XLA Ops:
  0.0 1.4 %fusion.70 = (f32[1,8,8192]{2,1,0:T(8,128)S(1)}, f32[1,8,8192]{2,1,0:T(8,128)S(1)}, f32[1,8,8192]{2,1,0:T(8,128)S(1)}, f32[1,8,8192]{2,1,0:T(8,128)S(1)}) fusion(f32[4,8,8192]{2,1,0:T(8,128)} %param.4), kind=kLoop, calls=%fused_computation.150 | loop fusion | bytes 2097152 | tf_op jit(solution)/shard_map/slice | solution.py:67
  1.4 0.9 broadcast_dynamic-update-slice_fusion.3
  2.4 0.7 bitcast_dynamic-update-slice_fusion.3
  3.1 0.9 broadcast_dynamic-update-slice_fusion.2
  4.0 0.7 bitcast_dynamic-update-slice_fusion.2
  4.7 0.9 broadcast_dynamic-update-slice_fusion.1
  5.5 0.7 bitcast_dynamic-update-slice_fusion.1
  6.2 0.9 broadcast_dynamic-update-slice_fusion
  7.1 0.7 bitcast_dynamic-update-slice_fusion
  7.8 0.7 broadcast_dynamic-update-slice_fusion.4
  8.5 13.6 %all-to-all-start = ((f32[32,8,2688]{2,1,0:T(8,128)}), f32[32,8,2688]{2,1,0:T(8,128)}, u32[]{:S(2)}, u32[]{:S(2)}) async-start(f32[32,8,2688]{2,1,0:T(8,128)} %broadcast_dynamic-update-slice_fusion.4), calls=%async_computation | async-start | bytes 5505024 | tf_op jit(solution)/shard_map/all_to_all | solution.py:75
  22.1 0.8 dynamic_slice.39
  23.8 0.8 dynamic_slice.40
  25.6 1.1 fusion.71
  26.7 62.2 %all-to-all-done = f32[32,8,2688]{2,1,0:T(8,128)} async-done(((f32[32,8,2688]{2,1,0:T(8,128)}), f32[32,8,2688]{2,1,0:T(8,128)}, u32[]{:S(2)}, u32[]{:S(2)}) %all-to-all-start) | async-done | bytes 2752544 | tf_op jit(solution)/shard_map/all_to_all | solution.py:75
  88.9 1.1 slice_bitcast_fusion.12
  90.1 0.9 slice_bitcast_fusion.8
  91.1 1.9 %multiply_sine_fusion = (f32[4,256,128]{2,1,0:T(8,128)S(1)}, f32[4,256,128]{2,1,0:T(8,128)S(1)}) fusion(f32[128]{0:T(128)S(1)} %pad_maximum_fusion.1, f32[4,256]{1,0:T(4,128)S(1)} %copy.9), kind=kLoop, calls=%fused_computation.49 | loop fusion | flops 131072 | bytes 1053184 | tf_op jit(solution)/shard_map/sin | solution.py:97
  93.5 0.6 fusion.40
  94.1 0.6 fusion.38
  95.2 3.8 %collective-permute-start = (f32[4,256,128]{2,1,0:T(8,128)S(1)}, f32[4,256,128]{2,1,0:T(8,128)S(1)}, u32[]{:S(2)}, u32[]{:S(2)}) collective-permute-start(f32[4,256,128]{2,1,0:T(8,128)S(1)} %pad_maximum_fusion), channel_id=1, source_target_pairs={{0,1},{1,0},{2,3},{3,2},{4,5},{5,4},{6,7},{7,6},{8,9},{9,8},{10,11... | collective-permute-start | bytes 1572872 | tf_op jit(solution)/shard_map/ppermute | solution.py:81
  99.0 0.6 add_add_fusion
  99.6 0.7 add_add_fusion.1
  100.3 2.2 %fusion.33 = (f32[256,512]{1,0:T(8,128)S(1)}, f32[256,512]{1,0:T(8,128)S(1)}, f32[256,512]{1,0:T(8,128)S(1)}, f32[256,512]{1,0:T(8,128)S(1)}, f32[256,512]{1,0:T...) fusion(f32[4,256,768]{2,1,0:T(8,128)S(1)} %add_add_fusion.1, ...), kind=kLoop, calls=%fused_computation.68 | loop fusion | flops 1048576 | bytes 10485760 | tf_op jit(solution)/shard_map/mul | solution.py:107
  102.8 2.4 %fusion = f32[4,256,1024]{2,1,0:T(8,128)S(1)} fusion(f32[4,256,256]{2,1,0:T(8,128)S(1)} %fusion.71, f32[1,256,1024]{2,1,0:T(8,128)S(1)} %maximum_bitcast_fusion.3, f32[1,256,1024]{2,1,0:T(8,128)S(1)} %maximum_bitcast_fusion.2, f32[1,256,1024]{2,1,0:T(8,128)S(1)} %maximum_bitcast_fusion.1, f32[1,256,1024]{2,1,0:T(8,128)S(1)} %maximum_bitcast_fusion), kind=kOutput, calls=%fused_computation | convolution fusion | flops 1613758464 | bytes 9437184 | tf_op jit(solution)/shard_map/aed,adc->aec/dot_general | solution.py:112
  105.8 3.8 %fusion.10 = f32[512,1024,1]{1,0,2:T(8,128)S(1)} fusion(f32[4,256,1024]{2,1,0:T(8,128)S(1)} %fusion, f32[1,256,512]{2,1,0:T(8,128)S(1)} %maximum_bitcast_fusion.7, f32[1,256,512]{2,1,0:T(8,128)S(1)} %maximum_bitcast_fusion.6, f32[1,256,512]{2,1,0:T(8,128)S(1)} %maximum_bitcast_fusion.5, f32[1,256,512]{2,1,0:T(8,128)S(1)} %maximum_bitcast_fusion.4), kind=kOutput, calls=%fused_computation.21 | convolution fusion | flops 3222798336 | bytes 8388608 | tf_op jit(solution)/shard_map/aer,aec->rc/dot_general | solution.py:113
  109.6 1.8 %fusion.21 = f32[512,1024]{1,0:T(8,128)S(1)} fusion(f32[512,1024,1]{1,0,2:T(8,128)S(1)} %fusion.10, s32[1024]{0:T(1024)S(1)} %get-tuple-element.49, s32[1024]{0:T(1024)S(1)} %get-tuple-element.52, s32[1024]{0:T(1024)S(1)} %get-tuple-element.50, s32[1024]{0:T(1024)S(1)} %get-tuple-element.51, pred[1024]{0:T(1024)(128)(4,1)S(1)} %get-tuple-element.53, ...), kind=kOutput, calls=%fused_computation.32 | convolution fusion | flops 1081081856 | bytes 4212736 | tf_op jit(solution)/shard_map/dot_general | solution.py:23
  111.4 1.8 %fusion.20 = f32[512,1024]{1,0:T(8,128)S(1)} fusion(f32[512,1024,1]{1,0,2:T(8,128)S(1)} %fusion.10, s32[1024]{0:T(1024)S(1)} %get-tuple-element.49, s32[1024]{0:T(1024)S(1)} %get-tuple-element.52, s32[1024]{0:T(1024)S(1)} %get-tuple-element.50, s32[1024]{0:T(1024)S(1)} %get-tuple-element.51, pred[1024]{0:T(1024)(128)(4,1)S(1)} %get-tuple-element.53, ...), kind=kOutput, calls=%fused_computation.31 | convolution fusion | flops 1080033280 | bytes 4212736 | tf_op jit(solution)/shard_map/dot_general | solution.py:23
  113.3 2.0 %add_add_fusion.3 = f32[512,1024]{1,0:T(8,128)S(1)} fusion(f32[512,1024]{1,0:T(8,128)S(1)} %fusion.20, f32[512,1024]{1,0:T(8,128)S(1)} %fusion.21, f32[512,1024,1]{1,0,2:T(8,128)S(1)} %fusion.10, s32[1024]{0:T(1024)S(1)} %get-tuple-element.49, s32[1024]{0:T(1024)S(1)} %get-tuple-element.52, s32[1024]{0:T(1024)S(1)} %get-tuple-element.50, ...), kind=kOutput, calls=%fused_computation.30 | convolution fusion | flops 1082654720 | bytes 8407040 | tf_op jit(solution)/shard_map/dot_general | solution.py:23
  115.3 0.7 fusion.23
  116.0 0.7 fusion.22
  116.7 2.2 %add_add_fusion.2 = f32[512,1024]{1,0:T(8,128)} fusion(f32[512,1024]{1,0:T(8,128)S(1)} %fusion.22, f32[512,1024]{1,0:T(8,128)S(1)} %fusion.23, f32[512,1024]{1,0:T(8,128)S(1)} %add_add_fusion.3, s32[512]{0:T(512)S(1)} %get-tuple-element.55, s32[512]{0:T(512)S(1)} %get-tuple-element.58, s32[512]{0:T(512)S(1)} %get-tuple-element.56, ...), kind=kOutput, calls=%fused_computation.29 | convolution fusion | flops 541851648 | bytes 8397824 | tf_op jit(solution)/shard_map/dot_general | solution.py:21
  (50 shorter events, 4.0 us)
Async XLA Ops:
  0.0 25.6 %copy-start = (f32[4,256,256]{2,1,0:T(8,128)S(1)}, f32[4,256,256]{2,1,0:T(8,128)}, u32[]{:S(2)}) copy-start(f32[4,256,256]{2,1,0:T(8,128)} %param.7) | copy-start | bytes 3145732
  0.0 2.3 %copy-start.1 = (f32[4,8]{1,0:T(4,128)S(1)}, f32[4,8]{1,0:T(4,128)}, u32[]{:S(2)}) copy-start(f32[4,8]{1,0:T(4,128)} %param.5) | copy-start | bytes 388
  8.5 80.4 %all-to-all-start = ((f32[32,8,2688]{2,1,0:T(8,128)}), f32[32,8,2688]{2,1,0:T(8,128)}, u32[]{:S(2)}, u32[]{:S(2)}) async-start(f32[32,8,2688]{2,1,0:T(8,128)} %broadcast_dynamic-update-slice_fusion.4), calls=%async_computation | async-start | bytes 5505024 | tf_op jit(solution)/shard_map/all_to_all | solution.py:75
  95.2 10.0 %collective-permute-start = (f32[4,256,128]{2,1,0:T(8,128)S(1)}, f32[4,256,128]{2,1,0:T(8,128)S(1)}, u32[]{:S(2)}, u32[]{:S(2)}) collective-permute-start(f32[4,256,128]{2,1,0:T(8,128)S(1)} %pad_maximum_fusion), channel_id=1, source_target_pairs={{0,1},{1,0},{2,3},{3,2},{4,5},{5,4},{6,7},{7,6},{8,9},{9,8},{10,11... | collective-permute-start | bytes 1572872 | tf_op jit(solution)/shard_map/ppermute | solution.py:81

commit v9 on v8

--- a/solution.py
+++ b/solution.py
@@ -1,6 +1,8 @@
 import jax
 import jax.numpy as jnp
 from jax import lax
+from jax.experimental import pallas as pl
+from jax.experimental.pallas import tpu as pltpu
 from jax.sharding import PartitionSpec as P
 
 high = lax.Precision.HIGH
@@ -37,6 +39,45 @@
     return (dst == 2 * (src % half) + src // half).astype(jnp.bfloat16)
 
 
+GROUPS = 4
+
+
+def build_payload(offsets, legendre, lon_tile, peers, col_pairs, half_rows):
+    arcs, epochs_local, pairs_total = legendre.shape
+    width = col_pairs + half_rows
+    per_step = peers // GROUPS
+    row_pairs = pairs_total // peers
+
+    def kernel(off_ref, leg_ref, lon_ref, out_ref):
+        step = pl.program_id(0)
+        col_off = pl.multiple_of(off_ref[0], LANES)
+        row_sub = off_ref[1]
+        cols = [leg_ref[a, :, pl.ds(col_off, col_pairs)] for a in range(arcs)]
+        lon = lon_ref[...]
+
+        def one_peer(j, carry):
+            base = pl.multiple_of((step * per_step + j) * row_pairs + row_sub, LANES)
+            for a in range(arcs):
+                out_ref[j, :, a * width : a * width + col_pairs] = cols[a]
+                out_ref[j, :, a * width + col_pairs : (a + 1) * width] = leg_ref[a, :, pl.ds(base, half_rows)]
+            out_ref[j, :, arcs * width :] = lon
+            return carry
+
+        lax.fori_loop(0, per_step, one_peer, 0)
+
+    return pl.pallas_call(
+        kernel,
+        out_shape=jax.ShapeDtypeStruct((peers, epochs_local, arcs * width + LANES), legendre.dtype),
+        grid=(GROUPS,),
+        in_specs=[
+            pl.BlockSpec(memory_space=pltpu.SMEM),
+            pl.BlockSpec((arcs, epochs_local, pairs_total), lambda i: (0, 0, 0)),
+            pl.BlockSpec((epochs_local, LANES), lambda i: (0, 0)),
+        ],
+        out_specs=pl.BlockSpec((per_step, epochs_local, arcs * width + LANES), lambda i: (i, 0, 0)),
+    )(offsets, legendre, lon_tile)
+
+
 SLOTS = 64
 
 
@@ -62,16 +103,9 @@
     core = grid_position % 2
     half_rows = row_pairs // 2
     width = col_pairs + half_rows
-    pieces = []
-    for arc in range(arcs):
-        col_values = lax.dynamic_slice_in_dim(legendre[arc], grid_position * col_pairs, col_pairs, 1)
-        pieces.append(jnp.broadcast_to(col_values[None], (obs_count, epochs_local, col_pairs)))
-        row_values = legendre[arc].reshape(epochs_local, obs_count, 2, half_rows)
-        row_values = lax.dynamic_index_in_dim(row_values, core, 2, keepdims=False)
-        pieces.append(jnp.transpose(row_values, (1, 0, 2)))
     lon_tile = jnp.pad(longitude.T, ((0, 0), (0, LANES - arcs)))
-    pieces.append(jnp.broadcast_to(lon_tile[None], (obs_count, epochs_local, LANES)))
-    payload = jnp.concatenate(pieces, axis=2)
+    offsets = jnp.stack([grid_position * col_pairs, core * half_rows]).astype(jnp.int32)
+    payload = build_payload(offsets, legendre, lon_tile, obs_count, col_pairs, half_rows)
     arrived = lax.all_to_all(payload, "obs", 0, 0, tiled=True).reshape(epochs, arcs * width + LANES)
     lon_all = arrived[:, arcs * width : arcs * width + arcs]
 

time: 120 us -> 117 us (0.975)
  local copies, waits for them, and re-layouts: 12.5 us -> 5.49 us
  Pallas kernels: 0 us -> 3.35 us
    unnamed x13 -> x3, local copies, waits for them, and re-layouts: 6.43 us -> 0.85 us
    pallas_call x0 -> x1, Pallas kernels: none -> 3.35 us  [build_payload(): pl.pallas_call(kernel, out_shape=jax.ShapeDtypeStruct((peers, epochs_loca...]
    slice x2 -> x1, local copies, waits for them, and re-layouts: 1.44 us -> 0.07 us  [the longest x1 1.36 us: shards(): legendre[arc]]
where the time goes in v9:
time: 117 us; the launch traced here: 116 us
  waiting for transfers between devices  62.2 us (53%)
  matrix products  20.1 us (17%)
  starting transfers between devices  17.3 us (15%)
  other arithmetic  7.13 us (6%)
  local copies, waits for them, and re-layouts  5.49 us (5%)
  Pallas kernels  3.35 us (3%)
    all_to_all x1, waiting for transfers between devices, shards(): lax.all_to_all(payload, 'obs', 0, 0, tiled=True)  62.2 us
    all_to_all x1, starting transfers between devices, shards(): lax.all_to_all(payload, 'obs', 0, 0, tiled=True)  13.6 us
    dot_general x9, matrix products, permute_exact(): term = jnp.dot(piece, perm, preferred_element_type=jnp.float32)  9.11 us
    dot_general x1, matrix products, shards(): jnp.einsum('aer,aec->rc', jnp.stack(row_designs), col_mixed, precision=high)  3.83 us
    ppermute x1, starting transfers between devices, shards(): theirs = lax.ppermute(mine, 'gc', swap)  3.78 us
    dot_general x3, matrix products, permute_exact(): term = jnp.dot(perm, piece, preferred_element_type=jnp.float32)  3.66 us
    pallas_call x1, Pallas kernels, build_payload(): pl.pallas_call(kernel, out_shape=jax.ShapeDtypeStruct((peers, epochs_loca...  3.35 us
    dot_general x1, matrix products, shards(): jnp.einsum('aed,adc->aec', gram, jnp.stack(col_designs), precision=high)  2.42 us
  transfers between devices with their start and end apart: 2, of which 1 were waited for; matrix products, arithmetic and copies ran while one was open for 9% of the time, Pallas kernels for 0%

profile of v9, /device:TPU:1, one launch (start us, length us, event | category | flops | bytes accessed | tf_op | source)
XLA Modules:
  0.0 115.9 jit_solution(346724190757528773)
XLA Ops:
  0.0 0.8 copy.8
  0.8 0.7 pad_add_fusion.1.off_ref
  1.5 0.6 pad.8.lon_ref
  2.1 3.3 %shard_map.46 = f32[32,8,2688]{2,1,0:T(8,128)} custom-call(s32[2]{0:T(128)} %pad_add_fusion.1.off_ref, f32[4,8,8192]{2,1,0:T(8,128)} %leg_ref.1, f32[8,128]{1,0:T(8,128)} %pad.8.lon_ref), custom_call_target="tpu_custom_call" | custom-call | tf_op jit(solution)/shard_map/pallas_call | solution.py:68
  5.4 13.6 %all-to-all-start = ((f32[32,8,2688]{2,1,0:T(8,128)}), f32[32,8,2688]{2,1,0:T(8,128)}, u32[]{:S(2)}, u32[]{:S(2)}) async-start(f32[32,8,2688]{2,1,0:T(8,128)} %shard_map.46), calls=%async_computation | async-start | bytes 5505024 | tf_op jit(solution)/shard_map/all_to_all | solution.py:109
  19.0 0.8 dynamic_slice.6
  20.0 0.3 reduce-window.16
  20.7 0.8 dynamic_slice.7
  21.6 0.3 reduce-window.24
  22.6 1.1 fusion.70
  23.6 62.2 %all-to-all-done = f32[32,8,2688]{2,1,0:T(8,128)} async-done(((f32[32,8,2688]{2,1,0:T(8,128)}), f32[32,8,2688]{2,1,0:T(8,128)}, u32[]{:S(2)}, u32[]{:S(2)}) %all-to-all-start) | async-done | bytes 2752544 | tf_op jit(solution)/shard_map/all_to_all | solution.py:109
  85.9 1.1 slice_bitcast_fusion.12
  87.0 0.9 slice_bitcast_fusion.8
  88.0 1.9 %multiply_sine_fusion = (f32[4,256,128]{2,1,0:T(8,128)S(1)}, f32[4,256,128]{2,1,0:T(8,128)S(1)}) fusion(f32[128]{0:T(128)S(1)} %pad_maximum_fusion.1, f32[4,256]{1,0:T(4,128)S(1)} %copy.9), kind=kLoop, calls=%fused_computation.49 | loop fusion | flops 131072 | bytes 1053184 | tf_op jit(solution)/shard_map/sin | solution.py:131
  89.9 0.5 fusion.39
  90.5 0.6 fusion.40
  91.0 0.6 fusion.38
  91.6 0.6 fusion.37
  92.2 3.8 %collective-permute-start = (f32[4,256,128]{2,1,0:T(8,128)S(1)}, f32[4,256,128]{2,1,0:T(8,128)S(1)}, u32[]{:S(2)}, u32[]{:S(2)}) collective-permute-start(f32[4,256,128]{2,1,0:T(8,128)S(1)} %pad_maximum_fusion), channel_id=1, source_target_pairs={{0,1},{1,0},{2,3},{3,2},{4,5},{5,4},{6,7},{7,6},{8,9},{9,8},{10,11... | collective-permute-start | bytes 1572872 | tf_op jit(solution)/shard_map/ppermute | solution.py:115
  96.0 0.6 add_add_fusion
  96.6 0.7 add_add_fusion.1
  97.2 2.2 %fusion.33 = (f32[256,512]{1,0:T(8,128)S(1)}, f32[256,512]{1,0:T(8,128)S(1)}, f32[256,512]{1,0:T(8,128)S(1)}, f32[256,512]{1,0:T(8,128)S(1)}, f32[256,512]{1,0:T...) fusion(f32[4,256,768]{2,1,0:T(8,128)S(1)} %add_add_fusion.1, ...), kind=kLoop, calls=%fused_computation.68 | loop fusion | flops 1048576 | bytes 10485760 | tf_op jit(solution)/shard_map/mul | solution.py:141
  99.5 0.1 maximum_bitcast_fusion
  99.7 2.4 %fusion = f32[4,256,1024]{2,1,0:T(8,128)S(1)} fusion(f32[4,256,256]{2,1,0:T(8,128)S(1)} %fusion.70, f32[1,256,1024]{2,1,0:T(8,128)S(1)} %get-tuple-element.42, f32[1,256,1024]{2,1,0:T(8,128)S(1)} %get-tuple-element.41, f32[1,256,1024]{2,1,0:T(8,128)S(1)} %get-tuple-element.40, f32[1,256,1024]{2,1,0:T(8,128)S(1)} %get-tuple-element.39), kind=kOutput, calls=%fused_computation | convolution fusion | flops 1613758464 | bytes 9437184 | tf_op jit(solution)/shard_map/aed,adc->aec/dot_general | solution.py:146
  102.3 0.2 fusion.48
  102.7 3.8 %fusion.10 = f32[512,1024,1]{1,0,2:T(8,128)S(1)} fusion(f32[4,256,1024]{2,1,0:T(8,128)S(1)} %fusion, f32[1,256,512]{2,1,0:T(8,128)S(1)} %get-tuple-element.46, f32[1,256,512]{2,1,0:T(8,128)S(1)} %get-tuple-element.45, f32[1,256,512]{2,1,0:T(8,128)S(1)} %get-tuple-element.44, f32[1,256,512]{2,1,0:T(8,128)S(1)} %get-tuple-element.43), kind=kOutput, calls=%fused_computation.21 | convolution fusion | flops 3222798336 | bytes 8388608 | tf_op jit(solution)/shard_map/aer,aec->rc/dot_general | solution.py:147
  106.6 1.8 %fusion.21 = f32[512,1024]{1,0:T(8,128)S(1)} fusion(f32[512,1024,1]{1,0,2:T(8,128)S(1)} %fusion.10, s32[1024]{0:T(1024)S(1)} %get-tuple-element.47, s32[1024]{0:T(1024)S(1)} %get-tuple-element.50, s32[1024]{0:T(1024)S(1)} %get-tuple-element.48, s32[1024]{0:T(1024)S(1)} %get-tuple-element.49, pred[1024]{0:T(1024)(128)(4,1)S(1)} %get-tuple-element.51, ...), kind=kOutput, calls=%fused_computation.32 | convolution fusion | flops 1081081856 | bytes 4212736 | tf_op jit(solution)/shard_map/dot_general | solution.py:25
  108.4 1.8 %fusion.20 = f32[512,1024]{1,0:T(8,128)S(1)} fusion(f32[512,1024,1]{1,0,2:T(8,128)S(1)} %fusion.10, s32[1024]{0:T(1024)S(1)} %get-tuple-element.47, s32[1024]{0:T(1024)S(1)} %get-tuple-element.50, s32[1024]{0:T(1024)S(1)} %get-tuple-element.48, s32[1024]{0:T(1024)S(1)} %get-tuple-element.49, pred[1024]{0:T(1024)(128)(4,1)S(1)} %get-tuple-element.51, ...), kind=kOutput, calls=%fused_computation.31 | convolution fusion | flops 1080033280 | bytes 4212736 | tf_op jit(solution)/shard_map/dot_general | solution.py:25
  110.2 2.0 %add_add_fusion.3 = f32[512,1024]{1,0:T(8,128)S(1)} fusion(f32[512,1024]{1,0:T(8,128)S(1)} %fusion.20, f32[512,1024]{1,0:T(8,128)S(1)} %fusion.21, f32[512,1024,1]{1,0,2:T(8,128)S(1)} %fusion.10, s32[1024]{0:T(1024)S(1)} %get-tuple-element.47, s32[1024]{0:T(1024)S(1)} %get-tuple-element.50, s32[1024]{0:T(1024)S(1)} %get-tuple-element.48, ...), kind=kOutput, calls=%fused_computation.30 | convolution fusion | flops 1082654720 | bytes 8407040 | tf_op jit(solution)/shard_map/dot_general | solution.py:25
  112.2 0.7 fusion.23
  113.0 0.7 fusion.22
  113.7 2.2 %add_add_fusion.2 = f32[512,1024]{1,0:T(8,128)} fusion(f32[512,1024]{1,0:T(8,128)S(1)} %fusion.22, f32[512,1024]{1,0:T(8,128)S(1)} %fusion.23, f32[512,1024]{1,0:T(8,128)S(1)} %add_add_fusion.3, s32[512]{0:T(512)S(1)} %get-tuple-element.53, s32[512]{0:T(512)S(1)} %get-tuple-element.56, s32[512]{0:T(512)S(1)} %get-tuple-element.54, ...), kind=kOutput, calls=%fused_computation.29 | convolution fusion | flops 541851648 | bytes 8397824 | tf_op jit(solution)/shard_map/dot_general | solution.py:23
  (34 shorter events, 1.9 us)
Async XLA Ops:
  0.0 22.6 %copy-start = (f32[4,256,256]{2,1,0:T(8,128)S(1)}, f32[4,256,256]{2,1,0:T(8,128)}, u32[]{:S(2)}) copy-start(f32[4,256,256]{2,1,0:T(8,128)} %param.7) | copy-start | bytes 3145732
  5.4 80.4 %all-to-all-start = ((f32[32,8,2688]{2,1,0:T(8,128)}), f32[32,8,2688]{2,1,0:T(8,128)}, u32[]{:S(2)}, u32[]{:S(2)}) async-start(f32[32,8,2688]{2,1,0:T(8,128)} %shard_map.46), calls=%async_computation | async-start | bytes 5505024 | tf_op jit(solution)/shard_map/all_to_all | solution.py:109
  92.2 10.0 %collective-permute-start = (f32[4,256,128]{2,1,0:T(8,128)S(1)}, f32[4,256,128]{2,1,0:T(8,128)S(1)}, u32[]{:S(2)}, u32[]{:S(2)}) collective-permute-start(f32[4,256,128]{2,1,0:T(8,128)S(1)} %pad_maximum_fusion), channel_id=1, source_target_pairs={{0,1},{1,0},{2,3},{3,2},{4,5},{5,4},{6,7},{7,6},{8,9},{9,8},{10,11... | collective-permute-start | bytes 1572872 | tf_op jit(solution)/shard_map/ppermute | solution.py:115

commit v10 on v9

--- a/solution.py
+++ b/solution.py
@@ -42,16 +42,17 @@
 GROUPS = 4
 
 
-def build_payload(offsets, legendre, lon_tile, peers, col_pairs, half_rows):
+def build_payload(legendre, longitude, peers, col_pairs, half_rows):
     arcs, epochs_local, pairs_total = legendre.shape
     width = col_pairs + half_rows
     per_step = peers // GROUPS
     row_pairs = pairs_total // peers
 
-    def kernel(off_ref, leg_ref, lon_ref, out_ref):
+    def kernel(leg_ref, lon_ref, out_ref):
         step = pl.program_id(0)
-        col_off = pl.multiple_of(off_ref[0], LANES)
-        row_sub = off_ref[1]
+        grid_position = lax.axis_index("gr") * lax.axis_size("gc") + lax.axis_index("gc")
+        col_off = pl.multiple_of(grid_position * col_pairs, LANES)
+        row_sub = (grid_position % 2) * half_rows
         cols = [leg_ref[a, :, pl.ds(col_off, col_pairs)] for a in range(arcs)]
         lon = lon_ref[...]
 
@@ -60,7 +61,8 @@
             for a in range(arcs):
                 out_ref[j, :, a * width : a * width + col_pairs] = cols[a]
                 out_ref[j, :, a * width + col_pairs : (a + 1) * width] = leg_ref[a, :, pl.ds(base, half_rows)]
-            out_ref[j, :, arcs * width :] = lon
+            out_ref[j, :, arcs * width :] = jnp.zeros((epochs_local, LANES), out_ref.dtype)
+            out_ref[j, :arcs, arcs * width : arcs * width + epochs_local] = lon
             return carry
 
         lax.fori_loop(0, per_step, one_peer, 0)
@@ -70,12 +72,11 @@
         out_shape=jax.ShapeDtypeStruct((peers, epochs_local, arcs * width + LANES), legendre.dtype),
         grid=(GROUPS,),
         in_specs=[
-            pl.BlockSpec(memory_space=pltpu.SMEM),
             pl.BlockSpec((arcs, epochs_local, pairs_total), lambda i: (0, 0, 0)),
-            pl.BlockSpec((epochs_local, LANES), lambda i: (0, 0)),
+            pl.BlockSpec((arcs, epochs_local), lambda i: (0, 0)),
         ],
         out_specs=pl.BlockSpec((per_step, epochs_local, arcs * width + LANES), lambda i: (i, 0, 0)),
-    )(offsets, legendre, lon_tile)
+    )(legendre, longitude)
 
 
 SLOTS = 64
@@ -103,11 +104,11 @@
     core = grid_position % 2
     half_rows = row_pairs // 2
     width = col_pairs + half_rows
-    lon_tile = jnp.pad(longitude.T, ((0, 0), (0, LANES - arcs)))
-    offsets = jnp.stack([grid_position * col_pairs, core * half_rows]).astype(jnp.int32)
-    payload = build_payload(offsets, legendre, lon_tile, obs_count, col_pairs, half_rows)
-    arrived = lax.all_to_all(payload, "obs", 0, 0, tiled=True).reshape(epochs, arcs * width + LANES)
-    lon_all = arrived[:, arcs * width : arcs * width + arcs]
+    payload = build_payload(legendre, longitude, obs_count, col_pairs, half_rows)
+    arrived = lax.all_to_all(payload, "obs", 0, 0, tiled=True)
+    lon_all = jnp.transpose(arrived[:, :arcs, arcs * width : arcs * width + epochs_local], (1, 0, 2))
+    lon_all = lon_all.reshape(arcs, epochs)
+    arrived = arrived.reshape(epochs, arcs * width + LANES)
 
     mine = jnp.stack([arrived[:, arc * width + col_pairs : (arc + 1) * width] for arc in range(arcs)])
     gc_count = lax.axis_size("gc")
@@ -127,7 +128,7 @@
         axis=0,
     )
     run_values = jnp.concatenate([col_value, row_value])
-    run_angles = lon_all.T[:, :, None] * run_values
+    run_angles = lon_all[:, :, None] * run_values
     run_cos, run_sin = lax.optimization_barrier((jnp.cos(run_angles), jnp.sin(run_angles)))
     cos_all = permute_exact(run_cos, hot)
     sin_all = permute_exact(run_sin, hot)

time: 117 us -> 115 us (0.983)
  local copies, waits for them, and re-layouts: 5.49 us -> 4.08 us
where the time goes in v10:
time: 115 us; the launch traced here: 114 us
  waiting for transfers between devices  62.2 us (54%)
  matrix products  20.1 us (17%)
  starting transfers between devices  17.4 us (15%)
  other arithmetic  6.51 us (6%)
  local copies, waits for them, and re-layouts  4.08 us (4%)
  Pallas kernels  3.37 us (3%)
    all_to_all x1, waiting for transfers between devices, shards(): arrived = lax.all_to_all(payload, 'obs', 0, 0, tiled=True)  62.2 us
    all_to_all x1, starting transfers between devices, shards(): arrived = lax.all_to_all(payload, 'obs', 0, 0, tiled=True)  13.6 us
    dot_general x9, matrix products, permute_exact(): term = jnp.dot(piece, perm, preferred_element_type=jnp.float32)  9.2 us
    dot_general x1, matrix products, shards(): jnp.einsum('aer,aec->rc', jnp.stack(row_designs), col_mixed, precision=high)  3.81 us
    ppermute x1, starting transfers between devices, shards(): theirs = lax.ppermute(mine, 'gc', swap)  3.79 us
    dot_general x3, matrix products, permute_exact(): term = jnp.dot(perm, piece, preferred_element_type=jnp.float32)  3.66 us
    pallas_call x1, Pallas kernels, build_payload(): pl.pallas_call(kernel, out_shape=jax.ShapeDtypeStruct((peers, epochs_loca...  3.37 us
    dot_general x1, matrix products, shards(): jnp.einsum('aed,adc->aec', gram, jnp.stack(col_designs), precision=high)  2.41 us
  transfers between devices with their start and end apart: 2, of which 1 were waited for; matrix products, arithmetic and copies ran while one was open for 9% of the time, Pallas kernels for 0%

profile of v10, /device:TPU:1, one launch (start us, length us, event | category | flops | bytes accessed | tf_op | source)
XLA Modules:
  0.0 114.0 jit_solution(13804121399859755638)
XLA Ops:
  0.0 3.4 %shard_map.46 = f32[32,8,2688]{2,1,0:T(8,128)} custom-call(f32[4,8,8192]{2,1,0:T(8,128)} %leg_ref.1, f32[4,8]{1,0:T(4,128)} %lon_ref.1), custom_call_target="tpu_custom_call" | custom-call | tf_op jit(solution)/shard_map/pallas_call | solution.py:70
  3.4 13.6 %all-to-all-start = ((f32[32,8,2688]{2,1,0:T(8,128)}), f32[32,8,2688]{2,1,0:T(8,128)}, u32[]{:S(2)}, u32[]{:S(2)}) async-start(f32[32,8,2688]{2,1,0:T(8,128)} %shard_map.46), calls=%async_computation | async-start | bytes 5505024 | tf_op jit(solution)/shard_map/all_to_all | solution.py:108
  17.0 0.8 dynamic_slice.6
  17.9 0.3 reduce-window.16
  18.5 0.1 select_reduce_fusion
  18.6 0.8 dynamic_slice.7
  19.6 0.3 reduce-window.24
  20.5 1.1 fusion.70
  21.6 62.2 %all-to-all-done = f32[32,8,2688]{2,1,0:T(8,128)} async-done(((f32[32,8,2688]{2,1,0:T(8,128)}), f32[32,8,2688]{2,1,0:T(8,128)}, u32[]{:S(2)}, u32[]{:S(2)}) %all-to-all-start) | async-done | bytes 2752544 | tf_op jit(solution)/shard_map/all_to_all | solution.py:108
  83.8 0.9 slice_bitcast_fusion.12
  84.8 1.9 %multiply_sine_fusion = (f32[4,256,128]{2,1,0:T(8,128)S(1)}, f32[4,256,128]{2,1,0:T(8,128)S(1)}) fusion(f32[128]{0:T(128)S(1)} %pad_maximum_fusion.1, f32[4,256]{1,0:T(4,128)S(1)} %mul.119), kind=kLoop, calls=%fused_computation.49 | loop fusion | flops 131072 | bytes 1053184 | tf_op jit(solution)/shard_map/sin | solution.py:132
  86.7 0.5 fusion.39
  87.3 0.6 fusion.40
  87.8 0.6 fusion.38
  88.4 0.6 fusion.37
  88.9 1.1 slice_bitcast_fusion.11
  90.1 3.8 %collective-permute-start = (f32[4,256,128]{2,1,0:T(8,128)S(1)}, f32[4,256,128]{2,1,0:T(8,128)S(1)}, u32[]{:S(2)}, u32[]{:S(2)}) collective-permute-start(f32[4,256,128]{2,1,0:T(8,128)S(1)} %pad_maximum_fusion), channel_id=1, source_target_pairs={{0,1},{1,0},{2,3},{3,2},{4,5},{5,4},{6,7},{7,6},{8,9},{9,8},{10,11... | collective-permute-start | bytes 1572872 | tf_op jit(solution)/shard_map/ppermute | solution.py:116
  93.9 0.6 add_add_fusion
  94.5 0.7 add_add_fusion.1
  95.2 2.2 %fusion.33 = (f32[256,512]{1,0:T(8,128)S(1)}, f32[256,512]{1,0:T(8,128)S(1)}, f32[256,512]{1,0:T(8,128)S(1)}, f32[256,512]{1,0:T(8,128)S(1)}, f32[256,512]{1,0:T...) fusion(f32[4,256,768]{2,1,0:T(8,128)S(1)} %add_add_fusion.1, ...), kind=kLoop, calls=%fused_computation.68 | loop fusion | flops 1048576 | bytes 10485760 | tf_op jit(solution)/shard_map/mul | solution.py:142
  97.4 0.1 maximum_bitcast_fusion
  97.6 0.2 maximum_bitcast_fusion.2
  97.7 2.4 %fusion = f32[4,256,1024]{2,1,0:T(8,128)S(1)} fusion(f32[4,256,256]{2,1,0:T(8,128)S(1)} %fusion.70, f32[1,256,1024]{2,1,0:T(8,128)S(1)} %get-tuple-element.42, f32[1,256,1024]{2,1,0:T(8,128)S(1)} %get-tuple-element.41, f32[1,256,1024]{2,1,0:T(8,128)S(1)} %get-tuple-element.40, f32[1,256,1024]{2,1,0:T(8,128)S(1)} %get-tuple-element.39), kind=kOutput, calls=%fused_computation | convolution fusion | flops 1613758464 | bytes 9437184 | tf_op jit(solution)/shard_map/aed,adc->aec/dot_general | solution.py:147
  100.3 0.2 fusion.48
  100.6 0.1 maximum_bitcast_fusion.6
  100.7 3.8 %fusion.10 = f32[512,1024,1]{1,0,2:T(8,128)S(1)} fusion(f32[4,256,1024]{2,1,0:T(8,128)S(1)} %fusion, f32[1,256,512]{2,1,0:T(8,128)S(1)} %get-tuple-element.46, f32[1,256,512]{2,1,0:T(8,128)S(1)} %get-tuple-element.45, f32[1,256,512]{2,1,0:T(8,128)S(1)} %get-tuple-element.44, f32[1,256,512]{2,1,0:T(8,128)S(1)} %get-tuple-element.43), kind=kOutput, calls=%fused_computation.21 | convolution fusion | flops 3222798336 | bytes 8388608 | tf_op jit(solution)/shard_map/aer,aec->rc/dot_general | solution.py:148
  104.5 1.8 %fusion.21 = f32[512,1024]{1,0:T(8,128)S(1)} fusion(f32[512,1024,1]{1,0,2:T(8,128)S(1)} %fusion.10, s32[1024]{0:T(1024)S(1)} %get-tuple-element.47, s32[1024]{0:T(1024)S(1)} %get-tuple-element.50, s32[1024]{0:T(1024)S(1)} %get-tuple-element.48, s32[1024]{0:T(1024)S(1)} %get-tuple-element.49, pred[1024]{0:T(1024)(128)(4,1)S(1)} %get-tuple-element.51, ...), kind=kOutput, calls=%fused_computation.32 | convolution fusion | flops 1081081856 | bytes 4212736 | tf_op jit(solution)/shard_map/dot_general | solution.py:25
  106.3 1.8 %fusion.20 = f32[512,1024]{1,0:T(8,128)S(1)} fusion(f32[512,1024,1]{1,0,2:T(8,128)S(1)} %fusion.10, s32[1024]{0:T(1024)S(1)} %get-tuple-element.47, s32[1024]{0:T(1024)S(1)} %get-tuple-element.50, s32[1024]{0:T(1024)S(1)} %get-tuple-element.48, s32[1024]{0:T(1024)S(1)} %get-tuple-element.49, pred[1024]{0:T(1024)(128)(4,1)S(1)} %get-tuple-element.51, ...), kind=kOutput, calls=%fused_computation.31 | convolution fusion | flops 1080033280 | bytes 4212736 | tf_op jit(solution)/shard_map/dot_general | solution.py:25
  108.2 2.1 %add_add_fusion.3 = f32[512,1024]{1,0:T(8,128)S(1)} fusion(f32[512,1024]{1,0:T(8,128)S(1)} %fusion.20, f32[512,1024]{1,0:T(8,128)S(1)} %fusion.21, f32[512,1024,1]{1,0,2:T(8,128)S(1)} %fusion.10, s32[1024]{0:T(1024)S(1)} %get-tuple-element.47, s32[1024]{0:T(1024)S(1)} %get-tuple-element.50, s32[1024]{0:T(1024)S(1)} %get-tuple-element.48, ...), kind=kOutput, calls=%fused_computation.30 | convolution fusion | flops 1082654720 | bytes 8407040 | tf_op jit(solution)/shard_map/dot_general | solution.py:25
  110.3 0.7 fusion.23
  111.0 0.7 fusion.22
  111.8 2.2 %add_add_fusion.2 = f32[512,1024]{1,0:T(8,128)} fusion(f32[512,1024]{1,0:T(8,128)S(1)} %fusion.22, f32[512,1024]{1,0:T(8,128)S(1)} %fusion.23, f32[512,1024]{1,0:T(8,128)S(1)} %add_add_fusion.3, s32[512]{0:T(512)S(1)} %get-tuple-element.53, s32[512]{0:T(512)S(1)} %get-tuple-element.56, s32[512]{0:T(512)S(1)} %get-tuple-element.54, ...), kind=kOutput, calls=%fused_computation.29 | convolution fusion | flops 541851648 | bytes 8397824 | tf_op jit(solution)/shard_map/dot_general | solution.py:23
  (32 shorter events, 1.5 us)
Async XLA Ops:
  0.0 20.5 %copy-start = (f32[4,256,256]{2,1,0:T(8,128)S(1)}, f32[4,256,256]{2,1,0:T(8,128)}, u32[]{:S(2)}) copy-start(f32[4,256,256]{2,1,0:T(8,128)} %param.7) | copy-start | bytes 3145732
  3.4 80.4 %all-to-all-start = ((f32[32,8,2688]{2,1,0:T(8,128)}), f32[32,8,2688]{2,1,0:T(8,128)}, u32[]{:S(2)}, u32[]{:S(2)}) async-start(f32[32,8,2688]{2,1,0:T(8,128)} %shard_map.46), calls=%async_computation | async-start | bytes 5505024 | tf_op jit(solution)/shard_map/all_to_all | solution.py:108
  90.1 10.0 %collective-permute-start = (f32[4,256,128]{2,1,0:T(8,128)S(1)}, f32[4,256,128]{2,1,0:T(8,128)S(1)}, u32[]{:S(2)}, u32[]{:S(2)}) collective-permute-start(f32[4,256,128]{2,1,0:T(8,128)S(1)} %pad_maximum_fusion), channel_id=1, source_target_pairs={{0,1},{1,0},{2,3},{3,2},{4,5},{5,4},{6,7},{7,6},{8,9},{9,8},{10,11... | collective-permute-start | bytes 1572872 | tf_op jit(solution)/shard_map/ppermute | solution.py:116

commit v11 on v10

--- a/solution.py
+++ b/solution.py
@@ -146,7 +146,18 @@
         ))
     col_mixed = jnp.einsum("aed,adc->aec", gram, jnp.stack(col_designs), precision=high)
     total = jnp.einsum("aer,aec->rc", jnp.stack(row_designs), col_mixed, precision=high)
-    return permute_exact(permute_exact(total, col_perm(col_pairs)), row_perm(row_pairs), left=True)
+    span = 2 * LANES
+    by_cols = jnp.concatenate(
+        [
+            permute_exact(
+                jnp.concatenate([total[:, k : k + LANES], total[:, col_pairs + k : col_pairs + k + LANES]], axis=1),
+                col_perm(LANES),
+            )
+            for k in range(0, col_pairs, LANES)
+        ],
+        axis=1,
+    )
+    return permute_exact(by_cols, row_perm(row_pairs), left=True)
 
 def solution(mesh):
     placed = (P(None, "obs", None), P(None, "obs"), P(), P())

time: 115 us -> 116 us (level)
    dot_general x9 -> x18, matrix products: 9.2 us -> 9.96 us  [permute_exact(): term = jnp.dot(piece, perm, preferred_element_type=jnp.float32)]
where the time goes in v11:
time: 116 us; the launch traced here: 115 us
  waiting for transfers between devices  62.2 us (54%)
  matrix products  21 us (18%)
  starting transfers between devices  17.4 us (15%)
  other arithmetic  6.51 us (6%)
  local copies, waits for them, and re-layouts  4.24 us (4%)
  Pallas kernels  3.37 us (3%)
    all_to_all x1, waiting for transfers between devices, shards(): arrived = lax.all_to_all(payload, 'obs', 0, 0, tiled=True)  62.2 us
    all_to_all x1, starting transfers between devices, shards(): arrived = lax.all_to_all(payload, 'obs', 0, 0, tiled=True)  13.6 us
    dot_general x18, matrix products, permute_exact(): term = jnp.dot(piece, perm, preferred_element_type=jnp.float32)  9.96 us
    dot_general x1, matrix products, shards(): jnp.einsum('aer,aec->rc', jnp.stack(row_designs), col_mixed, precision=high)  3.84 us
    ppermute x1, starting transfers between devices, shards(): theirs = lax.ppermute(mine, 'gc', swap)  3.79 us
    dot_general x3, matrix products, permute_exact(): term = jnp.dot(perm, piece, preferred_element_type=jnp.float32)  3.72 us
    pallas_call x1, Pallas kernels, build_payload(): pl.pallas_call(kernel, out_shape=jax.ShapeDtypeStruct((peers, epochs_loca...  3.37 us
    dot_general x1, matrix products, shards(): jnp.einsum('aed,adc->aec', gram, jnp.stack(col_designs), precision=high)  2.41 us
  transfers between devices with their start and end apart: 2, of which 1 were waited for; matrix products, arithmetic and copies ran while one was open for 9% of the time, Pallas kernels for 0%

profile of v11, /device:TPU:1, one launch (start us, length us, event | category | flops | bytes accessed | tf_op | source)
XLA Modules:
  0.0 115.0 jit_solution(10863249563832812537)
XLA Ops:
  0.0 3.4 %shard_map.46 = f32[32,8,2688]{2,1,0:T(8,128)} custom-call(f32[4,8,8192]{2,1,0:T(8,128)} %leg_ref.1, f32[4,8]{1,0:T(4,128)} %lon_ref.1), custom_call_target="tpu_custom_call" | custom-call | tf_op jit(solution)/shard_map/pallas_call | solution.py:70
  3.4 13.6 %all-to-all-start = ((f32[32,8,2688]{2,1,0:T(8,128)}), f32[32,8,2688]{2,1,0:T(8,128)}, u32[]{:S(2)}, u32[]{:S(2)}) async-start(f32[32,8,2688]{2,1,0:T(8,128)} %shard_map.46), calls=%async_computation | async-start | bytes 5505024 | tf_op jit(solution)/shard_map/all_to_all | solution.py:108
  17.0 0.8 dynamic_slice.6
  18.6 0.8 dynamic_slice.7
  20.5 1.1 fusion.93
  21.6 62.2 %all-to-all-done = f32[32,8,2688]{2,1,0:T(8,128)} async-done(((f32[32,8,2688]{2,1,0:T(8,128)}), f32[32,8,2688]{2,1,0:T(8,128)}, u32[]{:S(2)}, u32[]{:S(2)}) %all-to-all-start) | async-done | bytes 2752544 | tf_op jit(solution)/shard_map/all_to_all | solution.py:108
  83.8 0.9 slice_bitcast_fusion.12
  84.8 1.9 %multiply_sine_fusion = (f32[4,256,128]{2,1,0:T(8,128)S(1)}, f32[4,256,128]{2,1,0:T(8,128)S(1)}) fusion(f32[128]{0:T(128)S(1)} %pad_maximum_fusion.9, f32[4,256]{1,0:T(4,128)S(1)} %mul.137), kind=kLoop, calls=%fused_computation.66 | loop fusion | flops 131072 | bytes 1053184 | tf_op jit(solution)/shard_map/sin | solution.py:132
  86.7 0.5 fusion.46
  87.3 0.6 fusion.47
  87.8 0.6 fusion.45
  88.4 0.6 fusion.44
  88.9 1.1 slice_bitcast_fusion.11
  90.1 3.8 %collective-permute-start = (f32[4,256,128]{2,1,0:T(8,128)S(1)}, f32[4,256,128]{2,1,0:T(8,128)S(1)}, u32[]{:S(2)}, u32[]{:S(2)}) collective-permute-start(f32[4,256,128]{2,1,0:T(8,128)S(1)} %pad_maximum_fusion.1), channel_id=1, source_target_pairs={{0,1},{1,0},{2,3},{3,2},{4,5},{5,4},{6,7},{7,6},{8,9},{9,8},{10,11... | collective-permute-start | bytes 1572872 | tf_op jit(solution)/shard_map/ppermute | solution.py:116
  93.9 0.6 add_add_fusion
  94.5 0.7 add_add_fusion.1
  95.2 2.2 %fusion.36 = (f32[256,512]{1,0:T(8,128)S(1)}, f32[256,512]{1,0:T(8,128)S(1)}, f32[256,512]{1,0:T(8,128)S(1)}, f32[256,512]{1,0:T(8,128)S(1)}, f32[256,512]{1,0:T...) fusion(f32[4,256,768]{2,1,0:T(8,128)S(1)} %add_add_fusion.1, ...), kind=kLoop, calls=%fused_computation.89 | loop fusion | flops 1048576 | bytes 10485760 | tf_op jit(solution)/shard_map/mul | solution.py:142
  97.7 2.4 %fusion = f32[4,256,1024]{2,1,0:T(8,128)S(1)} fusion(f32[4,256,256]{2,1,0:T(8,128)S(1)} %fusion.93, f32[1,256,1024]{2,1,0:T(8,128)S(1)} %get-tuple-element.50, f32[1,256,1024]{2,1,0:T(8,128)S(1)} %get-tuple-element.49, f32[1,256,1024]{2,1,0:T(8,128)S(1)} %get-tuple-element.48, f32[1,256,1024]{2,1,0:T(8,128)S(1)} %get-tuple-element.47), kind=kOutput, calls=%fused_computation | convolution fusion | flops 1613758464 | bytes 9437184 | tf_op jit(solution)/shard_map/aed,adc->aec/dot_general | solution.py:147
  100.7 3.8 %fusion.17 = f32[512,1024]{1,0:T(8,128)S(1)} fusion(f32[4,256,1024]{2,1,0:T(8,128)S(1)} %fusion, f32[1,256,512]{2,1,0:T(8,128)S(1)} %get-tuple-element.54, f32[1,256,512]{2,1,0:T(8,128)S(1)} %get-tuple-element.53, f32[1,256,512]{2,1,0:T(8,128)S(1)} %get-tuple-element.52, f32[1,256,512]{2,1,0:T(8,128)S(1)} %get-tuple-element.51), kind=kOutput, calls=%fused_computation.25 | convolution fusion | flops 3222798336 | bytes 8388608 | tf_op jit(solution)/shard_map/aer,aec->rc/dot_general | solution.py:148
  104.7 0.5 fusion.48
  105.3 0.5 convolution_add_fusion.7
  105.8 0.5 convolution_add_fusion.6
  106.8 0.5 convolution_add_fusion.5
  107.4 0.5 convolution_add_fusion.4
  108.4 0.5 convolution_add_fusion.3
  108.9 0.5 convolution_add_fusion.2
  109.5 0.7 fusion.51
  110.2 0.5 convolution_add_fusion.1
  110.7 0.5 convolution_add_fusion
  111.3 0.8 fusion.22
  112.0 0.7 fusion.21
  112.8 2.2 %add_add_fusion.2 = f32[512,1024]{1,0:T(8,128)} fusion(f32[512,1024]{1,0:T(8,128)S(1)} %fusion.21, f32[512,1024]{1,0:T(8,128)S(1)} %fusion.22, f32[512,256]{0,1:T(8,128)S(1)} %convolution_add_fusion, f32[512,256]{0,1:T(8,128)S(1)} %convolution_add_fusion.2, f32[512,256]{0,1:T(8,128)S(1)} %convolution_add_fusion.4, ...), kind=kOutput, calls=%fused_computation.24 | convolution fusion | flops 543424512 | bytes 8397824 | tf_op jit(solution)/shard_map/dot_general | solution.py:23
  (42 shorter events, 4.1 us)
Async XLA Ops:
  0.0 20.5 %copy-start = (f32[4,256,256]{2,1,0:T(8,128)S(1)}, f32[4,256,256]{2,1,0:T(8,128)}, u32[]{:S(2)}) copy-start(f32[4,256,256]{2,1,0:T(8,128)} %param.7) | copy-start | bytes 3145732
  3.4 80.4 %all-to-all-start = ((f32[32,8,2688]{2,1,0:T(8,128)}), f32[32,8,2688]{2,1,0:T(8,128)}, u32[]{:S(2)}, u32[]{:S(2)}) async-start(f32[32,8,2688]{2,1,0:T(8,128)} %shard_map.46), calls=%async_computation | async-start | bytes 5505024 | tf_op jit(solution)/shard_map/all_to_all | solution.py:108
  90.1 10.0 %collective-permute-start = (f32[4,256,128]{2,1,0:T(8,128)S(1)}, f32[4,256,128]{2,1,0:T(8,128)S(1)}, u32[]{:S(2)}, u32[]{:S(2)}) collective-permute-start(f32[4,256,128]{2,1,0:T(8,128)S(1)} %pad_maximum_fusion.1), channel_id=1, source_target_pairs={{0,1},{1,0},{2,3},{3,2},{4,5},{5,4},{6,7},{7,6},{8,9},{9,8},{10,11... | collective-permute-start | bytes 1572872 | tf_op jit(solution)/shard_map/ppermute | solution.py:116

commit v12 on v10

--- a/solution.py
+++ b/solution.py
@@ -17,14 +17,20 @@
 
 
 def permute_exact(x, perm, left=False):
-    out = None
-    for piece in split3(x):
-        if left:
-            term = jnp.dot(perm, piece, preferred_element_type=jnp.float32)
-        else:
-            term = jnp.dot(piece, perm, preferred_element_type=jnp.float32)
-        out = term if out is None else out + term
-    return out
+    pieces = split3(x)
+    if left:
+        return jnp.einsum(
+            "dk,...kc->...dc",
+            jnp.concatenate([perm] * 3, axis=1),
+            jnp.concatenate(pieces, axis=-2),
+            preferred_element_type=jnp.float32,
+        )
+    return jnp.einsum(
+        "...k,kc->...c",
+        jnp.concatenate(pieces, axis=-1),
+        jnp.concatenate([perm] * 3, axis=0),
+        preferred_element_type=jnp.float32,
+    )
 
 
 def col_perm(half):

time: 115 us -> 112 us (0.974)
  other arithmetic: 6.51 us -> 11.1 us
  matrix products: 20.1 us -> 16.5 us
  waiting for transfers between devices: 62.2 us -> 58.7 us
    dot_general x12 -> x4, matrix products: 12.9 us -> 9.01 us  [the longest x3 5.86 us: permute_exact(): jnp.einsum('...k,kc->...c', jnp.concatenate(pieces, axis=-1), jnp.concate...]
    all_to_all x1, waiting for transfers between devices: 62.2 us -> 58.7 us  [shards(): arrived = lax.all_to_all(payload, 'obs', 0, 0, tiled=True)]
    eq x0 -> x2, other arithmetic: none -> 3.41 us  [the longest x1 2.52 us: col_perm(): return (dst == 2 * (src % half) + src // half).astype(jnp.bfloat16)]
  transfers between devices with their start and end apart: 2 -> 2, of which waited for: 1 -> 1; matrix products, arithmetic and copies ran while one was open for 9% -> 16% of each run, Pallas kernels for 0% -> 0%
where the time goes in v12:
time: 112 us
  waiting for transfers between devices  58.7 us (52%)
  starting transfers between devices  17.3 us (15%)
  matrix products  16.5 us (15%)
  other arithmetic  11.1 us (10%)
  local copies, waits for them, and re-layouts  4.22 us (4%)
  Pallas kernels  3.37 us (3%)
    all_to_all x1, waiting for transfers between devices, shards(): arrived = lax.all_to_all(payload, 'obs', 0, 0, tiled=True)  58.7 us
    all_to_all x1, starting transfers between devices, shards(): arrived = lax.all_to_all(payload, 'obs', 0, 0, tiled=True)  13.6 us
    dot_general x3, matrix products, permute_exact(): jnp.einsum('...k,kc->...c', jnp.concatenate(pieces, axis=-1), jnp.concate...  5.86 us
    dot_general x1, matrix products, shards(): jnp.einsum('aer,aec->rc', jnp.stack(row_designs), col_mixed, precision=high)  4.02 us
    ppermute x1, starting transfers between devices, shards(): theirs = lax.ppermute(mine, 'gc', swap)  3.77 us
    pallas_call x1, Pallas kernels, build_payload(): pl.pallas_call(kernel, out_shape=jax.ShapeDtypeStruct((peers, epochs_loca...  3.37 us
    dot_general x1, matrix products, permute_exact(): jnp.einsum('dk,...kc->...dc', jnp.concatenate([perm] * 3, axis=1), jnp.co...  3.15 us
    eq x1, other arithmetic, col_perm(): return (dst == 2 * (src % half) + src // half).astype(jnp.bfloat16)  2.52 us
  transfers between devices with their start and end apart: 2, of which 1 were waited for; matrix products, arithmetic and copies ran while one was open for 16% of the time, Pallas kernels for 0%

profile of v12, /device:TPU:1, one launch (start us, length us, event | category | flops | bytes accessed | tf_op | source)
XLA Modules:
  0.0 111.5 jit_solution(6356915629158769482)
XLA Ops:
  0.0 3.4 %shard_map.46 = f32[32,8,2688]{2,1,0:T(8,128)} custom-call(f32[4,8,8192]{2,1,0:T(8,128)} %leg_ref.1, f32[4,8]{1,0:T(4,128)} %lon_ref.1), custom_call_target="tpu_custom_call" | custom-call | tf_op jit(solution)/shard_map/pallas_call | solution.py:76
  3.4 13.6 %all-to-all-start = ((f32[32,8,2688]{2,1,0:T(8,128)}), f32[32,8,2688]{2,1,0:T(8,128)}, u32[]{:S(2)}, u32[]{:S(2)}) async-start(f32[32,8,2688]{2,1,0:T(8,128)} %shard_map.46), calls=%async_computation | async-start | bytes 5505024 | tf_op jit(solution)/shard_map/all_to_all | solution.py:114
  17.0 0.8 dynamic_slice.6
  17.7 0.1 slice_compare_fusion
  17.8 0.1 convert_bitcast_fusion
  17.9 0.3 reduce-window.16
  18.3 0.1 slice_reduce_fusion
  18.5 0.1 select_reduce_fusion
  18.6 0.8 dynamic_slice.7
  19.5 0.1 fusion.84
  19.6 0.3 reduce-window.24
  20.0 0.1 slice_reduce_fusion.1
  20.2 0.1 select_reduce_fusion.1
  20.7 0.9 add_compare_fusion.1
  21.6 1.1 fusion.93
  22.6 2.5 %add_compare_fusion = pred[1024,1024]{1,0:T(32,128)(4,1)} fusion(s32[1024]{0:T(1024)S(1)} %get-tuple-element.51, s32[1024]{0:T(1024)S(1)} %get-tuple-element.54, s32[1024]{0:T(1024)S(1)} %get-tuple-element.52, s32[1024]{0:T(1024)S(1)} %get-tuple-element.53, pred[1024]{0:T(1024)(128)(4,1)S(1)} %get-tuple-element.55, pred[1024]{0:T(1024)(128)(4,1)S(1)} %get-tuple-element.56), kind=kLoop, calls=%fused_computation.14 | loop fusion | flops 5242880 | bytes 1067008 | tf_op jit(solution)/shard_map/eq | solution.py:39
  25.1 58.7 %all-to-all-done = f32[32,8,2688]{2,1,0:T(8,128)} async-done(((f32[32,8,2688]{2,1,0:T(8,128)}), f32[32,8,2688]{2,1,0:T(8,128)}, u32[]{:S(2)}, u32[]{:S(2)}) %all-to-all-start) | async-done | bytes 2752544 | tf_op jit(solution)/shard_map/all_to_all | solution.py:114
  83.8 1.1 %slice_bitcast_fusion.11 = (f32[1,256,128]{2,1,0:T(8,128)S(1)}, f32[1,256,128]{2,1,0:T(8,128)S(1)}, f32[1,256,128]{2,1,0:T(8,128)S(1)}, f32[1,256,128]{2,1,0:T(8,128)S(1)}) fusion(f32[256,2688]{1,0:T(8,128)} %bitcast), kind=kLoop, calls=%fused_computation.127 | loop fusion | bytes 1048576 | tf_op jit(solution)/shard_map/stack | solution.py:119
  84.9 0.8 pad_maximum_fusion
  85.8 3.8 %collective-permute-start = (f32[4,256,128]{2,1,0:T(8,128)}, f32[4,256,128]{2,1,0:T(8,128)S(1)}, u32[]{:S(2)}, u32[]{:S(2)}) collective-permute-start(f32[4,256,128]{2,1,0:T(8,128)} %pad_maximum_fusion), channel_id=1, source_target_pairs={{0,1},{1,0},{2,3},{3,2},{4,5},{5,4},{6,7},{7,6},{8,9},{9,8},{10,11... | collective-permute-start | bytes 1572872 | tf_op jit(solution)/shard_map/ppermute | solution.py:122
  89.6 0.9 slice_bitcast_fusion.12
  90.5 0.1 mul.119
  90.6 1.9 %multiply_sine_fusion = (f32[4,256,128]{2,1,0:T(8,128)S(1)}, f32[4,256,128]{2,1,0:T(8,128)S(1)}) fusion(f32[128]{0:T(128)S(1)} %pad_maximum_fusion.1, f32[4,256]{1,0:T(4,128)S(1)} %mul.119), kind=kLoop, calls=%fused_computation.77 | loop fusion | flops 131072 | bytes 1053184 | tf_op jit(solution)/shard_map/sin | solution.py:138
  92.5 0.4 reduce-precision_convert_fusion.5
  92.9 1.0 fusion.40
  93.9 1.0 fusion.42
  94.9 2.2 %fusion.63 = (f32[256,512]{1,0:T(8,128)S(1)}, f32[256,512]{1,0:T(8,128)S(1)}, f32[256,512]{1,0:T(8,128)S(1)}, f32[256,512]{1,0:T(8,128)S(1)}, f32[256,512]{1,0:T...) fusion(f32[4,256,768]{2,1,0:T(8,128)S(1)} %fusion.42, f32[256,2688]{1,0:T(8,128)} %bitcast, ...), kind=kLoop, calls=%fused_computation.96 | loop fusion | flops 1048576 | bytes 10485760 | tf_op jit(solution)/shard_map/mul | solution.py:148
  97.4 2.4 %fusion.6 = f32[4,256,1024]{2,1,0:T(8,128)S(1)} fusion(f32[4,256,256]{2,1,0:T(8,128)S(1)} %fusion.93, f32[1,256,1024]{2,1,0:T(8,128)S(1)} %maximum_bitcast_fusion.3, f32[1,256,1024]{2,1,0:T(8,128)S(1)} %maximum_bitcast_fusion.2, f32[1,256,1024]{2,1,0:T(8,128)S(1)} %maximum_bitcast_fusion.1, f32[1,256,1024]{2,1,0:T(8,128)S(1)} %maximum_bitcast_fusion), kind=kOutput, calls=%fused_computation.6 | convolution fusion | flops 1613758464 | bytes 9437184 | tf_op jit(solution)/shard_map/aed,adc->aec/dot_general | solution.py:153
  99.9 0.2 fusion.71
  100.4 4.0 %reduce-precision_convert_fusion.3 = (bf16[512,1024]{1,0:T(8,128)(2,1)S(1)}, bf16[512,1024]{1,0:T(8,128)(2,1)S(1)}, bf16[512,1024]{1,0:T(8,128)(2,1)S(1)}) fusion(f32[4,256,1024]{2,1,0:T(8,128)S(1)} %fusion.6, f32[1,256,512]{2,1,0:T(8,128)S(1)} %maximum_bitcast_fusion.7, f32[1,256,512]{2,1,0:T(8,128)S(1)} %maximum_bitcast_fusion.6, ...), kind=kOutput, calls=%fused_computation.38 | convolution fusion | flops 3226468352 | bytes 9437184 | tf_op jit(solution)/shard_map/aer,aec->rc/dot_general | solution.py:154
  104.5 3.9 %reduce-precision_convert_fusion.1 = (bf16[512,1024]{1,0:T(8,128)(2,1)S(1)}, bf16[512,1024]{1,0:T(8,128)(2,1)S(1)}, bf16[512,1024]{1,0:T(8,128)(2,1)S(1)}) fusion(pred[1024,1024]{1,0:T(32,128)(4,1)S(1)} %copy-done.1, bf16[512,1024]{1,0:T(8,128)(2,1)S(1)} %get-tuple-element.37, bf16[512,1024]{1,0:T(8,128)(2,1)S(1)} %get-tuple-element.38, ...), kind=kOutput, calls=%fused_computation.34 | convolution fusion | flops 3240624128 | bytes 7340032 | tf_op jit(solution)/shard_map/...k,kc->...c/dot_general | solution.py:28
  108.4 3.1 %fusion.19 = f32[512,1024]{1,0:T(8,128)} fusion(bf16[512,1024]{1,0:T(8,128)(2,1)S(1)} %get-tuple-element.34, bf16[512,1024]{1,0:T(8,128)(2,1)S(1)} %get-tuple-element.35, bf16[512,1024]{1,0:T(8,128)(2,1)S(1)} %get-tuple-element.33, pred[512,512]{1,0:T(32,128)(4,1)S(1)} %copy-done.2), kind=kOutput, calls=%fused_computation.20 | convolution fusion | flops 1621622784 | bytes 5505024 | tf_op jit(solution)/shard_map/dk,...kc->...dc/dot_general | solution.py:22
  (41 shorter events, 1.4 us)
Async XLA Ops:
  0.0 21.5 %copy-start = (f32[4,256,256]{2,1,0:T(8,128)S(1)}, f32[4,256,256]{2,1,0:T(8,128)}, u32[]{:S(2)}) copy-start(f32[4,256,256]{2,1,0:T(8,128)} %param.7) | copy-start | bytes 3145732
  3.4 80.4 %all-to-all-start = ((f32[32,8,2688]{2,1,0:T(8,128)}), f32[32,8,2688]{2,1,0:T(8,128)}, u32[]{:S(2)}, u32[]{:S(2)}) async-start(f32[32,8,2688]{2,1,0:T(8,128)} %shard_map.46), calls=%async_computation | async-start | bytes 5505024 | tf_op jit(solution)/shard_map/all_to_all | solution.py:114
  85.8 14.1 %collective-permute-start = (f32[4,256,128]{2,1,0:T(8,128)}, f32[4,256,128]{2,1,0:T(8,128)S(1)}, u32[]{:S(2)}, u32[]{:S(2)}) collective-permute-start(f32[4,256,128]{2,1,0:T(8,128)} %pad_maximum_fusion), channel_id=1, source_target_pairs={{0,1},{1,0},{2,3},{3,2},{4,5},{5,4},{6,7},{7,6},{8,9},{9,8},{10,11... | collective-permute-start | bytes 1572872 | tf_op jit(solution)/shard_map/ppermute | solution.py:122
  100.4 4.0 %copy-start.1 = (pred[1024,1024]{1,0:T(32,128)(4,1)S(1)}, pred[1024,1024]{1,0:T(32,128)(4,1)}, u32[]{:S(2)}) copy-start(pred[1024,1024]{1,0:T(32,128)(4,1)} %add_compare_fusion) | copy-start | bytes 3145732
  104.5 3.9 %copy-start.2 = (pred[512,512]{1,0:T(32,128)(4,1)S(1)}, pred[512,512]{1,0:T(32,128)(4,1)}, u32[]{:S(2)}) copy-start(pred[512,512]{1,0:T(32,128)(4,1)} %add_compare_fusion.1) | copy-start | bytes 786436

commit v13 on v12

--- a/solution.py
+++ b/solution.py
@@ -65,8 +65,9 @@
         def one_peer(j, carry):
             base = pl.multiple_of((step * per_step + j) * row_pairs + row_sub, LANES)
             for a in range(arcs):
-                out_ref[j, :, a * width : a * width + col_pairs] = cols[a]
-                out_ref[j, :, a * width + col_pairs : (a + 1) * width] = leg_ref[a, :, pl.ds(base, half_rows)]
+                out_ref[j, :, a * col_pairs : (a + 1) * col_pairs] = cols[a]
+                rows_at = arcs * col_pairs + a * half_rows
+                out_ref[j, :, rows_at : rows_at + half_rows] = leg_ref[a, :, pl.ds(base, half_rows)]
             out_ref[j, :, arcs * width :] = jnp.zeros((epochs_local, LANES), out_ref.dtype)
             out_ref[j, :arcs, arcs * width : arcs * width + epochs_local] = lon
             return carry
@@ -116,13 +117,17 @@
     lon_all = lon_all.reshape(arcs, epochs)
     arrived = arrived.reshape(epochs, arcs * width + LANES)
 
-    mine = jnp.stack([arrived[:, arc * width + col_pairs : (arc + 1) * width] for arc in range(arcs)])
+    mine = arrived[:, arcs * col_pairs : arcs * width]
     gc_count = lax.axis_size("gc")
     swap = [(k, k ^ 1) for k in range(gc_count)]
     theirs = lax.ppermute(mine, "gc", swap)
-    row_all = jnp.where(
-        core == 0, jnp.concatenate([mine, theirs], axis=2), jnp.concatenate([theirs, mine], axis=2)
-    )
+    row_all = []
+    for arc in range(arcs):
+        mine_arc = mine[:, arc * half_rows : (arc + 1) * half_rows]
+        theirs_arc = theirs[:, arc * half_rows : (arc + 1) * half_rows]
+        row_all.append(jnp.where(
+            core == 0, jnp.concatenate([mine_arc, theirs_arc], axis=1), jnp.concatenate([theirs_arc, mine_arc], axis=1)
+        ))
 
     col_hot, col_value = runs_of(lax.dynamic_slice_in_dim(orders, grid_position * col_pairs, col_pairs, 0))
     row_hot, row_value = runs_of(lax.dynamic_slice_in_dim(orders, obs_position * row_pairs, row_pairs, 0))
@@ -142,7 +147,7 @@
     gram = jnp.einsum("afe,afd->aed", whitening, whitening, precision=high)
     col_designs, row_designs = [], []
     for arc in range(arcs):
-        col_values_all = arrived[:, arc * width : arc * width + col_pairs]
+        col_values_all = arrived[:, arc * col_pairs : (arc + 1) * col_pairs]
         row_values_all = row_all[arc]
         col_designs.append(jnp.concatenate(
             [col_values_all * cos_all[arc, :, :col_pairs], col_values_all * sin_all[arc, :, :col_pairs]], axis=1

time: 112 us -> 111 us (level)
  other arithmetic: 11.1 us -> 9.57 us
    slice x1 -> x3, local copies, waits for them, and re-layouts: 0.07 us -> 1.25 us  [the longest x1 1.14 us: shards(): mine_arc = mine[:, arc * half_rows:(arc + 1) * half_rows]]
    another operation x4 -> x3, local copies, waits for them, and re-layouts: 1.44 us -> 0.31 us  [the longest x1 1.14 us: shards(): jnp.stack([arrived[:, arc * width + col_pairs:(arc + 1) * width] for arc...]
  transfers between devices with their start and end apart: 2 -> 2, of which waited for: 1 -> 1; matrix products, arithmetic and copies ran while one was open for 16% -> 9% of each run, Pallas kernels for 0% -> 0%
where the time goes in v13:
time: 111 us
  waiting for transfers between devices  59.7 us (54%)
  starting transfers between devices  17.4 us (16%)
  matrix products  16.2 us (15%)
  other arithmetic  9.57 us (9%)
  local copies, waits for them, and re-layouts  4.26 us (4%)
  Pallas kernels  3.37 us (3%)
    all_to_all x1, waiting for transfers between devices, shards(): arrived = lax.all_to_all(payload, 'obs', 0, 0, tiled=True)  59.7 us
    all_to_all x1, starting transfers between devices, shards(): arrived = lax.all_to_all(payload, 'obs', 0, 0, tiled=True)  13.6 us
    dot_general x3, matrix products, permute_exact(): jnp.einsum('...k,kc->...c', jnp.concatenate(pieces, axis=-1), jnp.concate...  5.62 us
    dot_general x1, matrix products, shards(): jnp.einsum('aer,aec->rc', jnp.stack(row_designs), col_mixed, precision=high)  3.99 us
    ppermute x1, starting transfers between devices, shards(): theirs = lax.ppermute(mine, 'gc', swap)  3.78 us
    pallas_call x1, Pallas kernels, build_payload(): pl.pallas_call(kernel, out_shape=jax.ShapeDtypeStruct((peers, epochs_loca...  3.37 us
    dot_general x1, matrix products, permute_exact(): jnp.einsum('dk,...kc->...dc', jnp.concatenate([perm] * 3, axis=1), jnp.co...  3.15 us
    mul x1, other arithmetic, shards(): col_values_all * cos_all[arc, :, :col_pairs]  2.51 us
  transfers between devices with their start and end apart: 2, of which 1 were waited for; matrix products, arithmetic and copies ran while one was open for 9% of the time, Pallas kernels for 0%

profile of v13, /device:TPU:1, one launch (start us, length us, event | category | flops | bytes accessed | tf_op | source)
XLA Modules:
  0.0 110.8 jit_solution(3842977780393602447)
XLA Ops:
  0.0 3.4 %shard_map.46 = f32[32,8,2688]{2,1,0:T(8,128)} custom-call(f32[4,8,8192]{2,1,0:T(8,128)} %leg_ref.1, f32[4,8]{1,0:T(4,128)} %lon_ref.1), custom_call_target="tpu_custom_call" | custom-call | tf_op jit(solution)/shard_map/pallas_call | solution.py:77
  3.4 13.6 %all-to-all-start = ((f32[32,8,2688]{2,1,0:T(8,128)}), f32[32,8,2688]{2,1,0:T(8,128)}, u32[]{:S(2)}, u32[]{:S(2)}) async-start(f32[32,8,2688]{2,1,0:T(8,128)} %shard_map.46), calls=%async_computation | async-start | bytes 5505024 | tf_op jit(solution)/shard_map/all_to_all | solution.py:115
  17.0 0.8 dynamic_slice.6
  17.9 0.3 reduce-window.16
  18.3 0.1 slice_reduce_fusion
  18.5 0.1 select_reduce_fusion
  18.6 0.8 dynamic_slice.7
  19.5 0.3 reduce-window.24
  20.0 0.1 slice_reduce_fusion.1
  20.2 0.1 select_reduce_fusion.1
  20.7 0.9 add_compare_fusion.1
  21.5 1.1 fusion.95
  22.6 1.5 %add_compare_fusion = pred[1024,1024]{1,0:T(32,128)(4,1)S(1)} fusion(s32[1024]{0:T(1024)S(1)} %get-tuple-element.56, s32[1024]{0:T(1024)S(1)} %get-tuple-element.59, s32[1024]{0:T(1024)S(1)} %get-tuple-element.57, s32[1024]{0:T(1024)S(1)} %get-tuple-element.58, pred[1024]{0:T(1024)(128)(4,1)S(1)} %get-tuple-element.60, pred[1024]{0:T(1024)(128)(4,1)S(1)} %get-tuple-element.61), kind=kLoop, calls=%fused_computation.14 | loop fusion | flops 5242880 | bytes 1067008 | tf_op jit(solution)/shard_map/eq | solution.py:39
  24.1 59.7 %all-to-all-done = f32[32,8,2688]{2,1,0:T(8,128)} async-done(((f32[32,8,2688]{2,1,0:T(8,128)}), f32[32,8,2688]{2,1,0:T(8,128)}, u32[]{:S(2)}, u32[]{:S(2)}) %all-to-all-start) | async-done | bytes 2752544 | tf_op jit(solution)/shard_map/all_to_all | solution.py:115
  83.8 0.9 slice_bitcast_fusion.16
  84.7 0.1 mul.95
  84.8 1.9 %multiply_sine_fusion = (f32[4,256,128]{2,1,0:T(8,128)S(1)}, f32[4,256,128]{2,1,0:T(8,128)S(1)}) fusion(f32[128]{0:T(128)S(1)} %pad_maximum_fusion, f32[4,256]{1,0:T(4,128)S(1)} %mul.95), kind=kLoop, calls=%fused_computation.76 | loop fusion | flops 131072 | bytes 1053184 | tf_op jit(solution)/shard_map/sin | solution.py:143
  86.7 1.1 %fusion.93 = (f32[256,128]{1,0:T(8,128)S(1)}, f32[256,128]{1,0:T(8,128)S(1)}, f32[256,128]{1,0:T(8,128)S(1)}, f32[256,128]{1,0:T(8,128)S(1)}) fusion(f32[256,2688]{1,0:T(8,128)} %bitcast), kind=kLoop, calls=%fused_computation.169 | loop fusion | bytes 1048576 | tf_op jit(solution)/shard_map/slice | solution.py:126
  87.9 0.4 reduce-precision_convert_fusion.5
  88.3 1.0 fusion.40
  89.3 1.0 fusion.42
  90.3 2.5 %fusion.63 = (f32[256,512]{1,0:T(8,128)S(1)}, f32[256,512]{1,0:T(8,128)S(1)}, f32[256,512]{1,0:T(8,128)S(1)}, f32[256,512]{1,0:T(8,128)S(1)}, f32[256,512]{1,0:T...) fusion(f32[4,256,768]{2,1,0:T(8,128)S(1)} %fusion.42, ...), kind=kLoop, calls=%fused_computation.95 | loop fusion | flops 1048576 | bytes 11534336 | tf_op jit(solution)/shard_map/mul | solution.py:153
  92.8 3.8 %collective-permute-start = (f32[256,512]{1,0:T(8,128)S(1)}, f32[256,512]{1,0:T(8,128)S(1)}, u32[]{:S(2)}, u32[]{:S(2)}) collective-permute-start(f32[256,512]{1,0:T(8,128)S(1)} %get-tuple-element.28), channel_id=1, source_target_pairs={{0,1},{1,0},{2,3},{3,2},{4,5},{5,4},{6,7},{7,6},{8,9},{9,8},{10,11... | collective-permute-start | bytes 1572872 | tf_op jit(solution)/shard_map/ppermute | solution.py:123
  96.7 0.1 maximum_bitcast_fusion.1
  96.7 0.1 maximum_bitcast_fusion.2
  96.8 0.1 maximum_bitcast_fusion.3
  96.9 2.4 %fusion.6 = f32[4,256,1024]{2,1,0:T(8,128)S(1)} fusion(f32[4,256,256]{2,1,0:T(8,128)S(1)} %fusion.95, f32[1,256,1024]{2,1,0:T(8,128)S(1)} %maximum_bitcast_fusion.3, f32[1,256,1024]{2,1,0:T(8,128)S(1)} %maximum_bitcast_fusion.2, f32[1,256,1024]{2,1,0:T(8,128)S(1)} %maximum_bitcast_fusion.1, f32[1,256,1024]{2,1,0:T(8,128)S(1)} %maximum_bitcast_fusion), kind=kOutput, calls=%fused_computation.6 | convolution fusion | flops 1613758464 | bytes 9437184 | tf_op jit(solution)/shard_map/aed,adc->aec/dot_general | solution.py:158
  99.4 0.1 fusion.71
  99.5 0.1 fusion.70
  100.0 4.0 %reduce-precision_convert_fusion.3 = (bf16[512,1024]{1,0:T(8,128)(2,1)S(1)}, bf16[512,1024]{1,0:T(8,128)(2,1)S(1)}, bf16[512,1024]{1,0:T(8,128)(2,1)S(1)}) fusion(f32[4,256,1024]{2,1,0:T(8,128)S(1)} %fusion.6, f32[1,256,512]{2,1,0:T(8,128)S(1)} %maximum_bitcast_fusion.7, f32[1,256,512]{2,1,0:T(8,128)S(1)} %maximum_bitcast_fusion.6, ...), kind=kOutput, calls=%fused_computation.38 | convolution fusion | flops 3226468352 | bytes 9437184 | tf_op jit(solution)/shard_map/aer,aec->rc/dot_general | solution.py:159
  104.0 3.6 %reduce-precision_convert_fusion.1 = (bf16[512,1024]{1,0:T(8,128)(2,1)S(1)}, bf16[512,1024]{1,0:T(8,128)(2,1)S(1)}, bf16[512,1024]{1,0:T(8,128)(2,1)S(1)}) fusion(pred[1024,1024]{1,0:T(32,128)(4,1)S(1)} %add_compare_fusion, bf16[512,1024]{1,0:T(8,128)(2,1)S(1)} %get-tuple-element.37, bf16[512,1024]{1,0:T(8,128)(2,1)S(1)} %get-tuple-element.38, ...), kind=kOutput, calls=%fused_computation.34 | convolution fusion | flops 3240624128 | bytes 7340032 | tf_op jit(solution)/shard_map/...k,kc->...c/dot_general | solution.py:28
  107.6 3.1 %fusion.19 = f32[512,1024]{1,0:T(8,128)} fusion(bf16[512,1024]{1,0:T(8,128)(2,1)S(1)} %get-tuple-element.34, bf16[512,1024]{1,0:T(8,128)(2,1)S(1)} %get-tuple-element.35, bf16[512,1024]{1,0:T(8,128)(2,1)S(1)} %get-tuple-element.33, pred[512,512]{1,0:T(32,128)(4,1)S(1)} %copy-done.1), kind=kOutput, calls=%fused_computation.20 | convolution fusion | flops 1621622784 | bytes 5505024 | tf_op jit(solution)/shard_map/dk,...kc->...dc/dot_general | solution.py:22
  (40 shorter events, 1.4 us)
Async XLA Ops:
  0.0 21.5 %copy-start = (f32[4,256,256]{2,1,0:T(8,128)S(1)}, f32[4,256,256]{2,1,0:T(8,128)}, u32[]{:S(2)}) copy-start(f32[4,256,256]{2,1,0:T(8,128)} %param.7) | copy-start | bytes 3145732
  3.4 80.4 %all-to-all-start = ((f32[32,8,2688]{2,1,0:T(8,128)}), f32[32,8,2688]{2,1,0:T(8,128)}, u32[]{:S(2)}, u32[]{:S(2)}) async-start(f32[32,8,2688]{2,1,0:T(8,128)} %shard_map.46), calls=%async_computation | async-start | bytes 5505024 | tf_op jit(solution)/shard_map/all_to_all | solution.py:115
  92.8 6.6 %collective-permute-start = (f32[256,512]{1,0:T(8,128)S(1)}, f32[256,512]{1,0:T(8,128)S(1)}, u32[]{:S(2)}, u32[]{:S(2)}) collective-permute-start(f32[256,512]{1,0:T(8,128)S(1)} %get-tuple-element.28), channel_id=1, source_target_pairs={{0,1},{1,0},{2,3},{3,2},{4,5},{5,4},{6,7},{7,6},{8,9},{9,8},{10,11... | collective-permute-start | bytes 1572872 | tf_op jit(solution)/shard_map/ppermute | solution.py:123
  104.0 3.7 %copy-start.1 = (pred[512,512]{1,0:T(32,128)(4,1)S(1)}, pred[512,512]{1,0:T(32,128)(4,1)}, u32[]{:S(2)}) copy-start(pred[512,512]{1,0:T(32,128)(4,1)} %add_compare_fusion.1) | copy-start | bytes 786436

commit v14 on v13

--- a/solution.py
+++ b/solution.py
@@ -36,12 +36,6 @@
 def col_perm(half):
     src = lax.broadcasted_iota(jnp.int32, (2 * half, 2 * half), 0)
     dst = lax.broadcasted_iota(jnp.int32, (2 * half, 2 * half), 1)
-    return (dst == 2 * (src % half) + src // half).astype(jnp.bfloat16)
-
-
-def row_perm(half):
-    dst = lax.broadcasted_iota(jnp.int32, (2 * half, 2 * half), 0)
-    src = lax.broadcasted_iota(jnp.int32, (2 * half, 2 * half), 1)
     return (dst == 2 * (src % half) + src // half).astype(jnp.bfloat16)
 
 
@@ -156,8 +150,9 @@
             [row_values_all * cos_all[arc, :, col_pairs:], row_values_all * sin_all[arc, :, col_pairs:]], axis=1
         ))
     col_mixed = jnp.einsum("aed,adc->aec", gram, jnp.stack(col_designs), precision=high)
-    total = jnp.einsum("aer,aec->rc", jnp.stack(row_designs), col_mixed, precision=high)
-    return permute_exact(permute_exact(total, col_perm(col_pairs)), row_perm(row_pairs), left=True)
+    row_interleaved = permute_exact(jnp.stack(row_designs), col_perm(row_pairs))
+    total = jnp.einsum("aer,aec->rc", row_interleaved, col_mixed, precision=high)
+    return permute_exact(total, col_perm(col_pairs))
 
 def solution(mesh):
     placed = (P(None, "obs", None), P(None, "obs"), P(), P())

time: 111 us -> 112 us (level)
    dot_general x2 -> x1, matrix products: 7.14 us -> 3.98 us  [shards(): jnp.einsum('aer,aec->rc', row_interleaved, col_mixed, precision=high)]
    dot_general x3 -> x4, matrix products: 5.62 us -> 8.6 us  [permute_exact(): jnp.einsum('...k,kc->...c', jnp.concatenate(pieces, axis=-1), jnp.concate...]
    eq x1 -> x2, other arithmetic: 1.52 us -> 2.83 us  [col_perm(): return (dst == 2 * (src % half) + src // half).astype(jnp.bfloat16)]
where the time goes in v14:
time: 112 us; the launch traced here: 111 us
  waiting for transfers between devices  59.2 us (53%)
  starting transfers between devices  17.4 us (16%)
  matrix products  16 us (14%)
  other arithmetic  10.6 us (9%)
  local copies, waits for them, and re-layouts  4.57 us (4%)
  Pallas kernels  3.37 us (3%)
    all_to_all x1, waiting for transfers between devices, shards(): arrived = lax.all_to_all(payload, 'obs', 0, 0, tiled=True)  59.2 us
    all_to_all x1, starting transfers between devices, shards(): arrived = lax.all_to_all(payload, 'obs', 0, 0, tiled=True)  13.6 us
    dot_general x4, matrix products, permute_exact(): jnp.einsum('...k,kc->...c', jnp.concatenate(pieces, axis=-1), jnp.concate...  8.6 us
    dot_general x1, matrix products, shards(): jnp.einsum('aer,aec->rc', row_interleaved, col_mixed, precision=high)  3.98 us
    ppermute x1, starting transfers between devices, shards(): theirs = lax.ppermute(mine, 'gc', swap)  3.78 us
    pallas_call x1, Pallas kernels, build_payload(): pl.pallas_call(kernel, out_shape=jax.ShapeDtypeStruct((peers, epochs_loca...  3.37 us
    eq x2, other arithmetic, col_perm(): return (dst == 2 * (src % half) + src // half).astype(jnp.bfloat16)  2.83 us
    mul x1, other arithmetic, shards(): col_values_all * cos_all[arc, :, :col_pairs]  2.51 us
  transfers between devices with their start and end apart: 2, of which 1 were waited for; matrix products, arithmetic and copies ran while one was open for 9% of the time, Pallas kernels for 0%

profile of v14, /device:TPU:1, one launch (start us, length us, event | category | flops | bytes accessed | tf_op | source)
XLA Modules:
  0.0 111.5 jit_solution(2336979417137679977)
XLA Ops:
  0.0 3.4 %shard_map.46 = f32[32,8,2688]{2,1,0:T(8,128)} custom-call(f32[4,8,8192]{2,1,0:T(8,128)} %leg_ref.1, f32[4,8]{1,0:T(4,128)} %lon_ref.1), custom_call_target="tpu_custom_call" | custom-call | tf_op jit(solution)/shard_map/pallas_call | solution.py:71
  3.4 13.6 %all-to-all-start = ((f32[32,8,2688]{2,1,0:T(8,128)}), f32[32,8,2688]{2,1,0:T(8,128)}, u32[]{:S(2)}, u32[]{:S(2)}) async-start(f32[32,8,2688]{2,1,0:T(8,128)} %shard_map.46), calls=%async_computation | async-start | bytes 5505024 | tf_op jit(solution)/shard_map/all_to_all | solution.py:109
  17.0 0.8 dynamic_slice.6
  17.9 0.3 reduce-window.16
  18.3 0.8 dynamic_slice.7
  19.2 0.3 reduce-window.24
  19.6 0.1 slice_reduce_fusion.1
  19.8 0.1 select_reduce_fusion.1
  20.0 0.1 slice_reduce_fusion
  20.2 0.1 select_reduce_fusion
  20.7 1.3 %add_compare_fusion.1 = pred[512,512]{1,0:T(32,128)(4,1)} fusion(s32[512]{0:T(512)S(1)} %get-tuple-element.55, s32[512]{0:T(512)S(1)} %get-tuple-element.58, s32[512]{0:T(512)S(1)} %get-tuple-element.56, s32[512]{0:T(512)S(1)} %get-tuple-element.57, pred[512]{0:T(512)(128)(4,1)S(1)} %get-tuple-element.59, pred[512]{0:T(512)(128)(4,1)S(1)} %get-tuple-element.60), kind=kLoop, calls=%fused_computation.50 | loop fusion | flops 1310720 | bytes 271360 | tf_op jit(solution)/shard_map/eq | solution.py:39
  22.0 1.1 fusion.85
  23.0 1.5 %add_compare_fusion = pred[1024,1024]{1,0:T(32,128)(4,1)S(1)} fusion(s32[1024]{0:T(1024)S(1)} %get-tuple-element.61, s32[1024]{0:T(1024)S(1)} %get-tuple-element.64, s32[1024]{0:T(1024)S(1)} %get-tuple-element.62, s32[1024]{0:T(1024)S(1)} %get-tuple-element.63, pred[1024]{0:T(1024)(128)(4,1)S(1)} %get-tuple-element.65, pred[1024]{0:T(1024)(128)(4,1)S(1)} %get-tuple-element.66), kind=kLoop, calls=%fused_computation.14 | loop fusion | flops 5242880 | bytes 1067008 | tf_op jit(solution)/shard_map/eq | solution.py:39
  24.6 59.2 %all-to-all-done = f32[32,8,2688]{2,1,0:T(8,128)} async-done(((f32[32,8,2688]{2,1,0:T(8,128)}), f32[32,8,2688]{2,1,0:T(8,128)}, u32[]{:S(2)}, u32[]{:S(2)}) %all-to-all-start) | async-done | bytes 2752544 | tf_op jit(solution)/shard_map/all_to_all | solution.py:109
  83.8 0.9 slice_bitcast_fusion.16
  84.7 0.1 mul.93
  84.8 1.9 %multiply_sine_fusion = (f32[4,256,128]{2,1,0:T(8,128)S(1)}, f32[4,256,128]{2,1,0:T(8,128)S(1)}) fusion(f32[128]{0:T(128)S(1)} %pad_maximum_fusion.1, f32[4,256]{1,0:T(4,128)S(1)} %mul.93), kind=kLoop, calls=%fused_computation.69 | loop fusion | flops 131072 | bytes 1053184 | tf_op jit(solution)/shard_map/sin | solution.py:137
  86.7 1.1 %fusion.83 = (f32[256,128]{1,0:T(8,128)S(1)}, f32[256,128]{1,0:T(8,128)S(1)}, f32[256,128]{1,0:T(8,128)S(1)}, f32[256,128]{1,0:T(8,128)S(1)}) fusion(f32[256,2688]{1,0:T(8,128)} %bitcast), kind=kLoop, calls=%fused_computation.161 | loop fusion | bytes 1048576 | tf_op jit(solution)/shard_map/slice | solution.py:120
  87.9 0.4 reduce-precision_convert_fusion.5
  88.3 1.0 fusion.31
  89.3 1.0 fusion.33
  90.3 2.5 %fusion.54 = (f32[256,512]{1,0:T(8,128)S(1)}, f32[256,512]{1,0:T(8,128)S(1)}, f32[256,512]{1,0:T(8,128)S(1)}, f32[256,512]{1,0:T(8,128)S(1)}, f32[256,512]{1,0:T...) fusion(f32[4,256,768]{2,1,0:T(8,128)S(1)} %fusion.33, ...), kind=kLoop, calls=%fused_computation.88 | loop fusion | flops 1048576 | bytes 11534336 | tf_op jit(solution)/shard_map/mul | solution.py:147
  92.8 3.8 %collective-permute-start = (f32[256,512]{1,0:T(8,128)S(1)}, f32[256,512]{1,0:T(8,128)S(1)}, u32[]{:S(2)}, u32[]{:S(2)}) collective-permute-start(f32[256,512]{1,0:T(8,128)S(1)} %get-tuple-element.27), channel_id=1, source_target_pairs={{0,1},{1,0},{2,3},{3,2},{4,5},{5,4},{6,7},{7,6},{8,9},{9,8},{10,11... | collective-permute-start | bytes 1572872 | tf_op jit(solution)/shard_map/ppermute | solution.py:117
  96.6 0.1 maximum_bitcast_fusion.3
  96.9 2.4 %fusion.6 = f32[4,256,1024]{2,1,0:T(8,128)S(1)} fusion(f32[4,256,256]{2,1,0:T(8,128)S(1)} %fusion.85, f32[1,256,1024]{2,1,0:T(8,128)S(1)} %maximum_bitcast_fusion.3, f32[1,256,1024]{2,1,0:T(8,128)S(1)} %maximum_bitcast_fusion.2, f32[1,256,1024]{2,1,0:T(8,128)S(1)} %maximum_bitcast_fusion.1, f32[1,256,1024]{2,1,0:T(8,128)S(1)} %maximum_bitcast_fusion), kind=kOutput, calls=%fused_computation.6 | convolution fusion | flops 1613758464 | bytes 9437184 | tf_op jit(solution)/shard_map/aed,adc->aec/dot_general | solution.py:152
  99.4 0.1 fusion.61
  99.5 0.1 fusion.62
  100.0 0.5 reduce-precision_convert_fusion.3
  100.5 0.3 copy-done.1
  100.9 1.8 %fusion.14 = f32[4,256,512]{1,2,0:T(8,128)S(1)} fusion(bf16[4,256,512]{2,1,0:T(8,128)(2,1)S(1)} %get-tuple-element.37, bf16[4,256,512]{2,1,0:T(8,128)(2,1)S(1)} %get-tuple-element.36, bf16[4,256,512]{2,1,0:T(8,128)(2,1)S(1)} %get-tuple-element.35, pred[512,512]{1,0:T(32,128)(4,1)S(1)} %copy-done.1), kind=kOutput, calls=%fused_computation.15 | convolution fusion | flops 1621622784 | bytes 5505024 | tf_op jit(solution)/shard_map/...k,kc->...c/dot_general | solution.py:28
  102.7 4.0 %reduce-precision_convert_fusion.1 = (bf16[512,1024]{1,0:T(8,128)(2,1)S(1)}, bf16[512,1024]{1,0:T(8,128)(2,1)S(1)}, bf16[512,1024]{1,0:T(8,128)(2,1)S(1)}) fusion(f32[4,256,512]{1,2,0:T(8,128)S(1)} %fusion.14, f32[4,256,1024]{2,1,0:T(8,128)S(1)} %fusion.6), kind=kOutput, calls=%fused_computation.34 | convolution fusion | flops 3224895488 | bytes 9437184 | tf_op jit(solution)/shard_map/aer,aec->rc/dot_general | solution.py:154
  106.7 4.8 %fusion = f32[512,1024]{1,0:T(8,128)} fusion(pred[1024,1024]{1,0:T(32,128)(4,1)S(1)} %add_compare_fusion, bf16[512,1024]{1,0:T(8,128)(2,1)S(1)} %get-tuple-element.33, bf16[512,1024]{1,0:T(8,128)(2,1)S(1)} %get-tuple-element.34, bf16[512,1024]{1,0:T(8,128)(2,1)S(1)} %get-tuple-element.32), kind=kOutput, calls=%fused_computation | convolution fusion | flops 3236954112 | bytes 6291456 | tf_op jit(solution)/shard_map/...k,kc->...c/dot_general | solution.py:28
  (41 shorter events, 1.5 us)
Async XLA Ops:
  0.0 22.0 %copy-start = (f32[4,256,256]{2,1,0:T(8,128)S(1)}, f32[4,256,256]{2,1,0:T(8,128)}, u32[]{:S(2)}) copy-start(f32[4,256,256]{2,1,0:T(8,128)} %param.7) | copy-start | bytes 3145732
  3.4 80.4 %all-to-all-start = ((f32[32,8,2688]{2,1,0:T(8,128)}), f32[32,8,2688]{2,1,0:T(8,128)}, u32[]{:S(2)}, u32[]{:S(2)}) async-start(f32[32,8,2688]{2,1,0:T(8,128)} %shard_map.46), calls=%async_computation | async-start | bytes 5505024 | tf_op jit(solution)/shard_map/all_to_all | solution.py:109
  92.8 6.6 %collective-permute-start = (f32[256,512]{1,0:T(8,128)S(1)}, f32[256,512]{1,0:T(8,128)S(1)}, u32[]{:S(2)}, u32[]{:S(2)}) collective-permute-start(f32[256,512]{1,0:T(8,128)S(1)} %get-tuple-element.27), channel_id=1, source_target_pairs={{0,1},{1,0},{2,3},{3,2},{4,5},{5,4},{6,7},{7,6},{8,9},{9,8},{10,11... | collective-permute-start | bytes 1572872 | tf_op jit(solution)/shard_map/ppermute | solution.py:117
  99.9 1.0 copy-start.1

commit v15 on v13

--- a/solution.py
+++ b/solution.py
@@ -45,7 +45,7 @@
     return (dst == 2 * (src % half) + src // half).astype(jnp.bfloat16)
 
 
-GROUPS = 4
+GROUPS = 8
 
 
 def build_payload(legendre, longitude, peers, col_pairs, half_rows):

time: 111 us -> 113 us (1.018)
  Pallas kernels: 3.37 us -> 4.53 us
    pallas_call x1, Pallas kernels: 3.37 us -> 4.53 us  [build_payload(): pl.pallas_call(kernel, out_shape=jax.ShapeDtypeStruct((peers, epochs_loca...]
where the time goes in v15:
time: 113 us; the launch traced here: 112 us
  waiting for transfers between devices  59.7 us (53%)
  starting transfers between devices  17.4 us (15%)
  matrix products  16.2 us (14%)
  other arithmetic  9.57 us (8%)
  Pallas kernels  4.53 us (4%)
  local copies, waits for them, and re-layouts  4.26 us (4%)
    all_to_all x1, waiting for transfers between devices, shards(): arrived = lax.all_to_all(payload, 'obs', 0, 0, tiled=True)  59.7 us
    all_to_all x1, starting transfers between devices, shards(): arrived = lax.all_to_all(payload, 'obs', 0, 0, tiled=True)  13.6 us
    dot_general x3, matrix products, permute_exact(): jnp.einsum('...k,kc->...c', jnp.concatenate(pieces, axis=-1), jnp.concate...  5.62 us
    pallas_call x1, Pallas kernels, build_payload(): pl.pallas_call(kernel, out_shape=jax.ShapeDtypeStruct((peers, epochs_loca...  4.53 us
    dot_general x1, matrix products, shards(): jnp.einsum('aer,aec->rc', jnp.stack(row_designs), col_mixed, precision=high)  3.99 us
    ppermute x1, starting transfers between devices, shards(): theirs = lax.ppermute(mine, 'gc', swap)  3.78 us
    dot_general x1, matrix products, permute_exact(): jnp.einsum('dk,...kc->...dc', jnp.concatenate([perm] * 3, axis=1), jnp.co...  3.15 us
    mul x1, other arithmetic, shards(): col_values_all * cos_all[arc, :, :col_pairs]  2.51 us
  transfers between devices with their start and end apart: 2, of which 1 were waited for; matrix products, arithmetic and copies ran while one was open for 9% of the time, Pallas kernels for 0%

profile of v15, /device:TPU:1, one launch (start us, length us, event | category | flops | bytes accessed | tf_op | source)
XLA Modules:
  0.0 111.9 jit_solution(10617379474195411861)
XLA Ops:
  0.0 4.5 %shard_map.46 = f32[32,8,2688]{2,1,0:T(8,128)} custom-call(f32[4,8,8192]{2,1,0:T(8,128)} %leg_ref.1, f32[4,8]{1,0:T(4,128)} %lon_ref.1), custom_call_target="tpu_custom_call" | custom-call | tf_op jit(solution)/shard_map/pallas_call | solution.py:77
  4.5 13.6 %all-to-all-start = ((f32[32,8,2688]{2,1,0:T(8,128)}), f32[32,8,2688]{2,1,0:T(8,128)}, u32[]{:S(2)}, u32[]{:S(2)}) async-start(f32[32,8,2688]{2,1,0:T(8,128)} %shard_map.46), calls=%async_computation | async-start | bytes 5505024 | tf_op jit(solution)/shard_map/all_to_all | solution.py:115
  18.1 0.8 dynamic_slice.6
  19.0 0.3 reduce-window.16
  19.5 0.1 slice_reduce_fusion
  19.7 0.1 select_reduce_fusion
  19.8 0.8 dynamic_slice.7
  20.7 0.3 reduce-window.24
  21.1 0.1 slice_reduce_fusion.1
  21.3 0.1 select_reduce_fusion.1
  21.8 0.9 add_compare_fusion.1
  22.7 1.1 fusion.95
  23.8 1.5 %add_compare_fusion = pred[1024,1024]{1,0:T(32,128)(4,1)S(1)} fusion(s32[1024]{0:T(1024)S(1)} %get-tuple-element.56, s32[1024]{0:T(1024)S(1)} %get-tuple-element.59, s32[1024]{0:T(1024)S(1)} %get-tuple-element.57, s32[1024]{0:T(1024)S(1)} %get-tuple-element.58, pred[1024]{0:T(1024)(128)(4,1)S(1)} %get-tuple-element.60, pred[1024]{0:T(1024)(128)(4,1)S(1)} %get-tuple-element.61), kind=kLoop, calls=%fused_computation.14 | loop fusion | flops 5242880 | bytes 1067008 | tf_op jit(solution)/shard_map/eq | solution.py:39
  25.3 59.7 %all-to-all-done = f32[32,8,2688]{2,1,0:T(8,128)} async-done(((f32[32,8,2688]{2,1,0:T(8,128)}), f32[32,8,2688]{2,1,0:T(8,128)}, u32[]{:S(2)}, u32[]{:S(2)}) %all-to-all-start) | async-done | bytes 2752544 | tf_op jit(solution)/shard_map/all_to_all | solution.py:115
  85.0 0.9 slice_bitcast_fusion.16
  85.9 0.1 mul.95
  86.0 1.9 %multiply_sine_fusion = (f32[4,256,128]{2,1,0:T(8,128)S(1)}, f32[4,256,128]{2,1,0:T(8,128)S(1)}) fusion(f32[128]{0:T(128)S(1)} %pad_maximum_fusion, f32[4,256]{1,0:T(4,128)S(1)} %mul.95), kind=kLoop, calls=%fused_computation.76 | loop fusion | flops 131072 | bytes 1053184 | tf_op jit(solution)/shard_map/sin | solution.py:143
  87.9 1.1 %fusion.93 = (f32[256,128]{1,0:T(8,128)S(1)}, f32[256,128]{1,0:T(8,128)S(1)}, f32[256,128]{1,0:T(8,128)S(1)}, f32[256,128]{1,0:T(8,128)S(1)}) fusion(f32[256,2688]{1,0:T(8,128)} %bitcast), kind=kLoop, calls=%fused_computation.169 | loop fusion | bytes 1048576 | tf_op jit(solution)/shard_map/slice | solution.py:126
  89.0 0.4 reduce-precision_convert_fusion.5
  89.4 1.0 fusion.40
  90.4 1.0 fusion.42
  91.4 2.5 %fusion.63 = (f32[256,512]{1,0:T(8,128)S(1)}, f32[256,512]{1,0:T(8,128)S(1)}, f32[256,512]{1,0:T(8,128)S(1)}, f32[256,512]{1,0:T(8,128)S(1)}, f32[256,512]{1,0:T...) fusion(f32[4,256,768]{2,1,0:T(8,128)S(1)} %fusion.42, ...), kind=kLoop, calls=%fused_computation.95 | loop fusion | flops 1048576 | bytes 11534336 | tf_op jit(solution)/shard_map/mul | solution.py:153
  93.9 3.8 %collective-permute-start = (f32[256,512]{1,0:T(8,128)S(1)}, f32[256,512]{1,0:T(8,128)S(1)}, u32[]{:S(2)}, u32[]{:S(2)}) collective-permute-start(f32[256,512]{1,0:T(8,128)S(1)} %get-tuple-element.28), channel_id=1, source_target_pairs={{0,1},{1,0},{2,3},{3,2},{4,5},{5,4},{6,7},{7,6},{8,9},{9,8},{10,11... | collective-permute-start | bytes 1572872 | tf_op jit(solution)/shard_map/ppermute | solution.py:123
  97.8 0.1 maximum_bitcast_fusion.1
  97.9 0.1 maximum_bitcast_fusion.2
  98.0 0.1 maximum_bitcast_fusion.3
  98.1 2.4 %fusion.6 = f32[4,256,1024]{2,1,0:T(8,128)S(1)} fusion(f32[4,256,256]{2,1,0:T(8,128)S(1)} %fusion.95, f32[1,256,1024]{2,1,0:T(8,128)S(1)} %maximum_bitcast_fusion.3, f32[1,256,1024]{2,1,0:T(8,128)S(1)} %maximum_bitcast_fusion.2, f32[1,256,1024]{2,1,0:T(8,128)S(1)} %maximum_bitcast_fusion.1, f32[1,256,1024]{2,1,0:T(8,128)S(1)} %maximum_bitcast_fusion), kind=kOutput, calls=%fused_computation.6 | convolution fusion | flops 1613758464 | bytes 9437184 | tf_op jit(solution)/shard_map/aed,adc->aec/dot_general | solution.py:158
  100.5 0.1 fusion.71
  100.7 0.1 fusion.70
  101.1 4.0 %reduce-precision_convert_fusion.3 = (bf16[512,1024]{1,0:T(8,128)(2,1)S(1)}, bf16[512,1024]{1,0:T(8,128)(2,1)S(1)}, bf16[512,1024]{1,0:T(8,128)(2,1)S(1)}) fusion(f32[4,256,1024]{2,1,0:T(8,128)S(1)} %fusion.6, f32[1,256,512]{2,1,0:T(8,128)S(1)} %maximum_bitcast_fusion.7, f32[1,256,512]{2,1,0:T(8,128)S(1)} %maximum_bitcast_fusion.6, ...), kind=kOutput, calls=%fused_computation.38 | convolution fusion | flops 3226468352 | bytes 9437184 | tf_op jit(solution)/shard_map/aer,aec->rc/dot_general | solution.py:159
  105.1 3.6 %reduce-precision_convert_fusion.1 = (bf16[512,1024]{1,0:T(8,128)(2,1)S(1)}, bf16[512,1024]{1,0:T(8,128)(2,1)S(1)}, bf16[512,1024]{1,0:T(8,128)(2,1)S(1)}) fusion(pred[1024,1024]{1,0:T(32,128)(4,1)S(1)} %add_compare_fusion, bf16[512,1024]{1,0:T(8,128)(2,1)S(1)} %get-tuple-element.37, bf16[512,1024]{1,0:T(8,128)(2,1)S(1)} %get-tuple-element.38, ...), kind=kOutput, calls=%fused_computation.34 | convolution fusion | flops 3240624128 | bytes 7340032 | tf_op jit(solution)/shard_map/...k,kc->...c/dot_general | solution.py:28
  108.8 3.1 %fusion.19 = f32[512,1024]{1,0:T(8,128)} fusion(bf16[512,1024]{1,0:T(8,128)(2,1)S(1)} %get-tuple-element.34, bf16[512,1024]{1,0:T(8,128)(2,1)S(1)} %get-tuple-element.35, bf16[512,1024]{1,0:T(8,128)(2,1)S(1)} %get-tuple-element.33, pred[512,512]{1,0:T(32,128)(4,1)S(1)} %copy-done.1), kind=kOutput, calls=%fused_computation.20 | convolution fusion | flops 1621622784 | bytes 5505024 | tf_op jit(solution)/shard_map/dk,...kc->...dc/dot_general | solution.py:22
  (40 shorter events, 1.4 us)
Async XLA Ops:
  0.0 22.7 %copy-start = (f32[4,256,256]{2,1,0:T(8,128)S(1)}, f32[4,256,256]{2,1,0:T(8,128)}, u32[]{:S(2)}) copy-start(f32[4,256,256]{2,1,0:T(8,128)} %param.7) | copy-start | bytes 3145732
  4.5 80.4 %all-to-all-start = ((f32[32,8,2688]{2,1,0:T(8,128)}), f32[32,8,2688]{2,1,0:T(8,128)}, u32[]{:S(2)}, u32[]{:S(2)}) async-start(f32[32,8,2688]{2,1,0:T(8,128)} %shard_map.46), calls=%async_computation | async-start | bytes 5505024 | tf_op jit(solution)/shard_map/all_to_all | solution.py:115
  93.9 6.6 %collective-permute-start = (f32[256,512]{1,0:T(8,128)S(1)}, f32[256,512]{1,0:T(8,128)S(1)}, u32[]{:S(2)}, u32[]{:S(2)}) collective-permute-start(f32[256,512]{1,0:T(8,128)S(1)} %get-tuple-element.28), channel_id=1, source_target_pairs={{0,1},{1,0},{2,3},{3,2},{4,5},{5,4},{6,7},{7,6},{8,9},{9,8},{10,11... | collective-permute-start | bytes 1572872 | tf_op jit(solution)/shard_map/ppermute | solution.py:123
  105.1 3.7 %copy-start.1 = (pred[512,512]{1,0:T(32,128)(4,1)S(1)}, pred[512,512]{1,0:T(32,128)(4,1)}, u32[]{:S(2)}) copy-start(pred[512,512]{1,0:T(32,128)(4,1)} %add_compare_fusion.1) | copy-start | bytes 786436
